TPU v7x, 32 devices: a whole 2x2x4 slice. The times are simulated.
32 devices in a mesh: groups: 2 (over x), blk: 16 (over z, y, core).
Axes of the slice: x: 2, y: 2, z: 4, core: 2. Of those that a mesh axis runs over, the one named last changes fastest.
Arguments:
- layer_input_tokens: bfloat16 [384, 8192], P('groups', 'blk'), parts along dimension 0, may hold values from -6 to 6
- input_norm_gain: float32 [8192], replicated, may hold values from 0.5 to 1.5
- query_weight: bfloat16 [8192, 8192], P(None, 'blk'), may hold values from -0.0625 to 0.0625
- key_value_weight: bfloat16 [8192, 2048], P(None, 'blk'), may hold values from -0.0625 to 0.0625
- output_weight: bfloat16 [8192, 8192], P(None, 'blk'), may hold values from -0.5 to 0.5
- adapter_down_weight: bfloat16 [16, 64, 8192], P('blk'), may hold values from -0.0625 to 0.0625
- adapter_up_weight: bfloat16 [16, 64, 8192], P(None, None, 'blk'), may hold values from -0.75 to 0.75
- key_value_page_pool: bfloat16 [512, 128, 2048], P(('groups', 'blk')), parts along dimension 0, may hold values from -240 to 240
- request_adapter: int32 [128], P('groups'), parts along dimension 0, may hold values from 0 to 15
- adapter_storage_slot: int32 [16], replicated, may hold values from 0 to 15, each once
- cached_lengths: int32 [128], P('groups'), parts along dimension 0, may hold values from 1 to 512, as said below
- request_page_tables: int32 [128, 4], P('groups'), parts along dimension 0, may hold values from -1 to 255, as said below
Outputs:
- layer_out: bfloat16 [384, 8192], P('groups', 'blk'), parts along dimension 0
There are 2 independent parts, one for each index of `groups`. A program takes and returns all parts, laid end to end along the dimension named above; an argument that names none is the same for every part. Nothing has to cross between parts.
Inputs may be any that keep to these rules, and one draw needn't show every extreme that they name: `cached_lengths`: each request's cached length; the longest is exactly 512. `request_page_tables`: row r holds ceil(cached_lengths[r] / 128) page numbers first and -1 after them; no page is named twice in the whole table.
All inputs are finite; a program needn't handle non-finite values.
Results may differ from a plain program's by a relative error of at most 0.0085.
The roundings to bfloat16 on the way count: a program that leaves them out, or rounds other values in their place, can miss the bound.
Values may be sent and summed in bfloat16 or wider, within the bound.
No kernel may reach another device: no remote copies, remote signals or barrier semaphores. Data moves between devices by JAX's collectives and lax.ppermute only.
A program may use at most 128 MiB of HBM per device.

v0:
```python
import math

import jax
import jax.numpy as jnp
from jax import lax
from jax.sharding import PartitionSpec as P

QUERY_HEADS = 64
KEY_VALUE_HEADS = 8
HEAD_WIDTH = 128
PAGE_LENGTH = 128
NEW_TOKENS = 3


theta_base = 500000.0
neg_large = -1e30


def apply_rotation(values, token_positions, first_col, rot_limit):
    width_cols = values.shape[1]
    columns = first_col + jnp.arange(width_cols, dtype=jnp.int32)
    pair_index = (columns % HEAD_WIDTH // 2).astype(jnp.float32)
    inverse = jnp.exp(pair_index * (-2.0 * math.log(theta_base) / HEAD_WIDTH))
    angles = token_positions[:, None] * inverse[None, :]
    cos_val = jnp.cos(angles[:, 0::2])
    sine_val = jnp.sin(angles[:, 0::2])
    even_part = values[:, 0::2]
    odd_part = values[:, 1::2]
    turned = jnp.stack(
        [even_part * cos_val - odd_part * sine_val, even_part * sine_val + odd_part * cos_val],
        axis=-1,
    ).reshape(values.shape)
    return jnp.where((columns < rot_limit)[None, :], turned, values)


def normalize(layer_input_tokens, input_norm_gain):
    values = layer_input_tokens.astype(jnp.float32)
    mean_square = jnp.mean(values * values, axis=-1, keepdims=True)
    return (values * lax.rsqrt(mean_square + 1e-05) * input_norm_gain[None, :]).astype(jnp.bfloat16)


def positions_of(cached_lengths):
    steps_row = jnp.arange(NEW_TOKENS, dtype=jnp.int32)
    return (
        jnp.repeat(cached_lengths, NEW_TOKENS) + jnp.tile(steps_row, cached_lengths.shape[0])
    ).astype(jnp.float32)


def to_tokens(request_first_layout):
    request_count = request_first_layout.shape[0]
    trailing_shape = request_first_layout.shape[3:]
    query_group_width = QUERY_HEADS // KEY_VALUE_HEADS
    split_head_shape = request_first_layout.reshape(
        (request_count, KEY_VALUE_HEADS, NEW_TOKENS, query_group_width) + trailing_shape
    )
    order_axes = (0, 2, 1, 3) + tuple(range(4, 4 + len(trailing_shape)))
    return split_head_shape.transpose(order_axes).reshape(request_count * NEW_TOKENS, -1)


def local(
    layer_input_tokens,
    input_norm_gain,
    query_weight,
    key_value_weight,
    output_weight,
    adapter_down_weight,
    adapter_up_weight,
    key_value_page_pool,
    request_adapter,
    adapter_storage_slot,
    cached_lengths,
    request_page_tables,
):
    own_index = lax.axis_index("blk")
    gathered = lax.all_gather(layer_input_tokens, "blk", axis=1, tiled=True)
    normalized_input = normalize(gathered, input_norm_gain)
    request_count = cached_lengths.shape[0]
    adapter_total = adapter_storage_slot.shape[0]
    choose = request_adapter[:, None] == jnp.arange(adapter_total, dtype=jnp.int32)[None, :]
    req_slot = jnp.sum(jnp.where(choose, adapter_storage_slot[None, :], 0), axis=1)
    token_cache_slot = jnp.repeat(req_slot, NEW_TOKENS)
    local_token_count = adapter_down_weight.shape[0]
    local_pick = (
        token_cache_slot[:, None] - own_index * local_token_count
        == jnp.arange(local_token_count, dtype=jnp.int32)[None, :]
    )
    output_projected = jnp.einsum(
        "ly,mxy->lmx", normalized_input, adapter_down_weight, preferred_element_type=jnp.float32
    )
    partial_codes = jnp.sum(jnp.where(local_pick[:, :, None], output_projected, 0.0), axis=1)
    adapter_choice_index = lax.psum(partial_codes, "blk").astype(jnp.bfloat16)
    up_weight_rows = adapter_up_weight[token_cache_slot]
    adapter_query_update = jnp.einsum(
        "gk,gkq->gq", adapter_choice_index, up_weight_rows, preferred_element_type=jnp.float32
    )
    token_positions = positions_of(cached_lengths)
    query_cols = query_weight.shape[1]
    keyval_cols = key_value_weight.shape[1]
    query_part = apply_rotation(
        jnp.dot(normalized_input, query_weight, preferred_element_type=jnp.float32)
        + adapter_query_update,
        token_positions,
        own_index * query_cols,
        QUERY_HEADS * HEAD_WIDTH,
    ).astype(jnp.bfloat16)
    keyval_part = apply_rotation(
        jnp.dot(normalized_input, key_value_weight, preferred_element_type=jnp.float32),
        token_positions,
        own_index * keyval_cols,
        KEY_VALUE_HEADS * HEAD_WIDTH,
    ).astype(jnp.bfloat16)
    query_vectors, key_value_rows = (
        lax.all_gather(query_part, "blk", axis=1, tiled=True),
        lax.all_gather(keyval_part, "blk", axis=1, tiled=True),
    )
    query_group_width = QUERY_HEADS // KEY_VALUE_HEADS
    query_feature_width = query_group_width * NEW_TOKENS
    score_scale = 1.0 / math.sqrt(HEAD_WIDTH)
    query_req = (
        query_vectors.reshape(
            request_count, NEW_TOKENS, KEY_VALUE_HEADS, query_group_width, HEAD_WIDTH
        )
        .transpose(0, 2, 1, 3, 4)
        .reshape(request_count, KEY_VALUE_HEADS, query_feature_width, HEAD_WIDTH)
    )
    fresh_token_rows = key_value_rows.reshape(
        request_count, NEW_TOKENS, 2, KEY_VALUE_HEADS, HEAD_WIDTH
    )
    request_page_count = key_value_page_pool.shape[0]
    table_width = request_page_tables.shape[1]
    page_ids = own_index * request_page_count + jnp.arange(request_page_count, dtype=jnp.int32)
    matches = request_page_tables[None, :, :] == page_ids[:, None, None]
    page_owner = jnp.any(matches, axis=2)
    page_live = jnp.any(page_owner, axis=1)
    page_req = jnp.sum(
        jnp.where(page_owner, jnp.arange(request_count, dtype=jnp.int32)[None, :], 0), axis=1
    )
    page_slot = jnp.sum(
        jnp.where(matches, jnp.arange(table_width, dtype=jnp.int32)[None, None, :], 0), axis=(1, 2)
    )
    page_len = jnp.sum(jnp.where(page_owner, cached_lengths[None, :], 0), axis=1)
    key_pos = page_slot[:, None] * PAGE_LENGTH + jnp.arange(PAGE_LENGTH, dtype=jnp.int32)[None, :]
    key_valid = page_live[:, None] & (key_pos < page_len[:, None])
    valid_full = key_valid[:, None, None, :]
    gathered_cache_pages = key_value_page_pool.reshape(
        request_page_count, PAGE_LENGTH, 2, KEY_VALUE_HEADS, HEAD_WIDTH
    )
    query_page = query_req[page_req]
    scores = (
        jnp.einsum(
            "skqd,spkd->skqp",
            query_page,
            gathered_cache_pages[:, :, 0],
            preferred_element_type=jnp.float32,
        )
        * score_scale
    )
    masked = jnp.where(valid_full, scores, neg_large)
    page_peak = jnp.max(masked, axis=-1)
    req_peak = jnp.max(
        jnp.where(page_owner[:, :, None, None], page_peak[:, None], neg_large), axis=0
    )
    fresh_scores = (
        jnp.einsum(
            "rkqd,rjkd->rkqj",
            query_req,
            fresh_token_rows[:, :, 0],
            preferred_element_type=jnp.float32,
        )
        * score_scale
    )
    step_of = jnp.arange(query_feature_width, dtype=jnp.int32) // query_group_width
    fresh_ok = (jnp.arange(NEW_TOKENS, dtype=jnp.int32)[None, :] <= step_of[:, None])[None, None]
    fresh_masked = jnp.where(fresh_ok, fresh_scores, neg_large)
    top_score = lax.pmax(jnp.maximum(req_peak, jnp.max(fresh_masked, axis=-1)), "blk")
    weights = jnp.where(valid_full, jnp.exp(masked - top_score[page_req][..., None]), 0.0)
    page_num = jnp.einsum(
        "skqp,spkd->skqd",
        weights.astype(jnp.bfloat16),
        gathered_cache_pages[:, :, 1],
        preferred_element_type=jnp.float32,
    )
    owner_frac = page_owner.astype(jnp.float32)
    req_num = jnp.einsum("sr,skqd->rkqd", owner_frac, page_num, precision=lax.Precision.HIGHEST)
    req_den = jnp.einsum(
        "sr,skq->rkq", owner_frac, jnp.sum(weights, axis=-1), precision=lax.Precision.HIGHEST
    )
    fresh_weights = jnp.where(fresh_ok, jnp.exp(fresh_masked - top_score[..., None]), 0.0)
    fresh_num = jnp.einsum(
        "rkqj,rjkd->rkqd",
        fresh_weights.astype(jnp.bfloat16),
        fresh_token_rows[:, :, 1],
        preferred_element_type=jnp.float32,
    )
    fresh_den = jnp.sum(fresh_weights, axis=-1)
    num_tok = to_tokens(req_num)
    den_tok = to_tokens(req_den[..., None])
    fresh_num_tok = to_tokens(fresh_num)
    fresh_den_tok = to_tokens(fresh_den[..., None])
    num_all, den_all = lax.psum((num_tok, den_tok), "blk")
    totals = den_all + fresh_den_tok
    attended = ((num_all + fresh_num_tok) / jnp.repeat(totals, HEAD_WIDTH, axis=1)).astype(
        jnp.bfloat16
    )
    return jnp.dot(attended, output_weight, preferred_element_type=jnp.float32).astype(jnp.bfloat16)


def solution(mesh):
    placed = (
        P("groups", "blk"),
        P(),
        P(None, "blk"),
        P(None, "blk"),
        P(None, "blk"),
        P("blk", None, None),
        P(None, None, "blk"),
        P(("groups", "blk"), None, None),
        P("groups"),
        P(),
        P("groups"),
        P("groups", None),
    )
    return jax.shard_map(
        local, mesh=mesh, in_specs=placed, out_specs=P("groups", "blk"), check_vma=False
    )
```

profile of v0, /device:TPU:0, one launch (start us, length us, event | category | flops | bytes accessed | tf_op | source)
XLA Modules:
  0.0 458.2 jit_solution(6853859499092122322)
XLA Ops:
  6.5 0.7 all-gather.3.cloned.1.call-update
  7.3 0.8 select_reduce_fusion.2
  8.2 0.2 eq.54
  8.4 0.1 reshape.295
  8.5 0.7 add_convert_fusion
  9.3 0.1 convert_element_type.56
  9.5 7.3 %slice.33 = f32[192,256]{1,0:T(8,128)} slice(f32[192,512]{1,0:T(8,128)S(1)} %broadcast_multiply_fusion), slice={[0:192:1], [0:512:2]} | slice | bytes 393216 | tf_op jit(solution)/shard_map/slice | solution.py:25
  16.8 8.1 %gather_fusion = bf16[192,64,512]{2,1,0:T(8,128)(2,1)} fusion(bf16[16,64,512]{2,1,0:T(8,128)(2,1)S(1)} %copy-done.2, s32[1024]{0:T(1024)S(1)} %pad_clamp_fusion.1), kind=kCustom, calls=%fused_computation | custom fusion | bytes 25166592 | tf_op jit(solution)/shard_map/gather | solution.py:92
  25.0 0.7 fusion.49
  25.7 33.8 %all-gather.3.cloned.1.call-done = bf16[192,8192]{1,0:T(8,128)(2,1)} async-done(((bf16[192,512]{1,0:T(8,128)(2,1)}), bf16[192,8192]{1,0:T(8,128)(2,1)}) %all-gather.3.cloned.1.call-update) | async-done | bytes 3145744 | tf_op jit(solution)/shard_map/all_gather | solution.py:75
  59.5 2.6 fusion
  62.1 3.4 convolution_select_fusion
  65.5 59.5 %psum.21 = bf16[192,64]{0,1:T(8,128)(2,1)S(1)} all-reduce(f32[192,64]{0,1:T(8,128)S(1)} %convolution_select_fusion), channel_id=1, replica_groups=mesh['groups'=2,'blk'=16] {'blk'}, use_global_device_ids=true, to_apply=%region_6.7 | all-reduce | flops 12288 | bytes 73728 | tf_op jit(solution)/shard_map/psum | solution.py:91
  125.1 6.5 %fusion.53 = f32[192,1,512]{2,1,0:T(1,128)S(1)} fusion(bf16[192,64,1]{1,2,0:T(2,128)(2,1)S(1)} %copy.109, bf16[192,64,512]{2,1,0:T(8,128)(2,1)} %gather_fusion), kind=kOutput, calls=%fused_computation.118 | convolution fusion | flops 12582912 | bytes 13000704 | tf_op jit(solution)/shard_map/gk,gkq->gq/dot_general | solution.py:93
  131.6 5.3 %convolution_add_fusion = f32[192,512]{1,0:T(8,128)S(1)} fusion(bf16[8192,512]{1,0:T(8,128)(2,1)} %param.14, f32[192,1,512]{2,1,0:T(1,128)S(1)} %fusion.53, bf16[192,8192]{1,0:T(8,128)(2,1)S(1)} %copy-done.5, f32[8192]{0:T(1024)S(1)} %copy-done.11, f32[192]{0:T(256)S(1)} %add_rsqrt_fusion), kind=kOutput, calls=%fused_computation.28 | convolution fusion | flops 1617002496 | bytes 12354304 | tf_op jit(solution)/shard_map/dot_general | solution.py:100
  136.9 6.7 %slice.32 = f32[192,256]{1,0:T(8,128)S(1)} slice(f32[192,512]{1,0:T(8,128)S(1)} %convolution_add_fusion), slice={[0:192:1], [0:512:2]} | slice | bytes 393216 | tf_op jit(solution)/shard_map/slice | solution.py:27
  143.6 6.6 %slice.34 = f32[192,256]{1,0:T(8,128)S(1)} slice(f32[192,512]{1,0:T(8,128)S(1)} %convolution_add_fusion), slice={[0:192:1], [1:512:2]} | slice | bytes 393216 | tf_op jit(solution)/shard_map/slice | solution.py:28
  150.3 0.2 copy.91
  150.5 0.2 reshape.296
  150.8 0.1 copy.92
  150.9 0.7 select_convert_fusion
  151.6 0.2 all-reduce.2.cloned.1.call-start
  151.9 12.3 %copy.94 = bf16[16,128,2048]{1,2,0:T(8,128)(2,1)} copy(bf16[16,128,2048]{2,1,0:T(8,128)(2,1)} %param.19) | data formatting | bytes 16777216 | tf_op args[7]
  164.3 1.7 slice.37
  166.0 0.2 compare_reduce_fusion
  166.3 0.2 fusion.28
  166.6 0.3 fusion.50
  167.0 3.0 fusion.44
  170.0 1.7 slice.36
  171.7 1.7 slice.38
  173.8 22.4 %all_gather.11 = bf16[192,2048]{1,0:T(8,128)(2,1)S(1)} all-gather(bf16[192,128]{1,0:T(8,128)(2,1)S(1)} %select_convert_fusion.1), channel_id=1, replica_groups=mesh['groups'=2,'blk'=16] {'blk'}, dimensions={1}, use_global_device_ids=true | all-gather | bytes 835584 | tf_op jit(solution)/shard_map/all_gather | solution.py:114
  196.2 0.2 copy.118
  196.3 0.9 fusion.48
  197.3 2.4 all-gather.5.cloned.1.call-done
  199.7 2.8 copy.117
  202.5 1.8 copy-done.3
  204.2 2.3 copy.139
  206.5 2.6 gather_fusion.1
  209.1 3.5 fusion.51
  212.6 0.5 select_reduce_fusion
  213.1 0.1 copy.99
  213.2 3.7 fusion.52
  217.0 61.2 %pmax.7 = f32[64,8,24]{2,1,0:T(8,128)S(1)} all-reduce(f32[64,8,24]{2,1,0:T(8,128)S(1)} %max.5), channel_id=1, replica_groups=mesh['groups'=2,'blk'=16] {'blk'}, use_global_device_ids=true, to_apply=%region_11.12 | all-reduce | flops 12288 | bytes 98304 | tf_op jit(solution)/shard_map/pmax | solution.py:175
  278.2 0.6 gather_fusion.2
  278.8 4.5 fusion.9
  283.4 3.1 convolution_bitcast_fusion.1
  286.5 6.3 %copy.102 = f32[64,3,8,8,128]{4,3,2,1,0:T(8,128)} copy(f32[64,3,8,8,128]{4,0,3,1,2:T(8,128)S(1)} %convolution_bitcast_fusion.1) | data formatting | bytes 12582912 | tf_op jit(solution)/shard_map/transpose | solution.py:57
  292.8 7.2 %reshape.302 = f32[192,8192]{1,0:T(8,128)} reshape(f32[64,3,8,8,128]{4,3,2,1,0:T(8,128)} %copy.102) | data formatting | bytes 12582912 | tf_op jit(solution)/shard_map/reshape | solution.py:57
  300.0 1.8 convolution_bitcast_fusion
  301.8 3.3 copy.138
  305.1 7.5 %reshape.304 = f32[192,8192]{1,0:T(8,128)} reshape(f32[64,3,8,8,128]{4,3,2,1,0:T(8,128)} %bitcast.122) | data formatting | bytes 12582912 | tf_op jit(solution)/shard_map/reshape | solution.py:57
  312.6 0.9 fusion.21
  313.6 0.1 copy.107
  313.7 0.3 copy.108
  314.1 0.2 reshape.307
  314.3 0.9 fusion.11
  315.3 0.2 convolution_bitcast_fusion.2
  315.5 0.3 copy.106
  315.8 0.2 reshape.306
  316.1 61.3 %psum.23 = f32[192,64]{1,0:T(8,128)S(1)} all-reduce(f32[192,64]{1,0:T(8,128)S(1)} %reshape.306), channel_id=1, replica_groups=mesh['groups'=2,'blk'=16] {'blk'}, use_global_device_ids=true, to_apply=%region_14.15 | all-reduce | flops 12288 | bytes 98304 | tf_op jit(solution)/shard_map/psum | solution.py:200
  377.5 60.1 %all-reduce.2.cloned.1.call-done = f32[192,8192]{1,0:T(8,128)} async-done(((f32[192,8192]{1,0:T(8,128)}), f32[192,8192]{1,0:T(8,128)}) %all-reduce.2.cloned.1.call-update) | async-done | bytes 6291472 | tf_op jit(solution)/shard_map/psum | solution.py:200
  437.6 1.8 broadcast_in_dim.194
  439.3 1.0 copy-done.4
  440.4 10.9 %fusion.13 = bf16[192,512]{1,0:T(8,128)(2,1)} fusion(bf16[8192,512]{1,0:T(8,128)(2,1)} %param.16, f32[24,8,64,128]{3,2,1,0:T(8,128)S(1)} %bitcast.125, f32[192,8192]{1,0:T(8,128)} %all-reduce.2.cloned.1.call-done, f32[192,8192]{1,0:T(8,128)S(1)} %copy-done.4), kind=kOutput, calls=%fused_computation.29 | convolution fusion | flops 1615429632 | bytes 27459584 | tf_op jit(solution)/shard_map/dot_general | solution.py:205
  (58 shorter events, 1.5 us)
Async XLA Ops:
  6.5 160.4 %copy-start = (bf16[8192,128]{1,0:T(8,128)(2,1)S(1)}, bf16[8192,128]{1,0:T(8,128)(2,1)}, u32[]{:S(2)}) copy-start(bf16[8192,128]{1,0:T(8,128)(2,1)} %param.15) | copy-start | bytes 6291460
  6.5 10.3 %copy-start.2 = (bf16[16,64,512]{2,1,0:T(8,128)(2,1)S(1)}, bf16[16,64,512]{2,1,0:T(8,128)(2,1)}, u32[]{:S(2)}) copy-start(bf16[16,64,512]{2,1,0:T(8,128)(2,1)} %param.18) | copy-start | bytes 3145732
  6.5 52.9 %all-gather.3.cloned.1.call-start = ((), (), s32[]{:S(2)}) async-start(), calls=%async_computation | async-start | bytes 3342336 | tf_op jit(solution)/shard_map/all_gather | solution.py:75
  7.3 192.4 %all-gather.5.cloned.1.call-start = ((), (), s32[]{:S(2)}) async-start(), calls=%async_computation.1 | async-start | bytes 3342336 | tf_op jit(solution)/shard_map/all_gather | solution.py:113
  16.8 8.2 %copy-start.6 = (f32[192,256]{1,0:T(8,128)S(1)}, f32[192,256]{1,0:T(8,128)}, u32[]{:S(2)}) copy-start(f32[192,256]{1,0:T(8,128)} %slice.33) | copy-start | bytes 589828
  125.1 6.5 %copy-start.5 = (bf16[192,8192]{1,0:T(8,128)(2,1)S(1)}, bf16[192,8192]{1,0:T(8,128)(2,1)}, u32[]{:S(2)}) copy-start(bf16[192,8192]{1,0:T(8,128)(2,1)} %all-gather.3.cloned.1.call-done) | copy-start | bytes 9437188
  125.1 6.5 %copy-start.11 = (f32[8192]{0:T(1024)S(1)}, f32[8192]{0:T(1024)}, u32[]{:S(2)}) copy-start(f32[8192]{0:T(1024)} %param.13) | copy-start | bytes 98308
  151.6 285.9 %all-reduce.2.cloned.1.call-start = ((), (), s32[]{:S(2)}) async-start(), calls=%async_computation.2 | async-start | bytes 12582912 | tf_op jit(solution)/shard_map/psum | solution.py:200
  151.8 14.2 %copy-start.9 = (s32[64,4]{0,1:T(4,128)S(1)}, s32[64,4]{0,1:T(4,128)}, u32[]{:S(2)}) copy-start(s32[64,4]{0,1:T(4,128)} %param.23) | copy-start | bytes 3076
  151.9 14.3 %copy-start.10 = (s32[64]{0:T(128)S(1)}, s32[64]{0:T(128)}, u32[]{:S(2)}) copy-start(s32[64]{0:T(128)} %param.22) | copy-start | bytes 772
  202.5 1.8 copy-start.3
  278.8 7.7 %copy-start.7 = (f32[16,8,24]{2,1,0:T(8,128)}, f32[16,8,24]{2,1,0:T(8,128)S(1)}, u32[]{:S(2)}) copy-start(f32[16,8,24]{2,1,0:T(8,128)S(1)} %gather_fusion.2) | copy-start | bytes 36868
  305.1 9.2 %copy-start.8 = (f32[16,8,24]{2,1,0:T(8,128)S(1)}, f32[16,8,24]{2,1,0:T(8,128)}, u32[]{:S(2)}) copy-start(f32[16,8,24]{2,1,0:T(8,128)} %copy-done.7) | copy-start | bytes 36868
  437.6 2.8 copy-start.4
  440.4 10.9 %copy-start.1 = (bf16[8192,128]{1,0:T(8,128)(2,1)S(1)}, bf16[8192,128]{1,0:T(8,128)(2,1)}, u32[]{:S(2)}) copy-start(bf16[8192,128]{1,0:T(8,128)(2,1)} %param.15) | copy-start | bytes 6291460
Sparse Core Ops, SparseCore 0:
  9.5 49.8 all-gather.2
  151.7 47.8 all-gather.4
  300.1 137.4 all-reduce.1
where the time goes:
time: 465 us; the launch traced here: 458 us
  blocking collectives  204 us (44%)
  waiting for transfers between devices  97.1 us (21%)
  local copies, waits for them, and re-layouts  88.3 us (19%)
  matrix products  45.9 us (10%)
  between operations  14 us (3%)
  other arithmetic  8.24 us (2%)
    psum x1, blocking collectives, local(): num_all, den_all = lax.psum((num_tok, den_tok), 'blk')  61.3 us
    pmax x1, blocking collectives, local(): lax.pmax(jnp.maximum(req_peak, jnp.max(fresh_masked, axis=-1)), 'blk')  61.2 us
    psum x1, waiting for transfers between devices, local(): num_all, den_all = lax.psum((num_tok, den_tok), 'blk')  60.1 us
    psum x1, blocking collectives, local(): adapter_choice_index = lax.psum(partial_codes, 'blk').astype(jnp.bfloat16)  59.5 us
    all_gather x1, waiting for transfers between devices, local(): gathered = lax.all_gather(layer_input_tokens, 'blk', axis=1, tiled=True)  33.8 us
    all_gather x1, blocking collectives, local(): lax.all_gather(keyval_part, 'blk', axis=1, tiled=True)  22.4 us
    unnamed x27, local copies, waits for them, and re-layouts  18 us
    reshape x4, local copies, waits for them, and re-layouts, to_tokens(): split_head_shape.transpose(order_axes)  15.1 us
  transfers between devices with their start and end apart: 3, of which 3 were waited for; matrix products, arithmetic and copies ran while one was open for 13% of the time, Pallas kernels for 0%

commit v1 on v0

--- a/solution.py
+++ b/solution.py
@@ -55,6 +55,16 @@
     )
     order_axes = (0, 2, 1, 3) + tuple(range(4, 4 + len(trailing_shape)))
     return split_head_shape.transpose(order_axes).reshape(request_count * NEW_TOKENS, -1)
+
+
+def butterfly(value, combine):
+    size = lax.axis_size("blk")
+    step = 1
+    while step < size:
+        pairs = [(i, i ^ step) for i in range(size)]
+        value = combine(value, lax.ppermute(value, "blk", pairs))
+        step *= 2
+    return value
 
 
 def local(
@@ -88,7 +98,7 @@
         "ly,mxy->lmx", normalized_input, adapter_down_weight, preferred_element_type=jnp.float32
     )
     partial_codes = jnp.sum(jnp.where(local_pick[:, :, None], output_projected, 0.0), axis=1)
-    adapter_choice_index = lax.psum(partial_codes, "blk").astype(jnp.bfloat16)
+    adapter_choice_index = butterfly(partial_codes.astype(jnp.bfloat16), jnp.add)
     up_weight_rows = adapter_up_weight[token_cache_slot]
     adapter_query_update = jnp.einsum(
         "gk,gkq->gq", adapter_choice_index, up_weight_rows, preferred_element_type=jnp.float32
@@ -109,10 +119,11 @@
         own_index * keyval_cols,
         KEY_VALUE_HEADS * HEAD_WIDTH,
     ).astype(jnp.bfloat16)
-    query_vectors, key_value_rows = (
-        lax.all_gather(query_part, "blk", axis=1, tiled=True),
-        lax.all_gather(keyval_part, "blk", axis=1, tiled=True),
-    )
+    joined = lax.all_gather(
+        jnp.concatenate([query_part, keyval_part], axis=1), "blk", axis=1, tiled=False
+    )
+    query_vectors = joined[:, :, :query_cols].reshape(joined.shape[0], -1)
+    key_value_rows = joined[:, :, query_cols:].reshape(joined.shape[0], -1)
     query_group_width = QUERY_HEADS // KEY_VALUE_HEADS
     query_feature_width = query_group_width * NEW_TOKENS
     score_scale = 1.0 / math.sqrt(HEAD_WIDTH)
@@ -172,7 +183,7 @@
     step_of = jnp.arange(query_feature_width, dtype=jnp.int32) // query_group_width
     fresh_ok = (jnp.arange(NEW_TOKENS, dtype=jnp.int32)[None, :] <= step_of[:, None])[None, None]
     fresh_masked = jnp.where(fresh_ok, fresh_scores, neg_large)
-    top_score = lax.pmax(jnp.maximum(req_peak, jnp.max(fresh_masked, axis=-1)), "blk")
+    top_score = butterfly(jnp.maximum(req_peak, jnp.max(fresh_masked, axis=-1)), jnp.maximum)
     weights = jnp.where(valid_full, jnp.exp(masked - top_score[page_req][..., None]), 0.0)
     page_num = jnp.einsum(
         "skqp,spkd->skqd",
@@ -197,7 +208,13 @@
     den_tok = to_tokens(req_den[..., None])
     fresh_num_tok = to_tokens(fresh_num)
     fresh_den_tok = to_tokens(fresh_den[..., None])
-    num_all, den_all = lax.psum((num_tok, den_tok), "blk")
+    pad_width = HEAD_WIDTH - den_tok.shape[1] % HEAD_WIDTH
+    summed = lax.psum(
+        jnp.concatenate([num_tok, den_tok, jnp.zeros((den_tok.shape[0], pad_width), jnp.float32)], axis=1),
+        "blk",
+    )
+    num_all = summed[:, : num_tok.shape[1]]
+    den_all = summed[:, num_tok.shape[1] : num_tok.shape[1] + den_tok.shape[1]]
     totals = den_all + fresh_den_tok
     attended = ((num_all + fresh_num_tok) / jnp.repeat(totals, HEAD_WIDTH, axis=1)).astype(
         jnp.bfloat16

time: 465 us -> 419 us (0.901)
  blocking collectives: 204 us -> 0 us
  waiting for transfers between devices: 97.1 us -> 228 us
  local copies, waits for them, and re-layouts: 88.3 us -> 106 us
  starting transfers between devices: 0.26 us -> 8.43 us
    psum x2 -> x0, blocking collectives: 121 us -> none  [the longest x1 61.3 us: local(): num_all, den_all = lax.psum((num_tok, den_tok), 'blk')]
    psum x1, waiting for transfers between devices: 60.1 us -> 125 us  [local(): lax.psum(jnp.concatenate([num_tok, den_tok, jnp.zeros((den_tok.shape[0],...]
    pmax x1 -> x0, blocking collectives: 61.2 us -> none  [local(): lax.pmax(jnp.maximum(req_peak, jnp.max(fresh_masked, axis=-1)), 'blk')]
    ppermute x0 -> x8, waiting for transfers between devices: none -> 35.9 us  [butterfly(): value = combine(value, lax.ppermute(value, 'blk', pairs))]
    all_gather x1, waiting for transfers between devices: 2.43 us -> 34.9 us  [local(): lax.all_gather(jnp.concatenate([query_part, keyval_part], axis=1), 'blk',...]
    all_gather x1 -> x0, blocking collectives: 22.4 us -> none  [local(): lax.all_gather(keyval_part, 'blk', axis=1, tiled=True)]
    another operation x0 -> x2, local copies, waits for them, and re-layouts: none -> 10.4 us  [local(): query_vectors.reshape(request_count, NEW_TOKENS, KEY_VALUE_HEADS, query_g...]
    ppermute x0 -> x8, starting transfers between devices: none -> 8.35 us  [butterfly(): value = combine(value, lax.ppermute(value, 'blk', pairs))]
  transfers between devices with their start and end apart: 3 -> 11, of which waited for: 3 -> 10; matrix products, arithmetic and copies ran while one was open for 13% -> 13% of each run, Pallas kernels for 0% -> 0%
where the time goes in v1:
time: 419 us; the launch traced here: 413 us
  waiting for transfers between devices  228 us (54%)
  local copies, waits for them, and re-layouts  106 us (25%)
  matrix products  46.7 us (11%)
  between operations  14.1 us (3%)
  other arithmetic  9.68 us (2%)
  starting transfers between devices  8.43 us (2%)
    psum x1, waiting for transfers between devices, local(): lax.psum(jnp.concatenate([num_tok, den_tok, jnp.zeros((den_tok.shape[0],...  125 us
    ppermute x8, waiting for transfers between devices, butterfly(): value = combine(value, lax.ppermute(value, 'blk', pairs))  35.9 us
    all_gather x1, waiting for transfers between devices, local(): lax.all_gather(jnp.concatenate([query_part, keyval_part], axis=1), 'blk',...  34.9 us
    all_gather x1, waiting for transfers between devices, local(): gathered = lax.all_gather(layer_input_tokens, 'blk', axis=1, tiled=True)  31.1 us
    unnamed x22, local copies, waits for them, and re-layouts  15.2 us
    reshape x4, local copies, waits for them, and re-layouts, to_tokens(): split_head_shape.transpose(order_axes)  14.9 us
    dot_general x1, matrix products, local(): jnp.dot(attended, output_weight, preferred_element_type=jnp.float32)  10.9 us
    another operation x2, local copies, waits for them, and re-layouts, local(): query_vectors.reshape(request_count, NEW_TOKENS, KEY_VALUE_HEADS, query_g...  10.4 us
  transfers between devices with their start and end apart: 11, of which 10 were waited for; matrix products, arithmetic and copies ran while one was open for 13% of the time, Pallas kernels for 0%

profile of v1, /device:TPU:0, one launch (start us, length us, event | category | flops | bytes accessed | tf_op | source)
XLA Modules:
  0.0 412.7 jit_solution(6270110166324109549)
XLA Ops:
  6.5 0.7 all-gather.4.cloned.1.call-update
  7.3 0.8 select_reduce_fusion.2
  8.5 0.7 add_convert_fusion
  9.5 7.3 %slice.45 = f32[192,256]{1,0:T(8,128)} slice(f32[192,512]{1,0:T(8,128)S(1)} %broadcast_multiply_fusion), slice={[0:192:1], [0:512:2]} | slice | bytes 393216 | tf_op jit(solution)/shard_map/slice | solution.py:25
  16.9 1.7 slice.48
  18.7 8.7 %gather_fusion = bf16[192,64,512]{2,1,0:T(8,128)(2,1)} fusion(bf16[16,64,512]{2,1,0:T(8,128)(2,1)S(1)} %copy-done.2, s32[1024]{0:T(1024)S(1)} %pad_clamp_fusion.1), kind=kCustom, calls=%fused_computation | custom fusion | bytes 25166592 | tf_op jit(solution)/shard_map/gather | solution.py:102
  27.4 0.4 fusion.51
  27.7 0.7 fusion.50
  28.4 31.1 %all-gather.4.cloned.1.call-done = bf16[192,8192]{1,0:T(8,128)(2,1)} async-done(((bf16[192,512]{1,0:T(8,128)(2,1)}), bf16[192,8192]{1,0:T(8,128)(2,1)}) %all-gather.4.cloned.1.call-update) | async-done | bytes 3145744 | tf_op jit(solution)/shard_map/all_gather | solution.py:85
  59.5 2.8 fusion
  62.2 3.4 fusion.16
  65.6 0.3 collective-permute-start
  65.9 1.2 fusion.45
  67.1 1.7 slice.47
  68.8 1.7 slice.49
  70.5 1.3 collective-permute-start.1
  71.9 2.6 collective-permute-done.1
  75.0 3.5 collective-permute-done.2
  78.5 1.6 collective-permute-start.3
  80.1 3.3 collective-permute-done.3
  83.5 6.5 %fusion.54 = f32[192,1,512]{2,1,0:T(1,128)S(1)} fusion(bf16[192,64,1]{1,2,0:T(2,128)(2,1)S(1)} %copy.113, bf16[192,64,512]{2,1,0:T(8,128)(2,1)} %gather_fusion), kind=kOutput, calls=%fused_computation.122 | convolution fusion | flops 12582912 | bytes 13000704 | tf_op jit(solution)/shard_map/gk,gkq->gq/dot_general | solution.py:103
  90.0 5.3 %convolution_add_fusion = f32[192,512]{1,0:T(8,128)S(1)} fusion(bf16[8192,512]{1,0:T(8,128)(2,1)} %param.14, f32[192,1,512]{2,1,0:T(1,128)S(1)} %fusion.54, bf16[192,8192]{1,0:T(8,128)(2,1)S(1)} %copy-done.5, f32[8192]{0:T(1024)S(1)} %copy-done.9, f32[192]{0:T(256)S(1)} %add_rsqrt_fusion), kind=kOutput, calls=%fused_computation.29 | convolution fusion | flops 1617002496 | bytes 12354304 | tf_op jit(solution)/shard_map/dot_general | solution.py:110
  95.3 6.8 %slice.44 = f32[192,256]{1,0:T(8,128)S(1)} slice(f32[192,512]{1,0:T(8,128)S(1)} %convolution_add_fusion), slice={[0:192:1], [0:512:2]} | slice | bytes 393216 | tf_op jit(solution)/shard_map/slice | solution.py:27
  102.2 6.6 %slice.46 = f32[192,256]{1,0:T(8,128)S(1)} slice(f32[192,512]{1,0:T(8,128)S(1)} %convolution_add_fusion), slice={[0:192:1], [1:512:2]} | slice | bytes 393216 | tf_op jit(solution)/shard_map/slice | solution.py:28
  109.1 0.2 reshape.290
  109.5 0.7 pad_maximum_fusion.1
  110.4 12.3 %copy.99 = bf16[16,128,2048]{1,2,0:T(8,128)(2,1)} copy(bf16[16,128,2048]{2,1,0:T(8,128)(2,1)} %param.19) | data formatting | bytes 16777216 | tf_op args[7]
  123.3 34.9 %all-gather.6.cloned.1.call-done = bf16[192,10240]{1,0:T(8,128)(2,1)} async-done(((bf16[192,640]{1,0:T(8,128)(2,1)}), bf16[192,10240]{1,0:T(8,128)(2,1)}) %all-gather.6.cloned.1.call-update) | async-done | bytes 3932176 | tf_op jit(solution)/shard_map/all_gather | solution.py:122
  158.2 2.9 copy.124
  161.1 2.2 slice.64
  163.2 1.0 slice.66
  164.3 6.2 %reshape_reshape.6 = bf16[64,3,8,8,128]{4,3,2,1,0:T(8,128)(2,1)} reshape(bf16[192,16,512]{2,1,0:T(8,128)(2,1)} %slice.64) | data formatting | bytes 6291456 | tf_op jit(solution)/shard_map/reshape;reshape | solution.py:131
  170.5 4.2 %copy.145 = bf16[64,3,8,8,128]{4,3,1,2,0:T(8,128)(2,1)} copy(bf16[64,3,8,8,128]{4,3,2,1,0:T(8,128)(2,1)} %reshape_reshape.6) | data formatting | bytes 6291456 | tf_op jit(solution)/shard_map/reshape;reshape | solution.py:131
  174.7 2.6 gather_fusion.1
  177.2 3.5 fusion.52
  180.7 0.5 select_reduce_fusion
  181.4 1.2 fusion.49
  182.6 3.7 fusion.53
  186.3 0.3 collective-permute-start.4
  186.6 1.3 collective-permute-done.4
  187.9 0.6 collective-permute-start.5
  188.5 7.9 %collective-permute-done.5 = f32[64,8,24]{2,1,0:T(8,128)S(1)} collective-permute-done((f32[64,8,24]{2,1,0:T(8,128)S(1)}, f32[64,8,24]{2,1,0:T(8,128)S(1)}, u32[]{:S(2)}, u32[]{:S(2)}) %collective-permute-start.5) | collective-permute-done | bytes 49184 | tf_op jit(solution)/shard_map/ppermute | solution.py:65
  196.5 2.0 collective-permute-start.6
  198.5 5.9 %collective-permute-done.6 = f32[64,8,24]{2,1,0:T(8,128)S(1)} collective-permute-done((f32[64,8,24]{2,1,0:T(8,128)S(1)}, f32[64,8,24]{2,1,0:T(8,128)S(1)}, u32[]{:S(2)}, u32[]{:S(2)}) %collective-permute-start.6) | collective-permute-done | bytes 49184 | tf_op jit(solution)/shard_map/ppermute | solution.py:65
  204.4 2.0 collective-permute-start.7
  206.4 11.4 %collective-permute-done.7 = f32[64,8,24]{2,1,0:T(8,128)S(1)} collective-permute-done((f32[64,8,24]{2,1,0:T(8,128)S(1)}, f32[64,8,24]{2,1,0:T(8,128)S(1)}, u32[]{:S(2)}, u32[]{:S(2)}) %collective-permute-start.7) | collective-permute-done | bytes 49184 | tf_op jit(solution)/shard_map/ppermute | solution.py:65
  217.9 0.6 gather_fusion.2
  218.5 0.9 fusion.11
  219.4 5.8 %fusion.9 = f32[8,3,8,128,16]{3,2,1,0,4:T(8,128)} fusion(bf16[16,128,2,8,128]{1,4,3,2,0:T(8,128)(2,1)} %bitcast.117, f32[16,8,24,128]{3,2,1,0:T(8,128)S(1)} %get-tuple-element.20, f32[16,8,24]{2,1,0:T(8,128)S(1)} %gather_fusion.2, pred[16,128]{1,0:T(8,128)(4,1)S(1)} %fusion.30), kind=kOutput, calls=%fused_computation.24 | convolution fusion | flops 101842944 | bytes 7354368 | tf_op jit(solution)/shard_map/skqp,spkd->skqd/dot_general | solution.py:188
  225.5 0.3 copy.107
  225.8 0.2 reshape.296
  226.1 4.5 %convolution_bitcast_fusion.1 = f32[64,3,8,8,128]{4,0,3,1,2:T(8,128)S(1)} fusion(f32[8,3,8,128,16]{3,2,1,0,4:T(8,128)} %fusion.9, pred[16,64]{1,0:T(8,128)(4,1)S(1)} %get-tuple-element.6), kind=kOutput, calls=%fused_computation.19 | convolution fusion | flops 301989888 | bytes 7865344 | tf_op jit(solution)/shard_map/sr,skqd->rkqd/dot_general | solution.py:195
  230.5 6.5 %copy.105 = f32[64,3,8,8,128]{4,3,2,1,0:T(8,128)} copy(f32[64,3,8,8,128]{4,0,3,1,2:T(8,128)S(1)} %convolution_bitcast_fusion.1) | data formatting | bytes 12582912 | tf_op jit(solution)/shard_map/transpose | solution.py:57
  237.1 7.2 %reshape.294 = f32[192,8192]{1,0:T(8,128)} reshape(f32[64,3,8,8,128]{4,3,2,1,0:T(8,128)} %copy.105) | data formatting | bytes 12582912 | tf_op jit(solution)/shard_map/reshape | solution.py:57
  244.3 7.9 %concatenate.7 = f32[192,8320]{1,0:T(8,128)} concatenate(f32[192,8192]{1,0:T(8,128)} %reshape.294, f32[192,64]{1,0:T(8,128)S(1)} %reshape.296, f32[192,64]{1,0:T(8,128)S(1)} %broadcast_in_dim.182.clone), dimensions={1} | concatenate | bytes 12779520 | tf_op jit(solution)/shard_map/concatenate | solution.py:213
  252.2 1.8 convolution_bitcast_fusion
  254.0 3.6 copy.144
  257.6 7.2 %reshape.298 = f32[192,8192]{1,0:T(8,128)} reshape(f32[64,3,8,8,128]{4,3,2,1,0:T(8,128)} %bitcast.118) | data formatting | bytes 12582912 | tf_op jit(solution)/shard_map/reshape | solution.py:57
  264.8 0.9 fusion.22
  265.9 0.3 copy.112
  266.5 125.1 %all-reduce.2.cloned.1.call-done = f32[192,8320]{1,0:T(8,128)} async-done(((f32[192,8320]{1,0:T(8,128)}), f32[192,8320]{1,0:T(8,128)}) %all-reduce.2.cloned.1.call-update) | async-done | bytes 6389776 | tf_op jit(solution)/shard_map/psum | solution.py:212
  391.6 1.1 slice_add_fusion.1
  392.6 2.1 broadcast_in_dim.195
  394.7 10.9 %fusion.13 = bf16[192,512]{1,0:T(8,128)(2,1)} fusion(bf16[8192,512]{1,0:T(8,128)(2,1)} %param.16, f32[24,8,64,128]{3,2,1,0:T(8,128)S(1)} %bitcast.121, f32[192,8192]{1,0:T(8,128)S(1)} %copy-done.3, f32[192,8320]{1,0:T(8,128)} %all-reduce.2.cloned.1.call-done), kind=kOutput, calls=%fused_computation.30 | convolution fusion | flops 1615429632 | bytes 27459584 | tf_op jit(solution)/shard_map/dot_general | solution.py:222
  (79 shorter events, 3.7 us)
Async XLA Ops:
  6.5 59.4 %copy-start = (bf16[8192,128]{1,0:T(8,128)(2,1)S(1)}, bf16[8192,128]{1,0:T(8,128)(2,1)}, u32[]{:S(2)}) copy-start(bf16[8192,128]{1,0:T(8,128)(2,1)} %param.15) | copy-start | bytes 6291460
  6.5 12.1 %copy-start.2 = (bf16[16,64,512]{2,1,0:T(8,128)(2,1)S(1)}, bf16[16,64,512]{2,1,0:T(8,128)(2,1)}, u32[]{:S(2)}) copy-start(bf16[16,64,512]{2,1,0:T(8,128)(2,1)} %param.18) | copy-start | bytes 3145732
  6.5 52.9 %all-gather.4.cloned.1.call-start = ((), (), s32[]{:S(2)}) async-start(), calls=%async_computation | async-start | bytes 3342336 | tf_op jit(solution)/shard_map/all_gather | solution.py:85
  7.3 150.9 %all-gather.6.cloned.1.call-start = ((), (), s32[]{:S(2)}) async-start(), calls=%async_computation.2 | async-start | bytes 4177920 | tf_op jit(solution)/shard_map/all_gather | solution.py:122
  18.6 9.1 %copy-start.6 = (f32[192,256]{1,0:T(8,128)S(1)}, f32[192,256]{1,0:T(8,128)}, u32[]{:S(2)}) copy-start(f32[192,256]{1,0:T(8,128)} %slice.45) | copy-start | bytes 589828
  18.6 43.6 %copy-start.9 = (f32[8192]{0:T(1024)S(1)}, f32[8192]{0:T(1024)}, u32[]{:S(2)}) copy-start(f32[8192]{0:T(1024)} %param.13) | copy-start | bytes 98308
  59.5 6.5 %copy-start.4 = (bf16[192,8192]{1,0:T(8,128)(2,1)S(1)}, bf16[192,8192]{1,0:T(8,128)(2,1)}, u32[]{:S(2)}) copy-start(bf16[192,8192]{1,0:T(8,128)(2,1)} %all-gather.4.cloned.1.call-done) | copy-start | bytes 9437188
  65.6 4.9 %collective-permute-start = (bf16[192,64]{0,1:T(8,128)(2,1)S(1)}, bf16[192,64]{0,1:T(8,128)(2,1)S(1)}, u32[]{:S(2)}, u32[]{:S(2)}) collective-permute-start(bf16[192,64]{0,1:T(8,128)(2,1)S(1)} %fusion.16), channel_id=1, source_target_pairs={{0,1},{1,0},{2,3},{3,2},{4,5},{5,4},{6,7},{7,6},{8,9},{9,8},{10,11... | collective-permute-start | bytes 73736 | tf_op jit(solution)/shard_map/ppermute | solution.py:65
  70.5 4.0 collective-permute-start.1
  74.5 4.0 collective-permute-start.2
  78.5 4.9 %collective-permute-start.3 = (bf16[192,64]{0,1:T(8,128)(2,1)S(1)}, bf16[192,64]{0,1:T(8,128)(2,1)S(1)}, u32[]{:S(2)}, u32[]{:S(2)}) collective-permute-start(bf16[192,64]{0,1:T(8,128)(2,1)S(1)} %add.171), channel_id=1, source_target_pairs={{0,8},{1,9},{2,10},{3,11},{4,12},{5,13},{6,14},{7,15},{8,0},{9,1},... | collective-permute-start | bytes 73736 | tf_op jit(solution)/shard_map/ppermute | solution.py:65
  83.5 6.5 %copy-start.5 = (bf16[192,8192]{1,0:T(8,128)(2,1)S(1)}, bf16[192,8192]{1,0:T(8,128)(2,1)}, u32[]{:S(2)}) copy-start(bf16[192,8192]{1,0:T(8,128)(2,1)} %all-gather.4.cloned.1.call-done) | copy-start | bytes 9437188
  110.3 281.3 %all-reduce.2.cloned.1.call-start = ((), (), s32[]{:S(2)}) async-start(), calls=%async_computation.1 | async-start | bytes 12779520 | tf_op jit(solution)/shard_map/psum | solution.py:212
  110.4 12.3 %copy-start.7 = (s32[64,4]{0,1:T(4,128)S(1)}, s32[64,4]{0,1:T(4,128)}, u32[]{:S(2)}) copy-start(s32[64,4]{0,1:T(4,128)} %param.23) | copy-start | bytes 3076
  110.4 12.5 %copy-start.8 = (s32[64]{0:T(128)S(1)}, s32[64]{0:T(128)}, u32[]{:S(2)}) copy-start(s32[64]{0:T(128)} %param.22) | copy-start | bytes 772
  186.3 1.6 collective-permute-start.4
  187.9 8.5 %collective-permute-start.5 = (f32[64,8,24]{2,1,0:T(8,128)S(1)}, f32[64,8,24]{2,1,0:T(8,128)S(1)}, u32[]{:S(2)}, u32[]{:S(2)}) collective-permute-start(f32[64,8,24]{2,1,0:T(8,128)S(1)} %max.16), channel_id=1, source_target_pairs={{0,2},{1,3},{2,0},{3,1},{4,6},{5,7},{6,4},{7,5},{8,10},{9,11},{10,... | collective-permute-start | bytes 147464 | tf_op jit(solution)/shard_map/ppermute | solution.py:65
  196.5 7.9 %collective-permute-start.6 = (f32[64,8,24]{2,1,0:T(8,128)S(1)}, f32[64,8,24]{2,1,0:T(8,128)S(1)}, u32[]{:S(2)}, u32[]{:S(2)}) collective-permute-start(f32[64,8,24]{2,1,0:T(8,128)S(1)} %max.17), channel_id=1, source_target_pairs={{0,4},{1,5},{2,6},{3,7},{4,0},{5,1},{6,2},{7,3},{8,12},{9,13},{10,... | collective-permute-start | bytes 147464 | tf_op jit(solution)/shard_map/ppermute | solution.py:65
  204.4 13.5 %collective-permute-start.7 = (f32[64,8,24]{2,1,0:T(8,128)S(1)}, f32[64,8,24]{2,1,0:T(8,128)S(1)}, u32[]{:S(2)}, u32[]{:S(2)}) collective-permute-start(f32[64,8,24]{2,1,0:T(8,128)S(1)} %max.18), channel_id=1, source_target_pairs={{0,8},{1,9},{2,10},{3,11},{4,12},{5,13},{6,14},{7,15},{8,0},{9,1},... | collective-permute-start | bytes 147464 | tf_op jit(solution)/shard_map/ppermute | solution.py:65
  391.6 3.1 copy-start.3
  394.7 10.9 %copy-start.1 = (bf16[8192,128]{1,0:T(8,128)(2,1)S(1)}, bf16[8192,128]{1,0:T(8,128)(2,1)}, u32[]{:S(2)}) copy-start(bf16[8192,128]{1,0:T(8,128)(2,1)} %param.15) | copy-start | bytes 6291460
Sparse Core Ops, SparseCore 0:
  9.5 49.9 all-gather.3
  110.4 47.6 all-gather.5
  252.3 139.2 all-reduce.1

commit v2 on v1

--- a/solution.py
+++ b/solution.py
@@ -191,11 +191,32 @@
         gathered_cache_pages[:, :, 1],
         preferred_element_type=jnp.float32,
     )
-    owner_frac = page_owner.astype(jnp.float32)
-    req_num = jnp.einsum("sr,skqd->rkqd", owner_frac, page_num, precision=lax.Precision.HIGHEST)
-    req_den = jnp.einsum(
-        "sr,skq->rkq", owner_frac, jnp.sum(weights, axis=-1), precision=lax.Precision.HIGHEST
-    )
+    device_count = lax.axis_size("blk")
+    head_count = QUERY_HEADS
+    owner_cols = query_cols
+    owner_heads = max(1, owner_cols // HEAD_WIDTH)
+    head_repeat = min(owner_cols, HEAD_WIDTH)
+    owner_first_head = [(o * owner_cols) // HEAD_WIDTH for o in range(device_count)]
+    head_pick = jnp.asarray(
+        [[first + j for j in range(owner_heads)] for first in owner_first_head], jnp.int32
+    )
+    slot_num = to_tokens(page_num).reshape(request_page_count, NEW_TOKENS, device_count, owner_cols)
+    slot_den = to_tokens(jnp.sum(weights, axis=-1)[..., None]).reshape(
+        request_page_count, NEW_TOKENS, head_count
+    )
+    slot_den_owner = slot_den[:, :, head_pick]
+    packed = jnp.concatenate([slot_num, slot_den_owner], axis=3).transpose(2, 0, 1, 3)
+    received = lax.all_to_all(packed, "blk", 0, 0, tiled=True)
+    group_pages = device_count * request_page_count
+    all_page_ids = jnp.arange(group_pages, dtype=jnp.int32)
+    all_owner = jnp.any(request_page_tables[None, :, :] == all_page_ids[:, None, None], axis=2)
+    pick_req = all_owner.T.astype(jnp.float32)
+    summed = jnp.einsum(
+        "rp,px->rx",
+        pick_req,
+        received.reshape(group_pages, -1),
+        precision=lax.Precision.HIGHEST,
+    ).reshape(request_count, NEW_TOKENS, owner_cols + owner_heads)
     fresh_weights = jnp.where(fresh_ok, jnp.exp(fresh_masked - top_score[..., None]), 0.0)
     fresh_num = jnp.einsum(
         "rkqj,rjkd->rkqd",
@@ -204,21 +225,19 @@
         preferred_element_type=jnp.float32,
     )
     fresh_den = jnp.sum(fresh_weights, axis=-1)
-    num_tok = to_tokens(req_num)
-    den_tok = to_tokens(req_den[..., None])
-    fresh_num_tok = to_tokens(fresh_num)
-    fresh_den_tok = to_tokens(fresh_den[..., None])
-    pad_width = HEAD_WIDTH - den_tok.shape[1] % HEAD_WIDTH
-    summed = lax.psum(
-        jnp.concatenate([num_tok, den_tok, jnp.zeros((den_tok.shape[0], pad_width), jnp.float32)], axis=1),
-        "blk",
-    )
-    num_all = summed[:, : num_tok.shape[1]]
-    den_all = summed[:, num_tok.shape[1] : num_tok.shape[1] + den_tok.shape[1]]
-    totals = den_all + fresh_den_tok
-    attended = ((num_all + fresh_num_tok) / jnp.repeat(totals, HEAD_WIDTH, axis=1)).astype(
+    fresh_num_own = lax.dynamic_slice_in_dim(
+        to_tokens(fresh_num), own_index * owner_cols, owner_cols, axis=1
+    )
+    fresh_den_own = lax.dynamic_slice_in_dim(
+        to_tokens(fresh_den[..., None]), (own_index * owner_cols) // HEAD_WIDTH, owner_heads, axis=1
+    )
+    num_own = summed[:, :, :owner_cols].reshape(request_count * NEW_TOKENS, owner_cols)
+    den_own = summed[:, :, owner_cols:].reshape(request_count * NEW_TOKENS, owner_heads)
+    totals = den_own + fresh_den_own
+    attended_own = ((num_own + fresh_num_own) / jnp.repeat(totals, head_repeat, axis=1)).astype(
         jnp.bfloat16
     )
+    attended = lax.all_gather(attended_own, "blk", axis=1, tiled=True)
     return jnp.dot(attended, output_weight, preferred_element_type=jnp.float32).astype(jnp.bfloat16)
 
 

time: 419 us -> 362 us (0.86)
  waiting for transfers between devices: 228 us -> 175 us
  matrix products: 46.7 us -> 39.1 us
    psum x1 -> x0, waiting for transfers between devices: 125 us -> none  [local(): lax.psum(jnp.concatenate([num_tok, den_tok, jnp.zeros((den_tok.shape[0],...]
    all_gather x0 -> x1, waiting for transfers between devices: none -> 53.3 us  [local(): attended = lax.all_gather(attended_own, 'blk', axis=1, tiled=True)]
    all_to_all x0 -> x1, waiting for transfers between devices: none -> 19.5 us  [local(): received = lax.all_to_all(packed, 'blk', 0, 0, tiled=True)]
    concatenate x1 -> x0, local copies, waits for them, and re-layouts: 7.86 us -> none  [local(): jnp.concatenate([num_tok, den_tok, jnp.zeros((den_tok.shape[0], pad_width...]
    reshape x4 -> x2, local copies, waits for them, and re-layouts: 14.9 us -> 8.55 us  [to_tokens(): split_head_shape.transpose(order_axes)]
    transpose x3 -> x1, local copies, waits for them, and re-layouts: 7.2 us -> 1.17 us  [to_tokens(): split_head_shape.transpose(order_axes)]
    unnamed x22 -> x23, local copies, waits for them, and re-layouts: 15.2 us -> 15.3 us
  transfers between devices with their start and end apart: 11 -> 12, of which waited for: 10 -> 11; matrix products, arithmetic and copies ran while one was open for 13% -> 16% of each run, Pallas kernels for 0% -> 0%
where the time goes in v2:
time: 362 us; the launch traced here: 356 us
  waiting for transfers between devices  175 us (48%)
  local copies, waits for them, and re-layouts  103 us (28%)
  matrix products  39.1 us (11%)
  between operations  14 us (4%)
  other arithmetic  12.9 us (4%)
  starting transfers between devices  12.4 us (3%)
    all_gather x1, waiting for transfers between devices, local(): attended = lax.all_gather(attended_own, 'blk', axis=1, tiled=True)  53.3 us
    ppermute x8, waiting for transfers between devices, butterfly(): value = combine(value, lax.ppermute(value, 'blk', pairs))  35.9 us
    all_gather x1, waiting for transfers between devices, local(): lax.all_gather(jnp.concatenate([query_part, keyval_part], axis=1), 'blk',...  35 us
    all_gather x1, waiting for transfers between devices, local(): gathered = lax.all_gather(layer_input_tokens, 'blk', axis=1, tiled=True)  30.5 us
    all_to_all x1, waiting for transfers between devices, local(): received = lax.all_to_all(packed, 'blk', 0, 0, tiled=True)  19.5 us
    unnamed x23, local copies, waits for them, and re-layouts  15.3 us
    another operation x2, local copies, waits for them, and re-layouts, local(): query_vectors.reshape(request_count, NEW_TOKENS, KEY_VALUE_HEADS, query_g...  10.4 us
    slice x2, local copies, waits for them, and re-layouts, apply_rotation(): cos_val = jnp.cos(angles[:, 0::2])  9.56 us
  transfers between devices with their start and end apart: 12, of which 11 were waited for; matrix products, arithmetic and copies ran while one was open for 16% of the time, Pallas kernels for 0%

profile of v2, /device:TPU:0, one launch (start us, length us, event | category | flops | bytes accessed | tf_op | source)
XLA Modules:
  0.0 356.4 jit_solution(8480461503229381404)
XLA Ops:
  6.5 0.7 all-gather.5.cloned.1.call-update
  7.3 0.7 add_convert_fusion
  8.3 2.3 slice.48
  10.6 0.8 select_reduce_fusion.2
  12.0 7.3 %slice.45 = f32[192,256]{1,0:T(8,128)} slice(f32[192,512]{1,0:T(8,128)S(1)} %broadcast_multiply_fusion), slice={[0:192:1], [0:512:2]} | slice | bytes 393216 | tf_op jit(solution)/shard_map/slice | solution.py:25
  19.3 8.6 %gather_fusion = bf16[192,64,512]{2,1,0:T(8,128)(2,1)} fusion(bf16[16,64,512]{2,1,0:T(8,128)(2,1)S(1)} %copy-done.2, s32[1024]{0:T(1024)S(1)} %pad_clamp_fusion.2), kind=kCustom, calls=%fused_computation | custom fusion | bytes 25166592 | tf_op jit(solution)/shard_map/gather | solution.py:102
  28.3 0.7 fusion.44
  29.0 30.5 %all-gather.5.cloned.1.call-done = bf16[192,8192]{1,0:T(8,128)(2,1)} async-done(((bf16[192,512]{1,0:T(8,128)(2,1)}), bf16[192,8192]{1,0:T(8,128)(2,1)}) %all-gather.5.cloned.1.call-update) | async-done | bytes 3145744 | tf_op jit(solution)/shard_map/all_gather | solution.py:85
  59.5 2.8 fusion
  62.3 2.4 fusion.9
  65.1 1.2 fusion.39
  66.2 1.7 slice.49
  67.9 1.7 slice.47
  69.6 1.3 collective-permute-start.1
  71.0 2.6 collective-permute-done.1
  74.2 3.5 collective-permute-done.2
  77.6 1.6 collective-permute-start.3
  79.2 3.3 collective-permute-done.3
  82.7 6.5 %fusion.48 = f32[192,1,512]{2,1,0:T(1,128)S(1)} fusion(bf16[192,64,1]{1,2,0:T(2,128)(2,1)S(1)} %copy.154, bf16[192,64,512]{2,1,0:T(8,128)(2,1)} %gather_fusion), kind=kOutput, calls=%fused_computation.123 | convolution fusion | flops 12582912 | bytes 13000704 | tf_op jit(solution)/shard_map/gk,gkq->gq/dot_general | solution.py:103
  89.1 5.3 %convolution_add_fusion = f32[192,512]{1,0:T(8,128)S(1)} fusion(bf16[8192,512]{1,0:T(8,128)(2,1)} %param.15, f32[192,1,512]{2,1,0:T(1,128)S(1)} %fusion.48, bf16[192,8192]{1,0:T(8,128)(2,1)S(1)} %copy-done.4, f32[8192]{0:T(1024)S(1)} %copy-done.9, f32[192]{0:T(256)S(1)} %add_rsqrt_fusion), kind=kOutput, calls=%fused_computation.26 | convolution fusion | flops 1617002496 | bytes 12354304 | tf_op jit(solution)/shard_map/dot_general | solution.py:110
  94.4 6.8 %slice.46 = f32[192,256]{1,0:T(8,128)S(1)} slice(f32[192,512]{1,0:T(8,128)S(1)} %convolution_add_fusion), slice={[0:192:1], [1:512:2]} | slice | bytes 393216 | tf_op jit(solution)/shard_map/slice | solution.py:28
  101.3 6.7 %slice.44 = f32[192,256]{1,0:T(8,128)S(1)} slice(f32[192,512]{1,0:T(8,128)S(1)} %convolution_add_fusion), slice={[0:192:1], [0:512:2]} | slice | bytes 393216 | tf_op jit(solution)/shard_map/slice | solution.py:27
  108.7 0.7 pad_maximum_fusion.1
  109.4 12.3 %copy.132 = bf16[16,128,2048]{1,2,0:T(8,128)(2,1)} copy(bf16[16,128,2048]{2,1,0:T(8,128)(2,1)} %param.20) | data formatting | bytes 16777216 | tf_op args[7]
  122.3 35.0 %all-gather.9.cloned.1.call-done = bf16[192,10240]{1,0:T(8,128)(2,1)} async-done(((bf16[192,640]{1,0:T(8,128)(2,1)}), bf16[192,10240]{1,0:T(8,128)(2,1)}) %all-gather.9.cloned.1.call-update) | async-done | bytes 3932176 | tf_op jit(solution)/shard_map/all_gather | solution.py:122
  157.3 2.9 copy.163
  160.2 2.2 slice.66
  162.4 1.0 slice.68
  163.4 6.2 %reshape_reshape.12 = bf16[64,3,8,8,128]{4,3,2,1,0:T(8,128)(2,1)} reshape(bf16[192,16,512]{2,1,0:T(8,128)(2,1)} %slice.66) | data formatting | bytes 6291456 | tf_op jit(solution)/shard_map/reshape;reshape | solution.py:131
  169.6 4.2 %copy.181 = bf16[64,3,8,8,128]{4,3,1,2,0:T(8,128)(2,1)} copy(bf16[64,3,8,8,128]{4,3,2,1,0:T(8,128)(2,1)} %reshape_reshape.12) | data formatting | bytes 6291456 | tf_op jit(solution)/shard_map/reshape;reshape | solution.py:131
  173.8 2.6 gather_fusion.1
  176.4 3.5 fusion.46
  180.5 2.0 fusion.43
  182.5 3.7 %fusion.47 = (f32[64,8,24]{2,1,0:T(8,128)S(1)}, f32[64,8,24,3]{2,3,1,0:T(4,128)S(1)}) fusion(bf16[64,3,1,8,128]{4,3,2,1,0:T(8,128)(2,1)S(1)} %get-tuple-element.10, bf16[64,3,8,8,128]{4,3,2,1,0:T(8,128)(2,1)} %reshape_reshape.12, pred[24,3]{0,1:T(4,128)(4,1)S(1)} %iota_compare_fusion.2), kind=kOutput, calls=%fused_computation.122 | convolution fusion | flops 9535488 | bytes 3735624 | tf_op jit(solution)/shard_map/rkqd,rjkd->rkqj/dot_general | solution.py:175
  186.5 1.3 collective-permute-done.4
  188.4 7.9 %collective-permute-done.5 = f32[64,8,24]{2,1,0:T(8,128)S(1)} collective-permute-done((f32[64,8,24]{2,1,0:T(8,128)S(1)}, f32[64,8,24]{2,1,0:T(8,128)S(1)}, u32[]{:S(2)}, u32[]{:S(2)}) %collective-permute-start.5) | collective-permute-done | bytes 49184 | tf_op jit(solution)/shard_map/ppermute | solution.py:65
  196.4 2.0 collective-permute-start.6
  198.3 5.9 %collective-permute-done.6 = f32[64,8,24]{2,1,0:T(8,128)S(1)} collective-permute-done((f32[64,8,24]{2,1,0:T(8,128)S(1)}, f32[64,8,24]{2,1,0:T(8,128)S(1)}, u32[]{:S(2)}, u32[]{:S(2)}) %collective-permute-start.6) | collective-permute-done | bytes 49184 | tf_op jit(solution)/shard_map/ppermute | solution.py:65
  204.3 2.0 collective-permute-start.7
  206.3 11.4 %collective-permute-done.7 = f32[64,8,24]{2,1,0:T(8,128)S(1)} collective-permute-done((f32[64,8,24]{2,1,0:T(8,128)S(1)}, f32[64,8,24]{2,1,0:T(8,128)S(1)}, u32[]{:S(2)}, u32[]{:S(2)}) %collective-permute-start.7) | collective-permute-done | bytes 49184 | tf_op jit(solution)/shard_map/ppermute | solution.py:65
  218.4 0.9 fusion.7
  219.3 5.8 %fusion.5 = f32[16,8,3,8,128]{4,3,2,1,0:T(8,128)} fusion(bf16[16,128,2,8,128]{1,4,3,2,0:T(8,128)(2,1)} %bitcast.110, f32[16,8,24,128]{3,2,1,0:T(8,128)S(1)} %get-tuple-element.20, f32[16,8,24]{2,1,0:T(8,128)S(1)} %gather_fusion.2, pred[16,128]{1,0:T(8,128)(4,1)S(1)} %fusion.26), kind=kOutput, calls=%fused_computation.21 | convolution fusion | flops 101842944 | bytes 7354368 | tf_op jit(solution)/shard_map/skqp,spkd->skqd/dot_general | solution.py:188
  225.9 1.1 copy.142
  227.0 1.6 copy.182
  228.6 1.4 reshape_reshape.14
  230.0 1.7 maximum_bitcast_fusion
  231.8 1.9 copy.143
  233.7 3.7 %all-to-all-start = ((f32[16,16,3,516]{3,1,2,0:T(8,128)}), f32[16,16,3,516]{3,1,2,0:T(8,128)S(1)}, u32[]{:S(2)}, u32[]{:S(2)}) async-start(f32[16,16,3,516]{3,1,2,0:T(8,128)} %copy.143), calls=%async_computation | async-start | bytes 3932160 | tf_op jit(solution)/shard_map/all_to_all | solution.py:209
  237.8 1.6 fusion.15
  239.5 1.1 copy.150
  240.5 1.2 copy.151
  241.7 1.4 reshape.300
  243.3 2.8 convolution_bitcast_fusion
  246.1 3.4 copy.180
  249.5 7.2 %reshape.298 = f32[192,8192]{1,0:T(8,128)} reshape(f32[64,3,8,8,128]{4,3,2,1,0:T(8,128)} %bitcast.111) | data formatting | bytes 12582912 | tf_op jit(solution)/shard_map/reshape | solution.py:57
  256.7 19.5 %all-to-all-done = f32[16,16,3,516]{3,1,2,0:T(8,128)S(1)} async-done(((f32[16,16,3,516]{3,1,2,0:T(8,128)}), f32[16,16,3,516]{3,1,2,0:T(8,128)S(1)}, u32[]{:S(2)}, u32[]{:S(2)}) %all-to-all-start) | async-done | bytes 1585184 | tf_op jit(solution)/shard_map/all_to_all | solution.py:209
  276.2 2.6 copy.144
  278.7 3.1 reshape.295
  281.9 1.6 copy.145
  283.5 1.4 dot_general.42
  284.9 1.0 fusion.23
  287.5 1.8 fusion.21
  289.4 53.3 %all-gather.7.cloned.1.call-done = bf16[192,8192]{1,0:T(8,128)(2,1)} async-done(((bf16[192,512]{1,0:T(8,128)(2,1)}), bf16[192,8192]{1,0:T(8,128)(2,1)}) %all-gather.7.cloned.1.call-update) | async-done | bytes 3145744 | tf_op jit(solution)/shard_map/all_gather | solution.py:240
  342.7 6.9 %convolution_convert_fusion = bf16[192,512]{1,0:T(8,128)(2,1)} fusion(bf16[192,8192]{1,0:T(8,128)(2,1)} %all-gather.7.cloned.1.call-done, bf16[8192,512]{1,0:T(8,128)(2,1)} %param.17), kind=kOutput, calls=%fused_computation.27 | convolution fusion | flops 1610711040 | bytes 11730944 | tf_op jit(solution)/shard_map/dot_general | solution.py:241
  (99 shorter events, 9.0 us)
Async XLA Ops:
  6.5 58.5 %copy-start = (bf16[8192,128]{1,0:T(8,128)(2,1)S(1)}, bf16[8192,128]{1,0:T(8,128)(2,1)}, u32[]{:S(2)}) copy-start(bf16[8192,128]{1,0:T(8,128)(2,1)} %param.16) | copy-start | bytes 6291460
  6.5 12.7 %copy-start.2 = (bf16[16,64,512]{2,1,0:T(8,128)(2,1)S(1)}, bf16[16,64,512]{2,1,0:T(8,128)(2,1)}, u32[]{:S(2)}) copy-start(bf16[16,64,512]{2,1,0:T(8,128)(2,1)} %param.19) | copy-start | bytes 3145732
  6.5 52.9 %all-gather.5.cloned.1.call-start = ((), (), s32[]{:S(2)}) async-start(), calls=%async_computation.1 | async-start | bytes 3342336 | tf_op jit(solution)/shard_map/all_gather | solution.py:85
  7.3 150.0 %all-gather.9.cloned.1.call-start = ((), (), s32[]{:S(2)}) async-start(), calls=%async_computation.3 | async-start | bytes 4177920 | tf_op jit(solution)/shard_map/all_gather | solution.py:122
  19.2 8.7 %copy-start.6 = (f32[192,64]{1,0:T(8,128)S(1)}, f32[192,64]{1,0:T(8,128)}, u32[]{:S(2)}) copy-start(f32[192,64]{1,0:T(8,128)} %slice.48) | copy-start | bytes 147460
  19.3 9.1 %copy-start.5 = (f32[192,256]{1,0:T(8,128)S(1)}, f32[192,256]{1,0:T(8,128)}, u32[]{:S(2)}) copy-start(f32[192,256]{1,0:T(8,128)} %slice.45) | copy-start | bytes 589828
  27.9 34.3 %copy-start.9 = (f32[8192]{0:T(1024)S(1)}, f32[8192]{0:T(1024)}, u32[]{:S(2)}) copy-start(f32[8192]{0:T(1024)} %param.14) | copy-start | bytes 98308
  59.5 2.8 copy-start.3
  64.7 4.9 %collective-permute-start = (bf16[192,64]{0,1:T(8,128)(2,1)S(1)}, bf16[192,64]{0,1:T(8,128)(2,1)S(1)}, u32[]{:S(2)}, u32[]{:S(2)}) collective-permute-start(bf16[192,64]{0,1:T(8,128)(2,1)S(1)} %fusion.9), channel_id=1, source_target_pairs={{0,1},{1,0},{2,3},{3,2},{4,5},{5,4},{6,7},{7,6},{8,9},{9,8},{10,11... | collective-permute-start | bytes 73736 | tf_op jit(solution)/shard_map/ppermute | solution.py:65
  69.6 4.0 %collective-permute-start.1 = (bf16[192,64]{0,1:T(8,128)(2,1)S(1)}, bf16[192,64]{0,1:T(8,128)(2,1)S(1)}, u32[]{:S(2)}, u32[]{:S(2)}) collective-permute-start(bf16[192,64]{0,1:T(8,128)(2,1)S(1)} %add.180), channel_id=1, source_target_pairs={{0,2},{1,3},{2,0},{3,1},{4,6},{5,7},{6,4},{7,5},{8,10},{9,11},{10,... | collective-permute-start | bytes 73736 | tf_op jit(solution)/shard_map/ppermute | solution.py:65
  73.6 4.0 %collective-permute-start.2 = (bf16[192,64]{0,1:T(8,128)(2,1)S(1)}, bf16[192,64]{0,1:T(8,128)(2,1)S(1)}, u32[]{:S(2)}, u32[]{:S(2)}) collective-permute-start(bf16[192,64]{0,1:T(8,128)(2,1)S(1)} %add.181), channel_id=1, source_target_pairs={{0,4},{1,5},{2,6},{3,7},{4,0},{5,1},{6,2},{7,3},{8,12},{9,13},{10,... | collective-permute-start | bytes 73736 | tf_op jit(solution)/shard_map/ppermute | solution.py:65
  77.6 4.9 %collective-permute-start.3 = (bf16[192,64]{0,1:T(8,128)(2,1)S(1)}, bf16[192,64]{0,1:T(8,128)(2,1)S(1)}, u32[]{:S(2)}, u32[]{:S(2)}) collective-permute-start(bf16[192,64]{0,1:T(8,128)(2,1)S(1)} %add.182), channel_id=1, source_target_pairs={{0,8},{1,9},{2,10},{3,11},{4,12},{5,13},{6,14},{7,15},{8,0},{9,1},... | collective-permute-start | bytes 73736 | tf_op jit(solution)/shard_map/ppermute | solution.py:65
  82.6 6.5 %copy-start.4 = (bf16[192,8192]{1,0:T(8,128)(2,1)S(1)}, bf16[192,8192]{1,0:T(8,128)(2,1)}, u32[]{:S(2)}) copy-start(bf16[192,8192]{1,0:T(8,128)(2,1)} %all-gather.5.cloned.1.call-done) | copy-start | bytes 9437188
  109.4 12.3 %copy-start.7 = (s32[64,4]{0,1:T(4,128)S(1)}, s32[64,4]{0,1:T(4,128)}, u32[]{:S(2)}) copy-start(s32[64,4]{0,1:T(4,128)} %param.24) | copy-start | bytes 3076
  109.4 12.5 %copy-start.8 = (s32[64]{0:T(128)S(1)}, s32[64]{0:T(128)}, u32[]{:S(2)}) copy-start(s32[64]{0:T(128)} %param.23) | copy-start | bytes 772
  186.2 1.6 collective-permute-start.4
  187.8 8.5 %collective-permute-start.5 = (f32[64,8,24]{2,1,0:T(8,128)S(1)}, f32[64,8,24]{2,1,0:T(8,128)S(1)}, u32[]{:S(2)}, u32[]{:S(2)}) collective-permute-start(f32[64,8,24]{2,1,0:T(8,128)S(1)} %max.16), channel_id=1, source_target_pairs={{0,2},{1,3},{2,0},{3,1},{4,6},{5,7},{6,4},{7,5},{8,10},{9,11},{10,... | collective-permute-start | bytes 147464 | tf_op jit(solution)/shard_map/ppermute | solution.py:65
  196.4 7.9 %collective-permute-start.6 = (f32[64,8,24]{2,1,0:T(8,128)S(1)}, f32[64,8,24]{2,1,0:T(8,128)S(1)}, u32[]{:S(2)}, u32[]{:S(2)}) collective-permute-start(f32[64,8,24]{2,1,0:T(8,128)S(1)} %max.17), channel_id=1, source_target_pairs={{0,4},{1,5},{2,6},{3,7},{4,0},{5,1},{6,2},{7,3},{8,12},{9,13},{10,... | collective-permute-start | bytes 147464 | tf_op jit(solution)/shard_map/ppermute | solution.py:65
  204.3 13.5 %collective-permute-start.7 = (f32[64,8,24]{2,1,0:T(8,128)S(1)}, f32[64,8,24]{2,1,0:T(8,128)S(1)}, u32[]{:S(2)}, u32[]{:S(2)}) collective-permute-start(f32[64,8,24]{2,1,0:T(8,128)S(1)} %max.18), channel_id=1, source_target_pairs={{0,8},{1,9},{2,10},{3,11},{4,12},{5,13},{6,14},{7,15},{8,0},{9,1},... | collective-permute-start | bytes 147464 | tf_op jit(solution)/shard_map/ppermute | solution.py:65
  233.7 42.5 %all-to-all-start = ((f32[16,16,3,516]{3,1,2,0:T(8,128)}), f32[16,16,3,516]{3,1,2,0:T(8,128)S(1)}, u32[]{:S(2)}, u32[]{:S(2)}) async-start(f32[16,16,3,516]{3,1,2,0:T(8,128)} %copy.143), calls=%async_computation | async-start | bytes 3932160 | tf_op jit(solution)/shard_map/all_to_all | solution.py:209
  237.4 105.3 %all-gather.7.cloned.1.call-start = ((), (), s32[]{:S(2)}) async-start(), calls=%async_computation.2 | async-start | bytes 3342336 | tf_op jit(solution)/shard_map/all_gather | solution.py:240
  342.7 7.0 %copy-start.1 = (bf16[8192,128]{1,0:T(8,128)(2,1)S(1)}, bf16[8192,128]{1,0:T(8,128)(2,1)}, u32[]{:S(2)}) copy-start(bf16[8192,128]{1,0:T(8,128)(2,1)} %param.16) | copy-start | bytes 6291460
Sparse Core Ops, SparseCore 0:
  9.5 49.9 all-gather.4
  109.5 47.7 all-gather.8
  289.5 53.1 all-gather.6

commit v3 on v2

--- a/solution.py
+++ b/solution.py
@@ -3,6 +3,8 @@
 import jax
 import jax.numpy as jnp
 from jax import lax
+from jax.experimental import pallas as pl
+from jax.experimental.pallas import tpu as pltpu
 from jax.sharding import PartitionSpec as P
 
 QUERY_HEADS = 64
@@ -31,6 +33,36 @@
         axis=-1,
     ).reshape(values.shape)
     return jnp.where((columns < rot_limit)[None, :], turned, values)
+
+
+def rotation_kernel(values_ref, cos_ref, sine_ref, out_ref):
+    values = values_ref[...]
+    width = values.shape[1]
+    following = pltpu.roll(values, width - 1, 1)
+    preceding = pltpu.roll(values, 1, 1)
+    even = lax.broadcasted_iota(jnp.int32, values.shape, 1) % 2 == 0
+    cos_val = cos_ref[...]
+    sine_val = sine_ref[...]
+    out_ref[...] = jnp.where(
+        even, values * cos_val - following * sine_val, preceding * sine_val + values * cos_val
+    ).astype(out_ref.dtype)
+
+
+def rotate_columns(values, token_positions, global_cols, rot_limit):
+    pair_index = (global_cols % HEAD_WIDTH // 2).astype(jnp.float32)
+    inverse = jnp.exp(pair_index * (-2.0 * math.log(theta_base) / HEAD_WIDTH))
+    angles = token_positions[:, None] * inverse[None, :]
+    rotated = (global_cols < rot_limit)[None, :]
+    cos_val = jnp.where(rotated, jnp.cos(angles), 1.0)
+    sine_val = jnp.where(rotated, jnp.sin(angles), 0.0)
+    width = values.shape[1]
+    pad = -(-width // 128) * 128 - width
+    operands = [jnp.pad(a, ((0, 0), (0, pad))) for a in (values, cos_val, sine_val)]
+    out = pl.pallas_call(
+        rotation_kernel,
+        out_shape=jax.ShapeDtypeStruct(operands[0].shape, jnp.bfloat16),
+    )(*operands)
+    return out[:, :width]
 
 
 def normalize(layer_input_tokens, input_norm_gain):
@@ -106,33 +138,35 @@
     token_positions = positions_of(cached_lengths)
     query_cols = query_weight.shape[1]
     keyval_cols = key_value_weight.shape[1]
-    query_part = apply_rotation(
-        jnp.dot(normalized_input, query_weight, preferred_element_type=jnp.float32)
-        + adapter_query_update,
-        token_positions,
-        own_index * query_cols,
-        QUERY_HEADS * HEAD_WIDTH,
-    ).astype(jnp.bfloat16)
-    keyval_part = apply_rotation(
-        jnp.dot(normalized_input, key_value_weight, preferred_element_type=jnp.float32),
-        token_positions,
-        own_index * keyval_cols,
-        KEY_VALUE_HEADS * HEAD_WIDTH,
-    ).astype(jnp.bfloat16)
-    joined = lax.all_gather(
-        jnp.concatenate([query_part, keyval_part], axis=1), "blk", axis=1, tiled=False
-    )
+    both_parts = jnp.concatenate(
+        [
+            jnp.dot(normalized_input, query_weight, preferred_element_type=jnp.float32)
+            + adapter_query_update,
+            jnp.dot(normalized_input, key_value_weight, preferred_element_type=jnp.float32),
+        ],
+        axis=1,
+    )
+    global_cols = jnp.concatenate(
+        [
+            own_index * query_cols + jnp.arange(query_cols, dtype=jnp.int32),
+            own_index * keyval_cols + jnp.arange(keyval_cols, dtype=jnp.int32),
+        ]
+    )
+    limits = jnp.concatenate(
+        [
+            jnp.full((query_cols,), QUERY_HEADS * HEAD_WIDTH, jnp.int32),
+            jnp.full((keyval_cols,), KEY_VALUE_HEADS * HEAD_WIDTH, jnp.int32),
+        ]
+    )
+    rotated_parts = rotate_columns(both_parts, token_positions, global_cols, limits)
+    joined = lax.all_gather(rotated_parts, "blk", axis=1, tiled=False)
     query_vectors = joined[:, :, :query_cols].reshape(joined.shape[0], -1)
     key_value_rows = joined[:, :, query_cols:].reshape(joined.shape[0], -1)
     query_group_width = QUERY_HEADS // KEY_VALUE_HEADS
     query_feature_width = query_group_width * NEW_TOKENS
     score_scale = 1.0 / math.sqrt(HEAD_WIDTH)
-    query_req = (
-        query_vectors.reshape(
-            request_count, NEW_TOKENS, KEY_VALUE_HEADS, query_group_width, HEAD_WIDTH
-        )
-        .transpose(0, 2, 1, 3, 4)
-        .reshape(request_count, KEY_VALUE_HEADS, query_feature_width, HEAD_WIDTH)
+    query_split = query_vectors.reshape(
+        request_count, NEW_TOKENS, KEY_VALUE_HEADS, query_group_width, HEAD_WIDTH
     )
     fresh_token_rows = key_value_rows.reshape(
         request_count, NEW_TOKENS, 2, KEY_VALUE_HEADS, HEAD_WIDTH
@@ -156,7 +190,11 @@
     gathered_cache_pages = key_value_page_pool.reshape(
         request_page_count, PAGE_LENGTH, 2, KEY_VALUE_HEADS, HEAD_WIDTH
     )
-    query_page = query_req[page_req]
+    query_page = (
+        query_split[page_req]
+        .transpose(0, 2, 1, 3, 4)
+        .reshape(request_page_count, KEY_VALUE_HEADS, query_feature_width, HEAD_WIDTH)
+    )
     scores = (
         jnp.einsum(
             "skqd,spkd->skqp",
@@ -171,13 +209,18 @@
     req_peak = jnp.max(
         jnp.where(page_owner[:, :, None, None], page_peak[:, None], neg_large), axis=0
     )
+    query_wide = query_split.astype(jnp.float32)
+    fresh_keys = fresh_token_rows[:, :, 0].astype(jnp.float32)
     fresh_scores = (
-        jnp.einsum(
-            "rkqd,rjkd->rkqj",
-            query_req,
-            fresh_token_rows[:, :, 0],
-            preferred_element_type=jnp.float32,
+        jnp.stack(
+            [
+                jnp.sum(query_wide * fresh_keys[:, j][:, None, :, None, :], axis=-1)
+                for j in range(NEW_TOKENS)
+            ],
+            axis=-1,
         )
+        .transpose(0, 2, 1, 3, 4)
+        .reshape(request_count, KEY_VALUE_HEADS, query_feature_width, NEW_TOKENS)
         * score_scale
     )
     step_of = jnp.arange(query_feature_width, dtype=jnp.int32) // query_group_width
@@ -218,19 +261,30 @@
         precision=lax.Precision.HIGHEST,
     ).reshape(request_count, NEW_TOKENS, owner_cols + owner_heads)
     fresh_weights = jnp.where(fresh_ok, jnp.exp(fresh_masked - top_score[..., None]), 0.0)
-    fresh_num = jnp.einsum(
-        "rkqj,rjkd->rkqd",
-        fresh_weights.astype(jnp.bfloat16),
-        fresh_token_rows[:, :, 1],
+    fresh_by_head = (
+        fresh_weights.reshape(
+            request_count, KEY_VALUE_HEADS, NEW_TOKENS, query_group_width, NEW_TOKENS
+        )
+        .transpose(0, 2, 1, 3, 4)
+        .reshape(request_count, NEW_TOKENS, QUERY_HEADS, NEW_TOKENS)
+    )
+    first_head = (own_index * owner_cols) // HEAD_WIDTH
+    weights_own = lax.dynamic_slice_in_dim(fresh_by_head, first_head, owner_heads, axis=2)
+    value_col = (
+        KEY_VALUE_HEADS * HEAD_WIDTH
+        + (first_head // query_group_width) * HEAD_WIDTH
+        + (own_index * owner_cols) % HEAD_WIDTH
+    )
+    values_own = lax.dynamic_slice_in_dim(
+        key_value_rows.reshape(request_count, NEW_TOKENS, -1), value_col, head_repeat, axis=2
+    )
+    fresh_num_own = jnp.einsum(
+        "rihj,rjd->rihd",
+        weights_own.astype(jnp.bfloat16),
+        values_own,
         preferred_element_type=jnp.float32,
-    )
-    fresh_den = jnp.sum(fresh_weights, axis=-1)
-    fresh_num_own = lax.dynamic_slice_in_dim(
-        to_tokens(fresh_num), own_index * owner_cols, owner_cols, axis=1
-    )
-    fresh_den_own = lax.dynamic_slice_in_dim(
-        to_tokens(fresh_den[..., None]), (own_index * owner_cols) // HEAD_WIDTH, owner_heads, axis=1
-    )
+    ).reshape(request_count * NEW_TOKENS, owner_cols)
+    fresh_den_own = jnp.sum(weights_own, axis=-1).reshape(request_count * NEW_TOKENS, owner_heads)
     num_own = summed[:, :, :owner_cols].reshape(request_count * NEW_TOKENS, owner_cols)
     den_own = summed[:, :, owner_cols:].reshape(request_count * NEW_TOKENS, owner_heads)
     totals = den_own + fresh_den_own

time: 362 us -> 345 us (0.953); the launches traced: 356 us -> 343 us
  local copies, waits for them, and re-layouts: 103 us -> 59.6 us
  waiting for transfers between devices: 175 us -> 199 us
  other arithmetic: 12.9 us -> 20.4 us
    slice x7 -> x0, local copies, waits for them, and re-layouts: 28.3 us -> none  [the longest x2 9.56 us: apply_rotation(): cos_val = jnp.cos(angles[:, 0::2])]
    all_gather x1, waiting for transfers between devices: 30.5 us -> 49.5 us  [local(): gathered = lax.all_gather(layer_input_tokens, 'blk', axis=1, tiled=True)]
    all_to_all x1, waiting for transfers between devices: 19.5 us -> 29.5 us  [local(): received = lax.all_to_all(packed, 'blk', 0, 0, tiled=True)]
    reshape x7 -> x0, local copies, waits for them, and re-layouts: 9.25 us -> none  [the longest x2 8.55 us: to_tokens(): split_head_shape.transpose(order_axes)]
    ppermute x8, waiting for transfers between devices: 35.9 us -> 29.2 us  [butterfly(): value = combine(value, lax.ppermute(value, 'blk', pairs))]
    reduce_sum x1 -> x2, other arithmetic: 1.63 us -> 6.78 us  [the longest x1 6.76 us: local(): jnp.sum(query_wide * fresh_keys[:, j][:, None, :, None, :], axis=-1)]
    dot_general x2 -> x1, matrix products: 6.51 us -> 1.37 us  [local(): jnp.einsum('rihj,rjd->rihd', weights_own.astype(jnp.bfloat16), values_own...]
    reshape x2 -> x1, local copies, waits for them, and re-layouts: 4.98 us -> 0.17 us  [to_tokens(): request_first_layout.reshape((request_count, KEY_VALUE_HEADS, NEW_TOKENS,...]
  transfers between devices with their start and end apart: 12 -> 12, of which waited for: 11 -> 9; matrix products, arithmetic and copies ran while one was open for 16% -> 11% of each run, Pallas kernels for 0% -> 0%
where the time goes in v3:
time: 345 us; the launch traced here: 343 us
  waiting for transfers between devices  199 us (58%)
  local copies, waits for them, and re-layouts  59.6 us (17%)
  matrix products  36 us (10%)
  other arithmetic  20.4 us (6%)
  between operations  13.7 us (4%)
  starting transfers between devices  12.5 us (4%)
    all_gather x1, waiting for transfers between devices, local(): attended = lax.all_gather(attended_own, 'blk', axis=1, tiled=True)  53.3 us
    all_gather x1, waiting for transfers between devices, local(): gathered = lax.all_gather(layer_input_tokens, 'blk', axis=1, tiled=True)  49.5 us
    all_gather x1, waiting for transfers between devices, local(): joined = lax.all_gather(rotated_parts, 'blk', axis=1, tiled=False)  36.5 us
    all_to_all x1, waiting for transfers between devices, local(): received = lax.all_to_all(packed, 'blk', 0, 0, tiled=True)  29.5 us
    ppermute x8, waiting for transfers between devices, butterfly(): value = combine(value, lax.ppermute(value, 'blk', pairs))  29.2 us
    unnamed x27, local copies, waits for them, and re-layouts  15.4 us
    ppermute x8, starting transfers between devices, butterfly(): value = combine(value, lax.ppermute(value, 'blk', pairs))  8.72 us
    gather x1, local copies, waits for them, and re-layouts, local(): up_weight_rows = adapter_up_weight[token_cache_slot]  8.12 us
  transfers between devices with their start and end apart: 12, of which 9 were waited for; matrix products, arithmetic and copies ran while one was open for 11% of the time, Pallas kernels for 0%

profile of v3, /device:TPU:0, one launch (start us, length us, event | category | flops | bytes accessed | tf_op | source)
XLA Modules:
  0.0 343.4 jit_solution(16215735750313740680)
XLA Ops:
  6.5 0.7 all-gather.5.cloned.1.call-update
  7.3 0.8 select_reduce_fusion.2
  8.3 0.7 add_convert_fusion
  9.2 0.7 fusion.44
  9.9 49.5 %all-gather.5.cloned.1.call-done = bf16[192,8192]{1,0:T(8,128)(2,1)} async-done(((bf16[192,512]{1,0:T(8,128)(2,1)}), bf16[192,8192]{1,0:T(8,128)(2,1)}) %all-gather.5.cloned.1.call-update) | async-done | bytes 3145744 | tf_op jit(solution)/shard_map/all_gather | solution.py:117
  59.5 2.8 fusion
  62.3 2.5 fusion.11
  64.8 0.3 collective-permute-start
  65.1 2.8 fusion.20
  68.1 1.3 collective-permute-start.1
  69.5 2.6 collective-permute-done.1
  72.3 8.1 %gather_fusion = bf16[192,64,512]{2,1,0:T(8,128)(2,1)} fusion(bf16[16,64,512]{2,1,0:T(8,128)(2,1)S(1)} %copy-done.2, s32[1024]{0:T(1024)S(1)} %pad_clamp_fusion.2), kind=kCustom, calls=%fused_computation | custom fusion | bytes 25166592 | tf_op jit(solution)/shard_map/gather | solution.py:134
  80.5 1.9 collective-permute-start.3
  82.4 3.0 fusion.50
  85.6 6.5 %fusion.57 = f32[192,1,512]{2,1,0:T(1,128)S(1)} fusion(bf16[192,64,1]{1,2,0:T(2,128)(2,1)S(1)} %copy.228, bf16[192,64,512]{2,1,0:T(8,128)(2,1)} %gather_fusion), kind=kOutput, calls=%fused_computation.123 | convolution fusion | flops 12582912 | bytes 13000704 | tf_op jit(solution)/shard_map/gk,gkq->gq/dot_general | solution.py:135
  92.0 5.3 %convolution_add_fusion = f32[192,512]{1,0:T(8,128)S(1)} fusion(bf16[8192,512]{1,0:T(8,128)(2,1)} %param.15, f32[192,1,512]{2,1,0:T(1,128)S(1)} %fusion.57, bf16[192,8192]{1,0:T(8,128)(2,1)S(1)} %copy-done.8, f32[8192]{0:T(1024)S(1)} %copy-done.11, f32[192]{0:T(256)S(1)} %add_rsqrt_fusion), kind=kOutput, calls=%fused_computation.27 | convolution fusion | flops 1617002496 | bytes 12354304 | tf_op jit(solution)/shard_map/dot_general | solution.py:143
  97.4 0.8 pad_maximum_fusion.values_ref
  98.2 2.4 shard_map.127
  100.7 12.3 %copy.192 = bf16[16,128,2048]{1,2,0:T(8,128)(2,1)} copy(bf16[16,128,2048]{2,1,0:T(8,128)(2,1)} %param.20) | data formatting | bytes 16777216 | tf_op args[7]
  113.6 36.5 %all-gather.9.cloned.1.call-done = bf16[192,10240]{1,0:T(8,128)(2,1)} async-done(((bf16[192,640]{1,0:T(8,128)(2,1)}), bf16[192,10240]{1,0:T(8,128)(2,1)}) %all-gather.9.cloned.1.call-update) | async-done | bytes 3932176 | tf_op jit(solution)/shard_map/all_gather | solution.py:162
  150.1 2.9 copy.242
  152.9 2.2 slice.48
  155.3 6.3 %reshape_reshape.15 = bf16[64,3,8,8,128]{4,3,2,1,0:T(8,128)(2,1)} reshape(bf16[192,16,512]{2,1,0:T(8,128)(2,1)} %slice.48) | data formatting | bytes 6291456 | tf_op jit(solution)/shard_map/reshape;reshape | solution.py:168
  161.7 6.8 %fusion.3 = (f32[64,3,8,8]{3,2,1,0:T(8,128)S(1)}, f32[64,3,8,8]{3,2,1,0:T(8,128)S(1)}, f32[64,3,8,8]{3,2,1,0:T(8,128)S(1)}) fusion(bf16[64,3,8,8,128]{4,3,2,1,0:T(8,128)(2,1)} %reshape_reshape.15, f32[64,8,128]{2,1,0:T(8,128)S(1)} %get-tuple-element.16, f32[64,8,128]{2,1,0:T(8,128)S(1)} %get-tuple-element.15, f32[64,8,128]{2,1,0:T(8,128)S(1)} %get-tuple-element.14), kind=kLoop, calls=%fused_computation.12 | loop fusion | flops 10973184 | bytes 4079616 | tf_op jit(solution)/shard_map/reduce_sum | solution.py:217
  168.5 0.3 copy.195
  168.8 0.3 copy.196
  169.0 0.3 copy.197
  169.6 3.5 %gather_fusion.1 = bf16[16,3,8,8,128]{4,3,2,1,0:T(8,128)(2,1)} fusion(bf16[64,3,8,8,128]{4,3,2,1,0:T(8,128)(2,1)} %reshape_reshape.15, s32[1024]{0:T(1024)S(1)} %pad_clamp_fusion.1), kind=kCustom, calls=%fused_computation.1 | custom fusion | bytes 1572928 | tf_op jit(solution)/shard_map/gather | solution.py:194
  173.1 4.9 %fusion.56 = (f32[16,8,24]{2,1,0:T(8,128)S(1)}, f32[16,8,24,128]{3,2,1,0:T(8,128)}) fusion(bf16[16,128,2,8,128]{1,4,3,2,0:T(8,128)(2,1)} %bitcast.117, pred[16,128]{1,0:T(8,128)(4,1)S(1)} %fusion.38, bf16[16,3,8,8,128]{4,3,2,1,0:T(8,128)(2,1)} %gather_fusion.1), kind=kOutput, calls=%fused_computation.122 | convolution fusion | flops 101839872 | bytes 6567936 | tf_op jit(solution)/shard_map/skqd,spkd->skqp/dot_general | solution.py:199
  178.0 0.5 select_reduce_fusion
  178.6 0.3 collective-permute-start.4
  179.0 1.3 collective-permute-done.4
  180.3 0.6 collective-permute-start.5
  180.9 7.9 %collective-permute-done.5 = f32[64,8,24]{2,1,0:T(8,128)S(1)} collective-permute-done((f32[64,8,24]{2,1,0:T(8,128)S(1)}, f32[64,8,24]{2,1,0:T(8,128)S(1)}, u32[]{:S(2)}, u32[]{:S(2)}) %collective-permute-start.5) | collective-permute-done | bytes 49184 | tf_op jit(solution)/shard_map/ppermute | solution.py:97
  188.8 2.0 collective-permute-start.6
  190.8 5.9 %collective-permute-done.6 = f32[64,8,24]{2,1,0:T(8,128)S(1)} collective-permute-done((f32[64,8,24]{2,1,0:T(8,128)S(1)}, f32[64,8,24]{2,1,0:T(8,128)S(1)}, u32[]{:S(2)}, u32[]{:S(2)}) %collective-permute-start.6) | collective-permute-done | bytes 49184 | tf_op jit(solution)/shard_map/ppermute | solution.py:97
  196.7 2.0 collective-permute-start.7
  198.8 11.4 %collective-permute-done.7 = f32[64,8,24]{2,1,0:T(8,128)S(1)} collective-permute-done((f32[64,8,24]{2,1,0:T(8,128)S(1)}, f32[64,8,24]{2,1,0:T(8,128)S(1)}, u32[]{:S(2)}, u32[]{:S(2)}) %collective-permute-start.7) | collective-permute-done | bytes 49184 | tf_op jit(solution)/shard_map/ppermute | solution.py:97
  210.3 0.6 gather_fusion.2
  210.8 4.5 %fusion.8 = f32[16,8,3,8,128]{4,3,2,1,0:T(8,128)S(1)} fusion(bf16[16,128,2,8,128]{1,4,3,2,0:T(8,128)(2,1)} %bitcast.118, f32[16,8,24,128]{3,2,1,0:T(8,128)S(1)} %copy-done.5, f32[16,8,24]{2,1,0:T(8,128)S(1)} %gather_fusion.2, pred[16,128]{1,0:T(8,128)(4,1)S(1)} %fusion.38), kind=kOutput, calls=%fused_computation.24 | convolution fusion | flops 101842944 | bytes 7354368 | tf_op jit(solution)/shard_map/skqp,spkd->skqd/dot_general | solution.py:231
  215.4 0.9 fusion.9
  216.5 1.4 reshape_reshape.17
  218.1 0.7 gather_fusion.3
  218.7 0.4 copy.208
  219.1 1.6 maximum_bitcast_fusion
  220.7 1.9 copy.209
  222.6 3.7 %all-to-all-start = ((f32[16,16,3,516]{3,1,2,0:T(8,128)}), f32[16,16,3,516]{3,1,2,0:T(8,128)S(1)}, u32[]{:S(2)}, u32[]{:S(2)}) async-start(f32[16,16,3,516]{3,1,2,0:T(8,128)} %copy.209), calls=%async_computation | async-start | bytes 3932160 | tf_op jit(solution)/shard_map/all_to_all | solution.py:252
  226.7 1.4 copy.213
  228.1 1.4 copy.214
  229.5 0.3 copy.215
  229.8 3.4 reshape_reshape.19
  234.1 1.4 fusion.31
  235.5 29.5 %all-to-all-done = f32[16,16,3,516]{3,1,2,0:T(8,128)S(1)} async-done(((f32[16,16,3,516]{3,1,2,0:T(8,128)}), f32[16,16,3,516]{3,1,2,0:T(8,128)S(1)}, u32[]{:S(2)}, u32[]{:S(2)}) %all-to-all-start) | async-done | bytes 1585184 | tf_op jit(solution)/shard_map/all_to_all | solution.py:252
  265.1 2.5 copy.210
  267.6 3.1 reshape.306
  270.7 1.6 copy.211
  272.3 1.4 dot_general.38
  273.7 1.0 fusion.35
  275.1 0.3 copy.212
  275.3 0.2 reshape.307
  275.5 0.3 broadcast_in_dim.216
  275.8 0.8 fusion.21
  276.6 53.3 %all-gather.7.cloned.1.call-done = bf16[192,8192]{1,0:T(8,128)(2,1)} async-done(((bf16[192,512]{1,0:T(8,128)(2,1)}), bf16[192,8192]{1,0:T(8,128)(2,1)}) %all-gather.7.cloned.1.call-update) | async-done | bytes 3145744 | tf_op jit(solution)/shard_map/all_gather | solution.py:294
  329.9 6.9 %convolution_convert_fusion = bf16[192,512]{1,0:T(8,128)(2,1)} fusion(bf16[192,8192]{1,0:T(8,128)(2,1)} %all-gather.7.cloned.1.call-done, bf16[8192,512]{1,0:T(8,128)(2,1)} %param.17), kind=kOutput, calls=%fused_computation.28 | convolution fusion | flops 1610711040 | bytes 11730944 | tf_op jit(solution)/shard_map/dot_general | solution.py:295
  (98 shorter events, 4.5 us)
Async XLA Ops:
  6.5 75.9 %copy-start = (bf16[8192,128]{1,0:T(8,128)(2,1)S(1)}, bf16[8192,128]{1,0:T(8,128)(2,1)}, u32[]{:S(2)}) copy-start(bf16[8192,128]{1,0:T(8,128)(2,1)} %param.16) | copy-start | bytes 6291460
  6.5 55.7 %copy-start.11 = (f32[8192]{0:T(1024)S(1)}, f32[8192]{0:T(1024)}, u32[]{:S(2)}) copy-start(f32[8192]{0:T(1024)} %param.14) | copy-start | bytes 98308
  6.5 52.9 %all-gather.5.cloned.1.call-start = ((), (), s32[]{:S(2)}) async-start(), calls=%async_computation.1 | async-start | bytes 3342336 | tf_op jit(solution)/shard_map/all_gather | solution.py:117
  7.3 142.8 %all-gather.9.cloned.1.call-start = ((), (), s32[]{:S(2)}) async-start(), calls=%async_computation.3 | async-start | bytes 4177920 | tf_op jit(solution)/shard_map/all_gather | solution.py:162
  59.5 2.8 copy-start.7
  62.3 10.0 %copy-start.2 = (bf16[16,64,512]{2,1,0:T(8,128)(2,1)S(1)}, bf16[16,64,512]{2,1,0:T(8,128)(2,1)}, u32[]{:S(2)}) copy-start(bf16[16,64,512]{2,1,0:T(8,128)(2,1)} %param.19) | copy-start | bytes 3145732
  64.8 3.3 collective-permute-start
  68.1 4.0 %collective-permute-start.1 = (bf16[192,64]{0,1:T(8,128)(2,1)S(1)}, bf16[192,64]{0,1:T(8,128)(2,1)S(1)}, u32[]{:S(2)}, u32[]{:S(2)}) collective-permute-start(bf16[192,64]{0,1:T(8,128)(2,1)S(1)} %add.171), channel_id=1, source_target_pairs={{0,2},{1,3},{2,0},{3,1},{4,6},{5,7},{6,4},{7,5},{8,10},{9,11},{10,... | collective-permute-start | bytes 73736 | tf_op jit(solution)/shard_map/ppermute | solution.py:97
  72.1 8.3 %collective-permute-start.2 = (bf16[192,64]{0,1:T(8,128)(2,1)S(1)}, bf16[192,64]{0,1:T(8,128)(2,1)S(1)}, u32[]{:S(2)}, u32[]{:S(2)}) collective-permute-start(bf16[192,64]{0,1:T(8,128)(2,1)S(1)} %add.172), channel_id=1, source_target_pairs={{0,4},{1,5},{2,6},{3,7},{4,0},{5,1},{6,2},{7,3},{8,12},{9,13},{10,... | collective-permute-start | bytes 73736 | tf_op jit(solution)/shard_map/ppermute | solution.py:97
  80.5 5.0 %collective-permute-start.3 = (bf16[192,64]{0,1:T(8,128)(2,1)S(1)}, bf16[192,64]{0,1:T(8,128)(2,1)S(1)}, u32[]{:S(2)}, u32[]{:S(2)}) collective-permute-start(bf16[192,64]{0,1:T(8,128)(2,1)S(1)} %add.173), channel_id=1, source_target_pairs={{0,8},{1,9},{2,10},{3,11},{4,12},{5,13},{6,14},{7,15},{8,0},{9,1},... | collective-permute-start | bytes 73736 | tf_op jit(solution)/shard_map/ppermute | solution.py:97
  85.6 6.5 %copy-start.8 = (bf16[192,8192]{1,0:T(8,128)(2,1)S(1)}, bf16[192,8192]{1,0:T(8,128)(2,1)}, u32[]{:S(2)}) copy-start(bf16[192,8192]{1,0:T(8,128)(2,1)} %all-gather.5.cloned.1.call-done) | copy-start | bytes 9437188
  100.6 12.3 %copy-start.9 = (s32[64,4]{0,1:T(4,128)S(1)}, s32[64,4]{0,1:T(4,128)}, u32[]{:S(2)}) copy-start(s32[64,4]{0,1:T(4,128)} %param.24) | copy-start | bytes 3076
  100.7 12.5 %copy-start.10 = (s32[64]{0:T(128)S(1)}, s32[64]{0:T(128)}, u32[]{:S(2)}) copy-start(s32[64]{0:T(128)} %param.23) | copy-start | bytes 772
  155.3 6.3 %copy-start.6 = (bf16[192,16,128]{2,1,0:T(8,128)(2,1)}, bf16[192,16,128]{2,1,0:T(8,128)(2,1)S(1)}, u32[]{:S(2)}) copy-start(bf16[192,16,128]{2,1,0:T(8,128)(2,1)S(1)} %slice.50) | copy-start | bytes 2359300
  168.5 9.5 %copy-start.3 = (f32[64,3,8,8]{3,2,1,0:T(8,128)}, f32[64,3,8,8]{3,2,1,0:T(8,128)S(1)}, u32[]{:S(2)}) copy-start(f32[64,3,8,8]{3,2,1,0:T(8,128)S(1)} %get-tuple-element.6) | copy-start | bytes 147460
  168.5 9.5 %copy-start.4 = (f32[64,3,8,8]{3,2,1,0:T(8,128)}, f32[64,3,8,8]{3,2,1,0:T(8,128)S(1)}, u32[]{:S(2)}) copy-start(f32[64,3,8,8]{3,2,1,0:T(8,128)S(1)} %get-tuple-element.5) | copy-start | bytes 147460
  178.0 32.9 %copy-start.5 = (f32[16,8,24,128]{3,2,1,0:T(8,128)S(1)}, f32[16,8,24,128]{3,2,1,0:T(8,128)}, u32[]{:S(2)}) copy-start(f32[16,8,24,128]{3,2,1,0:T(8,128)} %get-tuple-element.20) | copy-start | bytes 4718596
  178.6 1.6 collective-permute-start.4
  180.3 8.5 %collective-permute-start.5 = (f32[64,8,24]{2,1,0:T(8,128)S(1)}, f32[64,8,24]{2,1,0:T(8,128)S(1)}, u32[]{:S(2)}, u32[]{:S(2)}) collective-permute-start(f32[64,8,24]{2,1,0:T(8,128)S(1)} %max.16), channel_id=1, source_target_pairs={{0,2},{1,3},{2,0},{3,1},{4,6},{5,7},{6,4},{7,5},{8,10},{9,11},{10,... | collective-permute-start | bytes 147464 | tf_op jit(solution)/shard_map/ppermute | solution.py:97
  188.8 7.9 %collective-permute-start.6 = (f32[64,8,24]{2,1,0:T(8,128)S(1)}, f32[64,8,24]{2,1,0:T(8,128)S(1)}, u32[]{:S(2)}, u32[]{:S(2)}) collective-permute-start(f32[64,8,24]{2,1,0:T(8,128)S(1)} %max.17), channel_id=1, source_target_pairs={{0,4},{1,5},{2,6},{3,7},{4,0},{5,1},{6,2},{7,3},{8,12},{9,13},{10,... | collective-permute-start | bytes 147464 | tf_op jit(solution)/shard_map/ppermute | solution.py:97
  196.7 13.5 %collective-permute-start.7 = (f32[64,8,24]{2,1,0:T(8,128)S(1)}, f32[64,8,24]{2,1,0:T(8,128)S(1)}, u32[]{:S(2)}, u32[]{:S(2)}) collective-permute-start(f32[64,8,24]{2,1,0:T(8,128)S(1)} %max.18), channel_id=1, source_target_pairs={{0,8},{1,9},{2,10},{3,11},{4,12},{5,13},{6,14},{7,15},{8,0},{9,1},... | collective-permute-start | bytes 147464 | tf_op jit(solution)/shard_map/ppermute | solution.py:97
  222.6 42.5 %all-to-all-start = ((f32[16,16,3,516]{3,1,2,0:T(8,128)}), f32[16,16,3,516]{3,1,2,0:T(8,128)S(1)}, u32[]{:S(2)}, u32[]{:S(2)}) async-start(f32[16,16,3,516]{3,1,2,0:T(8,128)} %copy.209), calls=%async_computation | async-start | bytes 3932160 | tf_op jit(solution)/shard_map/all_to_all | solution.py:252
  226.3 103.6 %all-gather.7.cloned.1.call-start = ((), (), s32[]{:S(2)}) async-start(), calls=%async_computation.2 | async-start | bytes 3342336 | tf_op jit(solution)/shard_map/all_gather | solution.py:294
  329.9 6.9 %copy-start.1 = (bf16[8192,128]{1,0:T(8,128)(2,1)S(1)}, bf16[8192,128]{1,0:T(8,128)(2,1)}, u32[]{:S(2)}) copy-start(bf16[8192,128]{1,0:T(8,128)(2,1)} %param.16) | copy-start | bytes 6291460
Sparse Core Ops, SparseCore 0:
  9.5 49.8 all-gather.4
  100.8 49.2 all-gather.8
  276.7 53.1 all-gather.6

commit v4 on v3

--- a/solution.py
+++ b/solution.py
@@ -93,9 +93,11 @@
     size = lax.axis_size("blk")
     step = 1
     while step < size:
-        pairs = [(i, i ^ step) for i in range(size)]
-        value = combine(value, lax.ppermute(value, "blk", pairs))
-        step *= 2
+        masks = [step] if step * 2 >= size else [step, step * 2, step * 3]
+        arrived = [lax.ppermute(value, "blk", [(i, i ^ m) for i in range(size)]) for m in masks]
+        for other in arrived:
+            value = combine(value, other)
+        step *= 2 ** len(masks[:2])
     return value
 
 
@@ -131,9 +133,15 @@
     )
     partial_codes = jnp.sum(jnp.where(local_pick[:, :, None], output_projected, 0.0), axis=1)
     adapter_choice_index = butterfly(partial_codes.astype(jnp.bfloat16), jnp.add)
-    up_weight_rows = adapter_up_weight[token_cache_slot]
-    adapter_query_update = jnp.einsum(
-        "gk,gkq->gq", adapter_choice_index, up_weight_rows, preferred_element_type=jnp.float32
+    slot_count, adapter_rank, _ = adapter_up_weight.shape
+    slot_pick = token_cache_slot[:, None] == jnp.arange(slot_count, dtype=jnp.int32)[None, :]
+    spread_codes = jnp.where(
+        slot_pick[:, :, None], adapter_choice_index[:, None, :], jnp.zeros((), jnp.bfloat16)
+    ).reshape(token_cache_slot.shape[0], slot_count * adapter_rank)
+    adapter_query_update = jnp.dot(
+        spread_codes,
+        adapter_up_weight.reshape(slot_count * adapter_rank, -1),
+        preferred_element_type=jnp.float32,
     )
     token_positions = positions_of(cached_lengths)
     query_cols = query_weight.shape[1]

time: 345 us -> 333 us (0.965)
  matrix products: 36 us -> 26.6 us
  local copies, waits for them, and re-layouts: 59.6 us -> 50.8 us
  starting transfers between devices: 12.5 us -> 16.6 us
    gather x1 -> x0, local copies, waits for them, and re-layouts: 8.12 us -> none  [local(): up_weight_rows = adapter_up_weight[token_cache_slot]]
    ppermute x8 -> x12, waiting for transfers between devices: 29.2 us -> 35.6 us  [butterfly(): lax.ppermute(value, 'blk', [(i, i ^ m) for i in range(size)])]
    dot_general x1, matrix products: 6.45 us -> 0.4 us  [local(): jnp.dot(spread_codes, adapter_up_weight.reshape(slot_count * adapter_rank...]
    ppermute x8 -> x12, starting transfers between devices: 8.72 us -> 12.8 us  [butterfly(): lax.ppermute(value, 'blk', [(i, i ^ m) for i in range(size)])]
  transfers between devices with their start and end apart: 12 -> 16, of which waited for: 9 -> 10; matrix products, arithmetic and copies ran while one was open for 11% -> 10% of each run, Pallas kernels for 0% -> 0%
where the time goes in v4:
time: 333 us; the launch traced here: 332 us
  waiting for transfers between devices  202 us (61%)
  local copies, waits for them, and re-layouts  50.8 us (15%)
  matrix products  26.6 us (8%)
  other arithmetic  20.4 us (6%)
  starting transfers between devices  16.6 us (5%)
  between operations  13.7 us (4%)
    all_gather x1, waiting for transfers between devices, local(): attended = lax.all_gather(attended_own, 'blk', axis=1, tiled=True)  53.3 us
    all_gather x1, waiting for transfers between devices, local(): gathered = lax.all_gather(layer_input_tokens, 'blk', axis=1, tiled=True)  46.8 us
    all_gather x1, waiting for transfers between devices, local(): joined = lax.all_gather(rotated_parts, 'blk', axis=1, tiled=False)  35.8 us
    ppermute x12, waiting for transfers between devices, butterfly(): lax.ppermute(value, 'blk', [(i, i ^ m) for i in range(size)])  35.6 us
    all_to_all x1, waiting for transfers between devices, local(): received = lax.all_to_all(packed, 'blk', 0, 0, tiled=True)  29.6 us
    unnamed x27, local copies, waits for them, and re-layouts  15.4 us
    ppermute x12, starting transfers between devices, butterfly(): lax.ppermute(value, 'blk', [(i, i ^ m) for i in range(size)])  12.8 us
    dot_general x1, matrix products, local(): jnp.dot(attended, output_weight, preferred_element_type=jnp.float32)  6.94 us
  transfers between devices with their start and end apart: 16, of which 10 were waited for; matrix products, arithmetic and copies ran while one was open for 10% of the time, Pallas kernels for 0%

profile of v4, /device:TPU:0, one launch (start us, length us, event | category | flops | bytes accessed | tf_op | source)
XLA Modules:
  0.0 332.4 jit_solution(7717899167018925434)
XLA Ops:
  6.5 0.7 all-gather.5.cloned.1.call-update
  7.3 0.8 select_reduce_fusion.2
  8.3 0.7 add_convert_fusion
  9.2 0.7 fusion.49
  9.9 2.8 fusion.23
  12.7 46.8 %all-gather.5.cloned.1.call-done = bf16[192,8192]{1,0:T(8,128)(2,1)} async-done(((bf16[192,512]{1,0:T(8,128)(2,1)}), bf16[192,8192]{1,0:T(8,128)(2,1)}) %all-gather.5.cloned.1.call-update) | async-done | bytes 3145744 | tf_op jit(solution)/shard_map/all_gather | solution.py:119
  59.5 2.8 fusion
  62.3 1.2 fusion.12
  63.5 1.2 collective-permute-start.2
  64.7 0.7 collective-permute-start.1
  65.5 5.2 %fusion.59 = f32[192,512]{1,0:T(8,128)S(1)} fusion(bf16[8192,512]{1,0:T(8,128)(2,1)} %param.15, bf16[192,8192]{1,0:T(8,128)(2,1)S(1)} %copy-done.6, f32[8192]{0:T(1024)S(1)} %copy-done.11, f32[192]{0:T(256)S(1)} %add_rsqrt_fusion), kind=kOutput, calls=%fused_computation.128 | convolution fusion | flops 1616904192 | bytes 11961088 | tf_op jit(solution)/shard_map/dot_general | solution.py:151
  70.8 1.5 collective-permute-start.5
  72.4 2.8 collective-permute-start.3
  75.2 1.1 fusion.56
  76.4 0.5 collective-permute-done.5
  76.9 1.0 collective-permute-done.4
  77.9 0.4 fusion.11
  78.3 0.8 pad_maximum_fusion.values_ref
  79.1 2.4 shard_map.127
  81.6 12.3 %copy.192 = bf16[16,128,2048]{1,2,0:T(8,128)(2,1)} copy(bf16[16,128,2048]{2,1,0:T(8,128)(2,1)} %param.20) | data formatting | bytes 16777216 | tf_op args[7]
  94.5 35.8 %all-gather.9.cloned.1.call-done = bf16[192,10240]{1,0:T(8,128)(2,1)} async-done(((bf16[192,640]{1,0:T(8,128)(2,1)}), bf16[192,10240]{1,0:T(8,128)(2,1)}) %all-gather.9.cloned.1.call-update) | async-done | bytes 3932176 | tf_op jit(solution)/shard_map/all_gather | solution.py:170
  130.3 2.9 copy.240
  133.4 2.2 slice.46
  135.6 6.0 %reshape_reshape.15 = bf16[64,3,8,8,128]{4,3,2,1,0:T(8,128)(2,1)} reshape(bf16[192,16,512]{2,1,0:T(8,128)(2,1)} %slice.46) | data formatting | bytes 6291456 | tf_op jit(solution)/shard_map/reshape;reshape | solution.py:176
  141.7 3.4 %gather_fusion = bf16[16,3,8,8,128]{4,3,2,1,0:T(8,128)(2,1)} fusion(bf16[64,3,8,8,128]{4,3,2,1,0:T(8,128)(2,1)} %reshape_reshape.15, s32[1024]{0:T(1024)S(1)} %pad_clamp_fusion.1), kind=kCustom, calls=%fused_computation | custom fusion | bytes 1572928 | tf_op jit(solution)/shard_map/gather | solution.py:202
  145.1 6.8 %fusion.3 = (f32[64,3,8,8]{3,2,1,0:T(8,128)S(1)}, f32[64,3,8,8]{3,2,1,0:T(8,128)S(1)}, f32[64,3,8,8]{3,2,1,0:T(8,128)S(1)}) fusion(bf16[64,3,8,8,128]{4,3,2,1,0:T(8,128)(2,1)} %reshape_reshape.15, f32[64,8,128]{2,1,0:T(8,128)S(1)} %get-tuple-element.16, f32[64,8,128]{2,1,0:T(8,128)S(1)} %get-tuple-element.15, f32[64,8,128]{2,1,0:T(8,128)S(1)} %get-tuple-element.14), kind=kLoop, calls=%fused_computation.11 | loop fusion | flops 10973184 | bytes 4079616 | tf_op jit(solution)/shard_map/reduce_sum | solution.py:225
  151.9 0.3 copy.197
  152.2 0.3 copy.196
  152.4 0.3 copy.195
  153.0 4.9 %fusion.63 = (f32[16,8,24]{2,1,0:T(8,128)S(1)}, f32[16,8,24,128]{3,2,1,0:T(8,128)}) fusion(bf16[16,128,2,8,128]{1,4,3,2,0:T(8,128)(2,1)} %bitcast.115, pred[16,128]{1,0:T(8,128)(4,1)S(1)} %fusion.43, bf16[16,3,8,8,128]{4,3,2,1,0:T(8,128)(2,1)} %gather_fusion), kind=kOutput, calls=%fused_computation.130 | convolution fusion | flops 101839872 | bytes 6567936 | tf_op jit(solution)/shard_map/skqd,spkd->skqp/dot_general | solution.py:207
  157.9 0.5 select_reduce_fusion
  158.6 0.5 collective-permute-start.8
  159.0 1.5 collective-permute-start.7
  160.5 6.4 %collective-permute-done.8 = f32[64,8,24]{2,1,0:T(8,128)S(1)} collective-permute-done((f32[64,8,24]{2,1,0:T(8,128)S(1)}, f32[64,8,24]{2,1,0:T(8,128)S(1)}, u32[]{:S(2)}, u32[]{:S(2)}) %collective-permute-start.8) | collective-permute-done | bytes 49184 | tf_op jit(solution)/shard_map/ppermute | solution.py:97
  166.9 6.0 %collective-permute-done.7 = f32[64,8,24]{2,1,0:T(8,128)S(1)} collective-permute-done((f32[64,8,24]{2,1,0:T(8,128)S(1)}, f32[64,8,24]{2,1,0:T(8,128)S(1)}, u32[]{:S(2)}, u32[]{:S(2)}) %collective-permute-start.7) | collective-permute-done | bytes 49184 | tf_op jit(solution)/shard_map/ppermute | solution.py:97
  172.9 2.2 collective-permute-start.11
  175.1 1.2 collective-permute-start.10
  176.4 1.0 collective-permute-start.9
  177.4 6.7 %collective-permute-done.11 = f32[64,8,24]{2,1,0:T(8,128)S(1)} collective-permute-done((f32[64,8,24]{2,1,0:T(8,128)S(1)}, f32[64,8,24]{2,1,0:T(8,128)S(1)}, u32[]{:S(2)}, u32[]{:S(2)}) %collective-permute-start.11) | collective-permute-done | bytes 49184 | tf_op jit(solution)/shard_map/ppermute | solution.py:97
  184.1 15.1 %collective-permute-done.10 = f32[64,8,24]{2,1,0:T(8,128)S(1)} collective-permute-done((f32[64,8,24]{2,1,0:T(8,128)S(1)}, f32[64,8,24]{2,1,0:T(8,128)S(1)}, u32[]{:S(2)}, u32[]{:S(2)}) %collective-permute-start.10) | collective-permute-done | bytes 49184 | tf_op jit(solution)/shard_map/ppermute | solution.py:97
  199.2 0.6 gather_fusion.1
  199.8 4.5 %fusion.8 = f32[16,8,3,8,128]{4,3,2,1,0:T(8,128)S(1)} fusion(bf16[16,128,2,8,128]{1,4,3,2,0:T(8,128)(2,1)} %bitcast.116, f32[16,8,24,128]{3,2,1,0:T(8,128)S(1)} %copy-done.4, f32[16,8,24]{2,1,0:T(8,128)S(1)} %gather_fusion.1, pred[16,128]{1,0:T(8,128)(4,1)S(1)} %fusion.43), kind=kOutput, calls=%fused_computation.23 | convolution fusion | flops 101842944 | bytes 7354368 | tf_op jit(solution)/shard_map/skqp,spkd->skqd/dot_general | solution.py:239
  204.3 0.9 fusion.9
  205.5 1.4 reshape_reshape.17
  207.1 0.7 gather_fusion.2
  207.7 0.4 copy.208
  208.1 1.6 maximum_bitcast_fusion
  209.7 1.9 copy.209
  211.6 3.7 %all-to-all-start = ((f32[16,16,3,516]{3,1,2,0:T(8,128)}), f32[16,16,3,516]{3,1,2,0:T(8,128)S(1)}, u32[]{:S(2)}, u32[]{:S(2)}) async-start(f32[16,16,3,516]{3,1,2,0:T(8,128)} %copy.209), calls=%async_computation | async-start | bytes 3932160 | tf_op jit(solution)/shard_map/all_to_all | solution.py:260
  215.7 1.4 copy.213
  217.1 1.4 copy.214
  218.5 0.3 copy.215
  218.8 3.4 %reshape_reshape.19 = bf16[64,3,2048]{2,1,0:T(4,128)(2,1)} reshape(bf16[192,16,128]{2,1,0:T(8,128)(2,1)} %copy-done.5) | data formatting | bytes 1572864 | tf_op jit(solution)/shard_map/reshape;reshape | solution.py:287
  223.1 1.4 fusion.36
  224.5 29.6 %all-to-all-done = f32[16,16,3,516]{3,1,2,0:T(8,128)S(1)} async-done(((f32[16,16,3,516]{3,1,2,0:T(8,128)}), f32[16,16,3,516]{3,1,2,0:T(8,128)S(1)}, u32[]{:S(2)}, u32[]{:S(2)}) %all-to-all-start) | async-done | bytes 1585184 | tf_op jit(solution)/shard_map/all_to_all | solution.py:260
  254.1 2.5 copy.210
  256.6 3.1 reshape.297
  259.7 1.6 copy.211
  261.3 1.4 dot_general.38
  262.7 1.0 fusion.40
  264.0 0.3 copy.212
  264.8 0.8 fusion.24
  265.6 53.3 %all-gather.7.cloned.1.call-done = bf16[192,8192]{1,0:T(8,128)(2,1)} async-done(((bf16[192,512]{1,0:T(8,128)(2,1)}), bf16[192,8192]{1,0:T(8,128)(2,1)}) %all-gather.7.cloned.1.call-update) | async-done | bytes 3145744 | tf_op jit(solution)/shard_map/all_gather | solution.py:302
  318.9 6.9 %convolution_convert_fusion = bf16[192,512]{1,0:T(8,128)(2,1)} fusion(bf16[192,8192]{1,0:T(8,128)(2,1)} %all-gather.7.cloned.1.call-done, bf16[8192,512]{1,0:T(8,128)(2,1)} %param.17), kind=kOutput, calls=%fused_computation.28 | convolution fusion | flops 1610711040 | bytes 11730944 | tf_op jit(solution)/shard_map/dot_general | solution.py:303
  (97 shorter events, 4.6 us)
Async XLA Ops:
  6.5 68.7 %copy-start = (bf16[8192,128]{1,0:T(8,128)(2,1)S(1)}, bf16[8192,128]{1,0:T(8,128)(2,1)}, u32[]{:S(2)}) copy-start(bf16[8192,128]{1,0:T(8,128)(2,1)} %param.16) | copy-start | bytes 6291460
  6.5 55.7 %copy-start.11 = (f32[8192]{0:T(1024)S(1)}, f32[8192]{0:T(1024)}, u32[]{:S(2)}) copy-start(f32[8192]{0:T(1024)} %param.14) | copy-start | bytes 98308
  6.5 55.7 %copy-start.9 = (bf16[1,64,8192]{2,1,0:T(8,128)(2,1)S(1)}, bf16[1,64,8192]{2,1,0:T(8,128)(2,1)}, u32[]{:S(2)}) copy-start(bf16[1,64,8192]{2,1,0:T(8,128)(2,1)} %param.18) | copy-start | bytes 3145732
  6.5 53.0 %all-gather.5.cloned.1.call-start = ((), (), s32[]{:S(2)}) async-start(), calls=%async_computation.1 | async-start | bytes 3342336 | tf_op jit(solution)/shard_map/all_gather | solution.py:119
  7.3 123.1 %all-gather.9.cloned.1.call-start = ((), (), s32[]{:S(2)}) async-start(), calls=%async_computation.3 | async-start | bytes 4177920 | tf_op jit(solution)/shard_map/all_gather | solution.py:170
  59.5 2.8 copy-start.6
  63.5 7.2 %collective-permute-start.2 = (bf16[192,64]{0,1:T(8,128)(2,1)S(1)}, bf16[192,64]{0,1:T(8,128)(2,1)S(1)}, u32[]{:S(2)}, u32[]{:S(2)}) collective-permute-start(bf16[192,64]{0,1:T(8,128)(2,1)S(1)} %fusion.12), channel_id=1, source_target_pairs={{0,3},{1,2},{2,1},{3,0},{4,7},{5,6},{6,5},{7,4},{8,11},{9,10},{10,... | collective-permute-start | bytes 73736 | tf_op jit(solution)/shard_map/ppermute | solution.py:97
  64.7 6.0 %collective-permute-start.1 = (bf16[192,64]{0,1:T(8,128)(2,1)S(1)}, bf16[192,64]{0,1:T(8,128)(2,1)S(1)}, u32[]{:S(2)}, u32[]{:S(2)}) collective-permute-start(bf16[192,64]{0,1:T(8,128)(2,1)S(1)} %fusion.12), channel_id=1, source_target_pairs={{0,2},{1,3},{2,0},{3,1},{4,6},{5,7},{6,4},{7,5},{8,10},{9,11},{10,... | collective-permute-start | bytes 73736 | tf_op jit(solution)/shard_map/ppermute | solution.py:97
  65.5 5.3 %collective-permute-start = (bf16[192,64]{0,1:T(8,128)(2,1)S(1)}, bf16[192,64]{0,1:T(8,128)(2,1)S(1)}, u32[]{:S(2)}, u32[]{:S(2)}) collective-permute-start(bf16[192,64]{0,1:T(8,128)(2,1)S(1)} %fusion.12), channel_id=1, source_target_pairs={{0,1},{1,0},{2,3},{3,2},{4,5},{5,4},{6,7},{7,6},{8,9},{9,8},{10,11... | collective-permute-start | bytes 73736 | tf_op jit(solution)/shard_map/ppermute | solution.py:97
  70.8 7.1 %copy-start.10 = (bf16[16,64,512]{2,1,0:T(8,128)(2,1)S(1)}, bf16[16,64,512]{2,1,0:T(8,128)(2,1)}, u32[]{:S(2)}) copy-start(bf16[16,64,512]{2,1,0:T(8,128)(2,1)} %param.19) | copy-start | bytes 3145732
  70.8 6.1 %collective-permute-start.5 = (bf16[192,64]{0,1:T(8,128)(2,1)S(1)}, bf16[192,64]{0,1:T(8,128)(2,1)S(1)}, u32[]{:S(2)}, u32[]{:S(2)}) collective-permute-start(bf16[192,64]{0,1:T(8,128)(2,1)S(1)} %add_add_fusion.1), channel_id=1, source_target_pairs={{0,12},{1,13},{2,14},{3,15},{4,8},{5,9},{6,10},{7,11},{8,4},{9,5},... | collective-permute-start | bytes 73736 | tf_op jit(solution)/shard_map/ppermute | solution.py:97
  72.3 5.6 %collective-permute-start.4 = (bf16[192,64]{0,1:T(8,128)(2,1)S(1)}, bf16[192,64]{0,1:T(8,128)(2,1)S(1)}, u32[]{:S(2)}, u32[]{:S(2)}) collective-permute-start(bf16[192,64]{0,1:T(8,128)(2,1)S(1)} %add_add_fusion.1), channel_id=1, source_target_pairs={{0,8},{1,9},{2,10},{3,11},{4,12},{5,13},{6,14},{7,15},{8,0},{9,1},... | collective-permute-start | bytes 73736 | tf_op jit(solution)/shard_map/ppermute | solution.py:97
  72.4 5.4 %collective-permute-start.3 = (bf16[192,64]{0,1:T(8,128)(2,1)S(1)}, bf16[192,64]{0,1:T(8,128)(2,1)S(1)}, u32[]{:S(2)}, u32[]{:S(2)}) collective-permute-start(bf16[192,64]{0,1:T(8,128)(2,1)S(1)} %add_add_fusion.1), channel_id=1, source_target_pairs={{0,4},{1,5},{2,6},{3,7},{4,0},{5,1},{6,2},{7,3},{8,12},{9,13},{10,... | collective-permute-start | bytes 73736 | tf_op jit(solution)/shard_map/ppermute | solution.py:97
  81.6 12.3 %copy-start.7 = (s32[64,4]{0,1:T(4,128)S(1)}, s32[64,4]{0,1:T(4,128)}, u32[]{:S(2)}) copy-start(s32[64,4]{0,1:T(4,128)} %param.24) | copy-start | bytes 3076
  81.6 12.5 %copy-start.8 = (s32[64]{0:T(128)S(1)}, s32[64]{0:T(128)}, u32[]{:S(2)}) copy-start(s32[64]{0:T(128)} %param.23) | copy-start | bytes 772
  133.4 8.2 %copy-start.5 = (bf16[192,16,128]{2,1,0:T(8,128)(2,1)}, bf16[192,16,128]{2,1,0:T(8,128)(2,1)S(1)}, u32[]{:S(2)}) copy-start(bf16[192,16,128]{2,1,0:T(8,128)(2,1)S(1)} %slice.48) | copy-start | bytes 2359300
  151.9 6.0 %copy-start.2 = (f32[64,3,8,8]{3,2,1,0:T(8,128)}, f32[64,3,8,8]{3,2,1,0:T(8,128)S(1)}, u32[]{:S(2)}) copy-start(f32[64,3,8,8]{3,2,1,0:T(8,128)S(1)} %get-tuple-element.6) | copy-start | bytes 147460
  151.9 6.0 %copy-start.3 = (f32[64,3,8,8]{3,2,1,0:T(8,128)}, f32[64,3,8,8]{3,2,1,0:T(8,128)S(1)}, u32[]{:S(2)}) copy-start(f32[64,3,8,8]{3,2,1,0:T(8,128)S(1)} %get-tuple-element.5) | copy-start | bytes 147460
  157.9 41.9 %copy-start.4 = (f32[16,8,24,128]{3,2,1,0:T(8,128)S(1)}, f32[16,8,24,128]{3,2,1,0:T(8,128)}, u32[]{:S(2)}) copy-start(f32[16,8,24,128]{3,2,1,0:T(8,128)} %get-tuple-element.20) | copy-start | bytes 4718596
  158.6 8.3 %collective-permute-start.8 = (f32[64,8,24]{2,1,0:T(8,128)S(1)}, f32[64,8,24]{2,1,0:T(8,128)S(1)}, u32[]{:S(2)}, u32[]{:S(2)}) collective-permute-start(f32[64,8,24]{2,1,0:T(8,128)S(1)} %max.21), channel_id=1, source_target_pairs={{0,3},{1,2},{2,1},{3,0},{4,7},{5,6},{6,5},{7,4},{8,11},{9,10},{10,... | collective-permute-start | bytes 147464 | tf_op jit(solution)/shard_map/ppermute | solution.py:97
  159.0 13.8 %collective-permute-start.7 = (f32[64,8,24]{2,1,0:T(8,128)S(1)}, f32[64,8,24]{2,1,0:T(8,128)S(1)}, u32[]{:S(2)}, u32[]{:S(2)}) collective-permute-start(f32[64,8,24]{2,1,0:T(8,128)S(1)} %max.21), channel_id=1, source_target_pairs={{0,2},{1,3},{2,0},{3,1},{4,6},{5,7},{6,4},{7,5},{8,10},{9,11},{10,... | collective-permute-start | bytes 147464 | tf_op jit(solution)/shard_map/ppermute | solution.py:97
  160.5 12.3 %collective-permute-start.6 = (f32[64,8,24]{2,1,0:T(8,128)S(1)}, f32[64,8,24]{2,1,0:T(8,128)S(1)}, u32[]{:S(2)}, u32[]{:S(2)}) collective-permute-start(f32[64,8,24]{2,1,0:T(8,128)S(1)} %max.21), channel_id=1, source_target_pairs={{0,1},{1,0},{2,3},{3,2},{4,5},{5,4},{6,7},{7,6},{8,9},{9,8},{10,11... | collective-permute-start | bytes 147464 | tf_op jit(solution)/shard_map/ppermute | solution.py:97
  172.9 11.2 %collective-permute-start.11 = (f32[64,8,24]{2,1,0:T(8,128)S(1)}, f32[64,8,24]{2,1,0:T(8,128)S(1)}, u32[]{:S(2)}, u32[]{:S(2)}) collective-permute-start(f32[64,8,24]{2,1,0:T(8,128)S(1)} %maximum_maximum_fusion.1), channel_id=1, source_target_pairs={{0,12},{1,13},{2,14},{3,15},{4,8},{5,9},{6,10},{7,11},{8,4},{9,5},... | collective-permute-start | bytes 147464 | tf_op jit(solution)/shard_map/ppermute | solution.py:97
  175.1 24.0 %collective-permute-start.10 = (f32[64,8,24]{2,1,0:T(8,128)S(1)}, f32[64,8,24]{2,1,0:T(8,128)S(1)}, u32[]{:S(2)}, u32[]{:S(2)}) collective-permute-start(f32[64,8,24]{2,1,0:T(8,128)S(1)} %maximum_maximum_fusion.1), channel_id=1, source_target_pairs={{0,8},{1,9},{2,10},{3,11},{4,12},{5,13},{6,14},{7,15},{8,0},{9,1},... | collective-permute-start | bytes 147464 | tf_op jit(solution)/shard_map/ppermute | solution.py:97
  176.4 22.8 %collective-permute-start.9 = (f32[64,8,24]{2,1,0:T(8,128)S(1)}, f32[64,8,24]{2,1,0:T(8,128)S(1)}, u32[]{:S(2)}, u32[]{:S(2)}) collective-permute-start(f32[64,8,24]{2,1,0:T(8,128)S(1)} %maximum_maximum_fusion.1), channel_id=1, source_target_pairs={{0,4},{1,5},{2,6},{3,7},{4,0},{5,1},{6,2},{7,3},{8,12},{9,13},{10,... | collective-permute-start | bytes 147464 | tf_op jit(solution)/shard_map/ppermute | solution.py:97
  211.6 42.5 %all-to-all-start = ((f32[16,16,3,516]{3,1,2,0:T(8,128)}), f32[16,16,3,516]{3,1,2,0:T(8,128)S(1)}, u32[]{:S(2)}, u32[]{:S(2)}) async-start(f32[16,16,3,516]{3,1,2,0:T(8,128)} %copy.209), calls=%async_computation | async-start | bytes 3932160 | tf_op jit(solution)/shard_map/all_to_all | solution.py:260
  215.3 103.6 %all-gather.7.cloned.1.call-start = ((), (), s32[]{:S(2)}) async-start(), calls=%async_computation.2 | async-start | bytes 3342336 | tf_op jit(solution)/shard_map/all_gather | solution.py:302
  318.9 6.9 %copy-start.1 = (bf16[8192,128]{1,0:T(8,128)(2,1)S(1)}, bf16[8192,128]{1,0:T(8,128)(2,1)}, u32[]{:S(2)}) copy-start(bf16[8192,128]{1,0:T(8,128)(2,1)} %param.16) | copy-start | bytes 6291460
Sparse Core Ops, SparseCore 0:
  9.5 49.9 all-gather.4
  81.7 48.6 all-gather.8
  265.7 53.1 all-gather.6

commit v5 on v4

--- a/solution.py
+++ b/solution.py
@@ -214,28 +214,7 @@
     )
     masked = jnp.where(valid_full, scores, neg_large)
     page_peak = jnp.max(masked, axis=-1)
-    req_peak = jnp.max(
-        jnp.where(page_owner[:, :, None, None], page_peak[:, None], neg_large), axis=0
-    )
-    query_wide = query_split.astype(jnp.float32)
-    fresh_keys = fresh_token_rows[:, :, 0].astype(jnp.float32)
-    fresh_scores = (
-        jnp.stack(
-            [
-                jnp.sum(query_wide * fresh_keys[:, j][:, None, :, None, :], axis=-1)
-                for j in range(NEW_TOKENS)
-            ],
-            axis=-1,
-        )
-        .transpose(0, 2, 1, 3, 4)
-        .reshape(request_count, KEY_VALUE_HEADS, query_feature_width, NEW_TOKENS)
-        * score_scale
-    )
-    step_of = jnp.arange(query_feature_width, dtype=jnp.int32) // query_group_width
-    fresh_ok = (jnp.arange(NEW_TOKENS, dtype=jnp.int32)[None, :] <= step_of[:, None])[None, None]
-    fresh_masked = jnp.where(fresh_ok, fresh_scores, neg_large)
-    top_score = butterfly(jnp.maximum(req_peak, jnp.max(fresh_masked, axis=-1)), jnp.maximum)
-    weights = jnp.where(valid_full, jnp.exp(masked - top_score[page_req][..., None]), 0.0)
+    weights = jnp.where(valid_full, jnp.exp(masked - page_peak[..., None]), 0.0)
     page_num = jnp.einsum(
         "skqp,spkd->skqd",
         weights.astype(jnp.bfloat16),
@@ -255,37 +234,65 @@
     slot_den = to_tokens(jnp.sum(weights, axis=-1)[..., None]).reshape(
         request_page_count, NEW_TOKENS, head_count
     )
-    slot_den_owner = slot_den[:, :, head_pick]
-    packed = jnp.concatenate([slot_num, slot_den_owner], axis=3).transpose(2, 0, 1, 3)
+    slot_peak = to_tokens(page_peak[..., None]).reshape(request_page_count, NEW_TOKENS, head_count)
+    packed = jnp.concatenate(
+        [
+            part.transpose(2, 0, 1, 3).reshape(device_count, request_page_count, -1)
+            for part in (slot_num, slot_den[:, :, head_pick], slot_peak[:, :, head_pick])
+        ],
+        axis=2,
+    )
     received = lax.all_to_all(packed, "blk", 0, 0, tiled=True)
     group_pages = device_count * request_page_count
-    all_page_ids = jnp.arange(group_pages, dtype=jnp.int32)
-    all_owner = jnp.any(request_page_tables[None, :, :] == all_page_ids[:, None, None], axis=2)
-    pick_req = all_owner.T.astype(jnp.float32)
-    summed = jnp.einsum(
-        "rp,px->rx",
-        pick_req,
-        received.reshape(group_pages, -1),
-        precision=lax.Precision.HIGHEST,
-    ).reshape(request_count, NEW_TOKENS, owner_cols + owner_heads)
-    fresh_weights = jnp.where(fresh_ok, jnp.exp(fresh_masked - top_score[..., None]), 0.0)
-    fresh_by_head = (
-        fresh_weights.reshape(
-            request_count, KEY_VALUE_HEADS, NEW_TOKENS, query_group_width, NEW_TOKENS
-        )
-        .transpose(0, 2, 1, 3, 4)
-        .reshape(request_count, NEW_TOKENS, QUERY_HEADS, NEW_TOKENS)
-    )
+    listed_pages = request_page_tables.reshape(-1)
+    listed_target = jnp.where(listed_pages >= 0, listed_pages, group_pages)
+    page_of_req = (
+        jnp.zeros((group_pages,), jnp.int32)
+        .at[listed_target]
+        .set(jnp.repeat(jnp.arange(request_count, dtype=jnp.int32), table_width), mode="drop")
+    )
+    page_used = jnp.zeros((group_pages,), jnp.bool_).at[listed_target].set(True, mode="drop")
+    owner_of_page = (
+        jnp.arange(request_count, dtype=jnp.int32)[:, None] == page_of_req[None, :]
+    ) & page_used[None, :]
+    arrived = received.reshape(group_pages, -1)
+    num_width = NEW_TOKENS * owner_cols
+    head_width = NEW_TOKENS * owner_heads
+    arrived_num = arrived[:, :num_width]
+    arrived_den = arrived[:, num_width : num_width + head_width]
+    arrived_peak = arrived[:, num_width + head_width :]
     first_head = (own_index * owner_cols) // HEAD_WIDTH
-    weights_own = lax.dynamic_slice_in_dim(fresh_by_head, first_head, owner_heads, axis=2)
+    kv_head = first_head // query_group_width
+    query_own = lax.dynamic_slice_in_dim(
+        query_vectors.reshape(request_count, NEW_TOKENS, QUERY_HEADS, HEAD_WIDTH),
+        first_head,
+        owner_heads,
+        axis=2,
+    )
+    fresh_rows = key_value_rows.reshape(request_count, NEW_TOKENS, -1)
+    keys_own = lax.dynamic_slice_in_dim(fresh_rows, kv_head * HEAD_WIDTH, HEAD_WIDTH, axis=2)
+    fresh_scores = (
+        jnp.einsum("rihd,rjd->rihj", query_own, keys_own, preferred_element_type=jnp.float32)
+        * score_scale
+    )
+    causal = (jnp.arange(NEW_TOKENS)[None, :] <= jnp.arange(NEW_TOKENS)[:, None])[None, :, None, :]
+    fresh_masked = jnp.where(causal, fresh_scores, neg_large)
+    slot_best = jnp.max(
+        jnp.where(owner_of_page[:, None, :], arrived_peak.T[None], neg_large), axis=2
+    )
+    top_flat = jnp.maximum(slot_best, jnp.max(fresh_masked, axis=-1).reshape(request_count, -1))
+    top_score = top_flat.reshape(request_count, NEW_TOKENS, owner_heads)
+    rescale = jnp.exp(arrived_peak - top_flat[page_of_req])
+    rescaled = jnp.concatenate(
+        [arrived_num * jnp.repeat(rescale, head_repeat, axis=1), arrived_den * rescale], axis=1
+    )
+    pick_req = owner_of_page.astype(jnp.float32)
+    summed = jnp.einsum("rp,px->rx", pick_req, rescaled, precision=lax.Precision.HIGHEST)
+    weights_own = jnp.where(causal, jnp.exp(fresh_masked - top_score[..., None]), 0.0)
     value_col = (
-        KEY_VALUE_HEADS * HEAD_WIDTH
-        + (first_head // query_group_width) * HEAD_WIDTH
-        + (own_index * owner_cols) % HEAD_WIDTH
-    )
-    values_own = lax.dynamic_slice_in_dim(
-        key_value_rows.reshape(request_count, NEW_TOKENS, -1), value_col, head_repeat, axis=2
-    )
+        KEY_VALUE_HEADS * HEAD_WIDTH + kv_head * HEAD_WIDTH + (own_index * owner_cols) % HEAD_WIDTH
+    )
+    values_own = lax.dynamic_slice_in_dim(fresh_rows, value_col, head_repeat, axis=2)
     fresh_num_own = jnp.einsum(
         "rihj,rjd->rihd",
         weights_own.astype(jnp.bfloat16),
@@ -293,8 +300,8 @@
         preferred_element_type=jnp.float32,
     ).reshape(request_count * NEW_TOKENS, owner_cols)
     fresh_den_own = jnp.sum(weights_own, axis=-1).reshape(request_count * NEW_TOKENS, owner_heads)
-    num_own = summed[:, :, :owner_cols].reshape(request_count * NEW_TOKENS, owner_cols)
-    den_own = summed[:, :, owner_cols:].reshape(request_count * NEW_TOKENS, owner_heads)
+    num_own = summed[:, :num_width].reshape(request_count * NEW_TOKENS, owner_cols)
+    den_own = summed[:, num_width:].reshape(request_count * NEW_TOKENS, owner_heads)
     totals = den_own + fresh_den_own
     attended_own = ((num_own + fresh_num_own) / jnp.repeat(totals, head_repeat, axis=1)).astype(
         jnp.bfloat16

time: 333 us -> 289 us (0.87)
  waiting for transfers between devices: 202 us -> 156 us
  local copies, waits for them, and re-layouts: 50.8 us -> 60.6 us
  starting transfers between devices: 16.6 us -> 10.9 us
  other arithmetic: 20.4 us -> 14.8 us
    ppermute x12 -> x6, waiting for transfers between devices: 35.6 us -> 1.48 us  [butterfly(): lax.ppermute(value, 'blk', [(i, i ^ m) for i in range(size)])]
    all_to_all x1, waiting for transfers between devices: 29.6 us -> 19.2 us  [local(): received = lax.all_to_all(packed, 'blk', 0, 0, tiled=True)]
    reduce_sum x2 -> x0, other arithmetic: 6.78 us -> none  [the longest x1 6.75 us: local(): jnp.sum(query_wide * fresh_keys[:, j][:, None, :, None, :], axis=-1)]
    ppermute x12 -> x6, starting transfers between devices: 12.8 us -> 6.41 us  [butterfly(): lax.ppermute(value, 'blk', [(i, i ^ m) for i in range(size)])]
    unnamed x27 -> x23, local copies, waits for them, and re-layouts: 15.4 us -> 17.5 us
  transfers between devices with their start and end apart: 16 -> 10, of which waited for: 10 -> 6; matrix products, arithmetic and copies ran while one was open for 10% -> 14% of each run, Pallas kernels for 0% -> 0%
where the time goes in v5:
time: 289 us; the launch traced here: 288 us
  waiting for transfers between devices  156 us (54%)
  local copies, waits for them, and re-layouts  60.6 us (21%)
  matrix products  29.2 us (10%)
  other arithmetic  14.8 us (5%)
  between operations  13.7 us (5%)
  starting transfers between devices  10.9 us (4%)
    all_gather x1, waiting for transfers between devices, local(): attended = lax.all_gather(attended_own, 'blk', axis=1, tiled=True)  52.2 us
    all_gather x1, waiting for transfers between devices, local(): gathered = lax.all_gather(layer_input_tokens, 'blk', axis=1, tiled=True)  46.8 us
    all_gather x1, waiting for transfers between devices, local(): joined = lax.all_gather(rotated_parts, 'blk', axis=1, tiled=False)  35.8 us
    all_to_all x1, waiting for transfers between devices, local(): received = lax.all_to_all(packed, 'blk', 0, 0, tiled=True)  19.2 us
    unnamed x23, local copies, waits for them, and re-layouts  17.5 us
    dot_general x1, matrix products, local(): jnp.dot(attended, output_weight, preferred_element_type=jnp.float32)  6.94 us
    ppermute x6, starting transfers between devices, butterfly(): lax.ppermute(value, 'blk', [(i, i ^ m) for i in range(size)])  6.41 us
    dot_general x1, matrix products, local(): jnp.einsum('skqp,spkd->skqd', weights.astype(jnp.bfloat16), gathered_cach...  5.8 us
  transfers between devices with their start and end apart: 10, of which 6 were waited for; matrix products, arithmetic and copies ran while one was open for 14% of the time, Pallas kernels for 0%

profile of v5, /device:TPU:0, one launch (start us, length us, event | category | flops | bytes accessed | tf_op | source)
XLA Modules:
  0.0 287.9 jit_solution(4538237480539986838)
XLA Ops:
  6.5 0.7 all-gather.5.cloned.1.call-update
  7.3 0.8 select_reduce_fusion.2
  8.1 0.1 eq.87
  8.3 0.7 add_convert_fusion
  9.2 0.7 fusion.46
  9.9 2.8 fusion.24
  12.7 46.8 %all-gather.5.cloned.1.call-done = bf16[192,8192]{1,0:T(8,128)(2,1)} async-done(((bf16[192,512]{1,0:T(8,128)(2,1)}), bf16[192,8192]{1,0:T(8,128)(2,1)}) %all-gather.5.cloned.1.call-update) | async-done | bytes 3145744 | tf_op jit(solution)/shard_map/all_gather | solution.py:119
  59.5 2.8 fusion
  62.3 1.2 fusion.13
  63.5 1.2 collective-permute-start.2
  64.7 0.7 collective-permute-start.1
  65.5 5.2 %fusion.62 = f32[192,512]{1,0:T(8,128)S(1)} fusion(bf16[8192,512]{1,0:T(8,128)(2,1)} %param.15, bf16[192,8192]{1,0:T(8,128)(2,1)S(1)} %copy-done.2, f32[8192]{0:T(1024)S(1)} %copy-done.8, f32[192]{0:T(256)S(1)} %add_rsqrt_fusion), kind=kOutput, calls=%fused_computation.124 | convolution fusion | flops 1616904192 | bytes 11961088 | tf_op jit(solution)/shard_map/dot_general | solution.py:151
  70.8 1.5 collective-permute-start.5
  72.3 0.1 collective-permute-start.4
  72.4 2.8 collective-permute-start.3
  75.2 1.1 fusion.59
  76.4 0.5 collective-permute-done.5
  76.9 1.0 collective-permute-done.4
  77.9 0.4 fusion.12
  78.3 0.8 pad_maximum_fusion.values_ref
  79.1 2.4 shard_map.127
  81.6 12.3 %copy.131 = bf16[16,128,2048]{1,2,0:T(8,128)(2,1)} copy(bf16[16,128,2048]{2,1,0:T(8,128)(2,1)} %param.20) | data formatting | bytes 16777216 | tf_op args[7]
  93.9 0.2 compare_reduce_fusion.1
  94.2 0.2 fusion.36
  94.5 35.8 %all-gather.9.cloned.1.call-done = bf16[192,10240]{1,0:T(8,128)(2,1)} async-done(((bf16[192,640]{1,0:T(8,128)(2,1)}), bf16[192,10240]{1,0:T(8,128)(2,1)}) %all-gather.9.cloned.1.call-update) | async-done | bytes 3932176 | tf_op jit(solution)/shard_map/all_gather | solution.py:170
  130.3 4.8 %copy.168 = bf16[24,8,16,640]{3,2,1,0:T(8,128)(2,1)} copy(bf16[24,8,16,640]{3,1,2,0:T(8,128)(2,1)} %bitcast.110) | data formatting | bytes 7864320
  135.1 2.2 slice.44
  137.3 3.7 %reshape_reshape.18 = bf16[64,3,8,8,128]{4,3,2,1,0:T(8,128)(2,1)} reshape(bf16[192,16,512]{2,1,0:T(8,128)(2,1)S(1)} %slice.44) | data formatting | bytes 6291456 | tf_op jit(solution)/shard_map/reshape;reshape | solution.py:176
  141.0 3.4 %gather_fusion = bf16[16,3,8,8,128]{4,3,2,1,0:T(8,128)(2,1)} fusion(bf16[64,3,8,8,128]{4,3,2,1,0:T(8,128)(2,1)} %reshape_reshape.18, s32[1024]{0:T(1024)S(1)} %pad_clamp_fusion.2), kind=kCustom, calls=%fused_computation | custom fusion | bytes 1572928 | tf_op jit(solution)/shard_map/gather | solution.py:202
  144.5 3.7 %fusion.64 = (f32[16,8,24]{2,1,0:T(8,128)S(1)}, f32[16,8,24,128]{3,2,1,0:T(8,128)S(1)}) fusion(bf16[16,128,2,8,128]{1,4,3,2,0:T(8,128)(2,1)} %bitcast.105, pred[16,128]{1,0:T(8,128)(4,1)S(1)} %fusion.38, bf16[16,3,8,8,128]{4,3,2,1,0:T(8,128)(2,1)} %gather_fusion), kind=kOutput, calls=%fused_computation.125 | convolution fusion | flops 101839872 | bytes 6567936 | tf_op jit(solution)/shard_map/skqd,spkd->skqp/dot_general | solution.py:207
  148.2 5.8 %fusion.9 = f32[16,8,3,8,128]{4,3,2,1,0:T(8,128)} fusion(bf16[16,128,2,8,128]{1,4,3,2,0:T(8,128)(2,1)} %bitcast.106, f32[16,8,24,128]{3,2,1,0:T(8,128)S(1)} %get-tuple-element.16, f32[16,8,24]{2,1,0:T(8,128)S(1)} %get-tuple-element.15, pred[16,128]{1,0:T(8,128)(4,1)S(1)} %fusion.38), kind=kOutput, calls=%fused_computation.23 | convolution fusion | flops 101842944 | bytes 7354368 | tf_op jit(solution)/shard_map/skqp,spkd->skqd/dot_general | solution.py:218
  154.0 1.6 fusion.10
  155.6 2.8 copy.182
  158.4 2.6 reshape_reshape.19
  161.1 0.7 gather_fusion.2
  161.8 0.2 copy.147
  161.9 0.9 copy.136
  162.9 0.7 gather_fusion.1
  163.6 0.2 copy.146
  163.8 3.8 %copy.135 = f32[16,16,3,512]{3,2,1,0:T(4,128)} copy(f32[16,16,3,512]{3,0,2,1:T(8,128)} %bitcast.107) | data formatting | bytes 3145728 | tf_op jit(solution)/shard_map/transpose | solution.py:240
  167.7 3.9 %reshape.332 = f32[16,16,1536]{2,1,0:T(8,128)} reshape(f32[16,16,3,512]{3,2,1,0:T(4,128)} %copy.135) | data formatting | bytes 3145728 | tf_op jit(solution)/shard_map/reshape | solution.py:240
  171.5 2.4 concatenate.28
  174.0 4.4 %all-to-all-start = ((f32[16,16,1560]{2,1,0:T(8,128)}), f32[16,16,1560]{2,1,0:T(8,128)}, u32[]{:S(2)}, u32[]{:S(2)}) async-start(f32[16,16,1560]{2,1,0:T(8,128)} %concatenate.28), calls=%async_computation | async-start | bytes 3407872 | tf_op jit(solution)/shard_map/all_to_all | solution.py:245
  178.8 1.4 scatter_custom_fusion
  180.2 1.5 scatter_custom_fusion.1
  181.8 2.2 slice.49
  184.0 3.7 %reshape_reshape.22 = bf16[64,3,64,128]{3,2,1,0:T(8,128)(2,1)} reshape(bf16[192,16,512]{2,1,0:T(8,128)(2,1)S(1)} %slice.44) | data formatting | bytes 6291456 | tf_op jit(solution)/shard_map/reshape;reshape | solution.py:267
  187.7 2.4 reshape_reshape.23
  190.1 2.9 fusion.28
  192.9 0.2 copy.149
  193.4 19.2 %all-to-all-done = f32[16,16,1560]{2,1,0:T(8,128)} async-done(((f32[16,16,1560]{2,1,0:T(8,128)}), f32[16,16,1560]{2,1,0:T(8,128)}, u32[]{:S(2)}, u32[]{:S(2)}) %all-to-all-start) | async-done | bytes 1597472 | tf_op jit(solution)/shard_map/all_to_all | solution.py:245
  212.6 1.0 slice_bitcast_fusion.8
  213.7 0.2 select_reduce_fusion
  214.0 0.7 gather_fusion.3
  214.7 1.1 slice_multiply_fusion.1
  216.1 0.5 copy.154
  216.5 1.6 slice_multiply_fusion
  218.1 0.7 fusion.5
  219.5 0.2 copy.157
  219.9 1.2 fusion.30
  221.1 0.3 broadcast_in_dim.249
  221.4 0.8 fusion.25
  222.2 52.2 %all-gather.7.cloned.1.call-done = bf16[192,8192]{1,0:T(8,128)(2,1)} async-done(((bf16[192,512]{1,0:T(8,128)(2,1)}), bf16[192,8192]{1,0:T(8,128)(2,1)}) %all-gather.7.cloned.1.call-update) | async-done | bytes 3145744 | tf_op jit(solution)/shard_map/all_gather | solution.py:309
  274.4 6.9 %convolution_convert_fusion = bf16[192,512]{1,0:T(8,128)(2,1)} fusion(bf16[192,8192]{1,0:T(8,128)(2,1)} %all-gather.7.cloned.1.call-done, bf16[8192,512]{1,0:T(8,128)(2,1)} %param.17), kind=kOutput, calls=%fused_computation.28 | convolution fusion | flops 1610711040 | bytes 11730944 | tf_op jit(solution)/shard_map/dot_general | solution.py:310
  (85 shorter events, 2.8 us)
Async XLA Ops:
  6.5 68.7 %copy-start = (bf16[8192,128]{1,0:T(8,128)(2,1)S(1)}, bf16[8192,128]{1,0:T(8,128)(2,1)}, u32[]{:S(2)}) copy-start(bf16[8192,128]{1,0:T(8,128)(2,1)} %param.16) | copy-start | bytes 6291460
  6.5 55.7 %copy-start.8 = (f32[8192]{0:T(1024)S(1)}, f32[8192]{0:T(1024)}, u32[]{:S(2)}) copy-start(f32[8192]{0:T(1024)} %param.14) | copy-start | bytes 98308
  6.5 55.7 %copy-start.6 = (bf16[1,64,8192]{2,1,0:T(8,128)(2,1)S(1)}, bf16[1,64,8192]{2,1,0:T(8,128)(2,1)}, u32[]{:S(2)}) copy-start(bf16[1,64,8192]{2,1,0:T(8,128)(2,1)} %param.18) | copy-start | bytes 3145732
  6.5 53.0 %all-gather.5.cloned.1.call-start = ((), (), s32[]{:S(2)}) async-start(), calls=%async_computation.1 | async-start | bytes 3342336 | tf_op jit(solution)/shard_map/all_gather | solution.py:119
  7.3 123.1 %all-gather.9.cloned.1.call-start = ((), (), s32[]{:S(2)}) async-start(), calls=%async_computation.3 | async-start | bytes 4177920 | tf_op jit(solution)/shard_map/all_gather | solution.py:170
  59.5 2.8 copy-start.2
  63.5 7.2 %collective-permute-start.2 = (bf16[192,64]{0,1:T(8,128)(2,1)S(1)}, bf16[192,64]{0,1:T(8,128)(2,1)S(1)}, u32[]{:S(2)}, u32[]{:S(2)}) collective-permute-start(bf16[192,64]{0,1:T(8,128)(2,1)S(1)} %fusion.13), channel_id=1, source_target_pairs={{0,3},{1,2},{2,1},{3,0},{4,7},{5,6},{6,5},{7,4},{8,11},{9,10},{10,... | collective-permute-start | bytes 73736 | tf_op jit(solution)/shard_map/ppermute | solution.py:97
  64.7 6.0 %collective-permute-start.1 = (bf16[192,64]{0,1:T(8,128)(2,1)S(1)}, bf16[192,64]{0,1:T(8,128)(2,1)S(1)}, u32[]{:S(2)}, u32[]{:S(2)}) collective-permute-start(bf16[192,64]{0,1:T(8,128)(2,1)S(1)} %fusion.13), channel_id=1, source_target_pairs={{0,2},{1,3},{2,0},{3,1},{4,6},{5,7},{6,4},{7,5},{8,10},{9,11},{10,... | collective-permute-start | bytes 73736 | tf_op jit(solution)/shard_map/ppermute | solution.py:97
  65.5 5.3 %collective-permute-start = (bf16[192,64]{0,1:T(8,128)(2,1)S(1)}, bf16[192,64]{0,1:T(8,128)(2,1)S(1)}, u32[]{:S(2)}, u32[]{:S(2)}) collective-permute-start(bf16[192,64]{0,1:T(8,128)(2,1)S(1)} %fusion.13), channel_id=1, source_target_pairs={{0,1},{1,0},{2,3},{3,2},{4,5},{5,4},{6,7},{7,6},{8,9},{9,8},{10,11... | collective-permute-start | bytes 73736 | tf_op jit(solution)/shard_map/ppermute | solution.py:97
  70.8 7.1 %copy-start.7 = (bf16[16,64,512]{2,1,0:T(8,128)(2,1)S(1)}, bf16[16,64,512]{2,1,0:T(8,128)(2,1)}, u32[]{:S(2)}) copy-start(bf16[16,64,512]{2,1,0:T(8,128)(2,1)} %param.19) | copy-start | bytes 3145732
  70.8 6.1 %collective-permute-start.5 = (bf16[192,64]{0,1:T(8,128)(2,1)S(1)}, bf16[192,64]{0,1:T(8,128)(2,1)S(1)}, u32[]{:S(2)}, u32[]{:S(2)}) collective-permute-start(bf16[192,64]{0,1:T(8,128)(2,1)S(1)} %add_add_fusion.1), channel_id=1, source_target_pairs={{0,12},{1,13},{2,14},{3,15},{4,8},{5,9},{6,10},{7,11},{8,4},{9,5},... | collective-permute-start | bytes 73736 | tf_op jit(solution)/shard_map/ppermute | solution.py:97
  72.3 5.6 %collective-permute-start.4 = (bf16[192,64]{0,1:T(8,128)(2,1)S(1)}, bf16[192,64]{0,1:T(8,128)(2,1)S(1)}, u32[]{:S(2)}, u32[]{:S(2)}) collective-permute-start(bf16[192,64]{0,1:T(8,128)(2,1)S(1)} %add_add_fusion.1), channel_id=1, source_target_pairs={{0,8},{1,9},{2,10},{3,11},{4,12},{5,13},{6,14},{7,15},{8,0},{9,1},... | collective-permute-start | bytes 73736 | tf_op jit(solution)/shard_map/ppermute | solution.py:97
  72.4 5.4 %collective-permute-start.3 = (bf16[192,64]{0,1:T(8,128)(2,1)S(1)}, bf16[192,64]{0,1:T(8,128)(2,1)S(1)}, u32[]{:S(2)}, u32[]{:S(2)}) collective-permute-start(bf16[192,64]{0,1:T(8,128)(2,1)S(1)} %add_add_fusion.1), channel_id=1, source_target_pairs={{0,4},{1,5},{2,6},{3,7},{4,0},{5,1},{6,2},{7,3},{8,12},{9,13},{10,... | collective-permute-start | bytes 73736 | tf_op jit(solution)/shard_map/ppermute | solution.py:97
  81.5 12.3 %copy-start.4 = (s32[64,4]{0,1:T(4,128)S(1)}, s32[64,4]{0,1:T(4,128)}, u32[]{:S(2)}) copy-start(s32[64,4]{0,1:T(4,128)} %param.24) | copy-start | bytes 3076
  81.5 12.5 %copy-start.5 = (s32[64]{0:T(128)S(1)}, s32[64]{0:T(128)}, u32[]{:S(2)}) copy-start(s32[64]{0:T(128)} %param.23) | copy-start | bytes 772
  174.0 38.7 %all-to-all-start = ((f32[16,16,1560]{2,1,0:T(8,128)}), f32[16,16,1560]{2,1,0:T(8,128)}, u32[]{:S(2)}, u32[]{:S(2)}) async-start(f32[16,16,1560]{2,1,0:T(8,128)} %concatenate.28), calls=%async_computation | async-start | bytes 3407872 | tf_op jit(solution)/shard_map/all_to_all | solution.py:245
  178.4 96.0 %all-gather.7.cloned.1.call-start = ((), (), s32[]{:S(2)}) async-start(), calls=%async_computation.2 | async-start | bytes 3342336 | tf_op jit(solution)/shard_map/all_gather | solution.py:309
  190.1 25.8 %copy-start.3 = (bf16[64,3,2048]{2,1,0:T(4,128)(2,1)}, bf16[64,3,2048]{2,1,0:T(4,128)(2,1)S(1)}, u32[]{:S(2)}) copy-start(bf16[64,3,2048]{2,1,0:T(4,128)(2,1)S(1)} %reshape_reshape.23) | copy-start | bytes 2359300
  274.4 6.9 %copy-start.1 = (bf16[8192,128]{1,0:T(8,128)(2,1)S(1)}, bf16[8192,128]{1,0:T(8,128)(2,1)}, u32[]{:S(2)}) copy-start(bf16[8192,128]{1,0:T(8,128)(2,1)} %param.16) | copy-start | bytes 6291460
Sparse Core Ops, SparseCore 0:
  9.5 49.9 all-gather.4
  81.7 48.6 all-gather.8
  222.3 52.0 all-gather.6

commit v6 on v4

--- a/solution.py
+++ b/solution.py
@@ -167,27 +167,42 @@
         ]
     )
     rotated_parts = rotate_columns(both_parts, token_positions, global_cols, limits)
-    joined = lax.all_gather(rotated_parts, "blk", axis=1, tiled=False)
-    query_vectors = joined[:, :, :query_cols].reshape(joined.shape[0], -1)
-    key_value_rows = joined[:, :, query_cols:].reshape(joined.shape[0], -1)
+    device_count = lax.axis_size("blk")
+    request_page_count = key_value_page_pool.shape[0]
+    table_width = request_page_tables.shape[1]
+    group_pages = device_count * request_page_count
+    listed_pages = request_page_tables.reshape(-1)
+    listed_target = jnp.where(listed_pages >= 0, listed_pages, group_pages)
+    page_of_req = (
+        jnp.zeros((group_pages,), jnp.int32)
+        .at[listed_target]
+        .set(jnp.repeat(jnp.arange(request_count, dtype=jnp.int32), table_width), mode="drop")
+    )
+    page_used = jnp.zeros((group_pages,), jnp.bool_).at[listed_target].set(True, mode="drop")
+    owner_of_page = (
+        jnp.arange(request_count, dtype=jnp.int32)[:, None] == page_of_req[None, :]
+    ) & page_used[None, :]
+    part_rows = rotated_parts.reshape(request_count, NEW_TOKENS, -1)
+    part_width = part_rows.shape[2]
+    outgoing = part_rows[page_of_req].reshape(
+        device_count, request_page_count, NEW_TOKENS * part_width
+    )
+    incoming = (
+        lax.all_to_all(outgoing, "blk", 0, 0, tiled=True)
+        .reshape(device_count, request_page_count, NEW_TOKENS, part_width)
+        .transpose(1, 2, 0, 3)
+    )
+    slot_queries = incoming[..., :query_cols].reshape(request_page_count, NEW_TOKENS, -1)
+    slot_fresh = incoming[..., query_cols:].reshape(
+        request_page_count, NEW_TOKENS, 2, KEY_VALUE_HEADS, HEAD_WIDTH
+    )
     query_group_width = QUERY_HEADS // KEY_VALUE_HEADS
     query_feature_width = query_group_width * NEW_TOKENS
     score_scale = 1.0 / math.sqrt(HEAD_WIDTH)
-    query_split = query_vectors.reshape(
-        request_count, NEW_TOKENS, KEY_VALUE_HEADS, query_group_width, HEAD_WIDTH
-    )
-    fresh_token_rows = key_value_rows.reshape(
-        request_count, NEW_TOKENS, 2, KEY_VALUE_HEADS, HEAD_WIDTH
-    )
-    request_page_count = key_value_page_pool.shape[0]
-    table_width = request_page_tables.shape[1]
     page_ids = own_index * request_page_count + jnp.arange(request_page_count, dtype=jnp.int32)
     matches = request_page_tables[None, :, :] == page_ids[:, None, None]
     page_owner = jnp.any(matches, axis=2)
     page_live = jnp.any(page_owner, axis=1)
-    page_req = jnp.sum(
-        jnp.where(page_owner, jnp.arange(request_count, dtype=jnp.int32)[None, :], 0), axis=1
-    )
     page_slot = jnp.sum(
         jnp.where(matches, jnp.arange(table_width, dtype=jnp.int32)[None, None, :], 0), axis=(1, 2)
     )
@@ -195,54 +210,50 @@
     key_pos = page_slot[:, None] * PAGE_LENGTH + jnp.arange(PAGE_LENGTH, dtype=jnp.int32)[None, :]
     key_valid = page_live[:, None] & (key_pos < page_len[:, None])
     valid_full = key_valid[:, None, None, :]
-    gathered_cache_pages = key_value_page_pool.reshape(
+    takes_fresh = page_live & (page_slot == 0)
+    step_of = jnp.arange(query_feature_width, dtype=jnp.int32) // query_group_width
+    fresh_valid = takes_fresh[:, None, None, None] & (
+        jnp.arange(NEW_TOKENS, dtype=jnp.int32)[None, None, None, :] <= step_of[None, None, :, None]
+    )
+    cache_pages = key_value_page_pool.reshape(
         request_page_count, PAGE_LENGTH, 2, KEY_VALUE_HEADS, HEAD_WIDTH
     )
     query_page = (
-        query_split[page_req]
+        slot_queries.reshape(
+            request_page_count, NEW_TOKENS, KEY_VALUE_HEADS, query_group_width, HEAD_WIDTH
+        )
         .transpose(0, 2, 1, 3, 4)
         .reshape(request_page_count, KEY_VALUE_HEADS, query_feature_width, HEAD_WIDTH)
     )
     scores = (
         jnp.einsum(
-            "skqd,spkd->skqp",
-            query_page,
-            gathered_cache_pages[:, :, 0],
-            preferred_element_type=jnp.float32,
+            "skqd,spkd->skqp", query_page, cache_pages[:, :, 0], preferred_element_type=jnp.float32
         )
         * score_scale
     )
+    fresh_scores = (
+        jnp.einsum(
+            "skqd,sjkd->skqj", query_page, slot_fresh[:, :, 0], preferred_element_type=jnp.float32
+        )
+        * score_scale
+    )
     masked = jnp.where(valid_full, scores, neg_large)
-    page_peak = jnp.max(masked, axis=-1)
-    req_peak = jnp.max(
-        jnp.where(page_owner[:, :, None, None], page_peak[:, None], neg_large), axis=0
-    )
-    query_wide = query_split.astype(jnp.float32)
-    fresh_keys = fresh_token_rows[:, :, 0].astype(jnp.float32)
-    fresh_scores = (
-        jnp.stack(
-            [
-                jnp.sum(query_wide * fresh_keys[:, j][:, None, :, None, :], axis=-1)
-                for j in range(NEW_TOKENS)
-            ],
-            axis=-1,
-        )
-        .transpose(0, 2, 1, 3, 4)
-        .reshape(request_count, KEY_VALUE_HEADS, query_feature_width, NEW_TOKENS)
-        * score_scale
-    )
-    step_of = jnp.arange(query_feature_width, dtype=jnp.int32) // query_group_width
-    fresh_ok = (jnp.arange(NEW_TOKENS, dtype=jnp.int32)[None, :] <= step_of[:, None])[None, None]
-    fresh_masked = jnp.where(fresh_ok, fresh_scores, neg_large)
-    top_score = butterfly(jnp.maximum(req_peak, jnp.max(fresh_masked, axis=-1)), jnp.maximum)
-    weights = jnp.where(valid_full, jnp.exp(masked - top_score[page_req][..., None]), 0.0)
+    fresh_masked = jnp.where(fresh_valid, fresh_scores, neg_large)
+    page_peak = jnp.maximum(jnp.max(masked, axis=-1), jnp.max(fresh_masked, axis=-1))
+    weights = jnp.where(valid_full, jnp.exp(masked - page_peak[..., None]), 0.0)
+    fresh_weights = jnp.where(fresh_valid, jnp.exp(fresh_masked - page_peak[..., None]), 0.0)
     page_num = jnp.einsum(
         "skqp,spkd->skqd",
         weights.astype(jnp.bfloat16),
-        gathered_cache_pages[:, :, 1],
+        cache_pages[:, :, 1],
         preferred_element_type=jnp.float32,
-    )
-    device_count = lax.axis_size("blk")
+    ) + jnp.einsum(
+        "skqj,sjkd->skqd",
+        fresh_weights.astype(jnp.bfloat16),
+        slot_fresh[:, :, 1],
+        preferred_element_type=jnp.float32,
+    )
+    page_den = jnp.sum(weights, axis=-1) + jnp.sum(fresh_weights, axis=-1)
     head_count = QUERY_HEADS
     owner_cols = query_cols
     owner_heads = max(1, owner_cols // HEAD_WIDTH)
@@ -252,53 +263,34 @@
         [[first + j for j in range(owner_heads)] for first in owner_first_head], jnp.int32
     )
     slot_num = to_tokens(page_num).reshape(request_page_count, NEW_TOKENS, device_count, owner_cols)
-    slot_den = to_tokens(jnp.sum(weights, axis=-1)[..., None]).reshape(
-        request_page_count, NEW_TOKENS, head_count
-    )
-    slot_den_owner = slot_den[:, :, head_pick]
-    packed = jnp.concatenate([slot_num, slot_den_owner], axis=3).transpose(2, 0, 1, 3)
-    received = lax.all_to_all(packed, "blk", 0, 0, tiled=True)
-    group_pages = device_count * request_page_count
-    all_page_ids = jnp.arange(group_pages, dtype=jnp.int32)
-    all_owner = jnp.any(request_page_tables[None, :, :] == all_page_ids[:, None, None], axis=2)
-    pick_req = all_owner.T.astype(jnp.float32)
+    slot_den = to_tokens(page_den[..., None]).reshape(request_page_count, NEW_TOKENS, head_count)
+    slot_peak = to_tokens(page_peak[..., None]).reshape(request_page_count, NEW_TOKENS, head_count)
+    packed = jnp.concatenate(
+        [
+            part.transpose(2, 0, 1, 3).reshape(device_count, request_page_count, -1)
+            for part in (slot_num, slot_den[:, :, head_pick], slot_peak[:, :, head_pick])
+        ],
+        axis=2,
+    )
+    arrived = lax.all_to_all(packed, "blk", 0, 0, tiled=True).reshape(group_pages, -1)
+    num_width = NEW_TOKENS * owner_cols
+    head_width = NEW_TOKENS * owner_heads
+    arrived_num = arrived[:, :num_width]
+    arrived_den = arrived[:, num_width : num_width + head_width]
+    arrived_peak = arrived[:, num_width + head_width :]
+    top_flat = jnp.max(
+        jnp.where(owner_of_page[:, None, :], arrived_peak.T[None], neg_large), axis=2
+    )
+    rescale = jnp.exp(arrived_peak - top_flat[page_of_req])
+    rescaled = jnp.concatenate(
+        [arrived_num * jnp.repeat(rescale, head_repeat, axis=1), arrived_den * rescale], axis=1
+    )
     summed = jnp.einsum(
-        "rp,px->rx",
-        pick_req,
-        received.reshape(group_pages, -1),
-        precision=lax.Precision.HIGHEST,
-    ).reshape(request_count, NEW_TOKENS, owner_cols + owner_heads)
-    fresh_weights = jnp.where(fresh_ok, jnp.exp(fresh_masked - top_score[..., None]), 0.0)
-    fresh_by_head = (
-        fresh_weights.reshape(
-            request_count, KEY_VALUE_HEADS, NEW_TOKENS, query_group_width, NEW_TOKENS
-        )
-        .transpose(0, 2, 1, 3, 4)
-        .reshape(request_count, NEW_TOKENS, QUERY_HEADS, NEW_TOKENS)
-    )
-    first_head = (own_index * owner_cols) // HEAD_WIDTH
-    weights_own = lax.dynamic_slice_in_dim(fresh_by_head, first_head, owner_heads, axis=2)
-    value_col = (
-        KEY_VALUE_HEADS * HEAD_WIDTH
-        + (first_head // query_group_width) * HEAD_WIDTH
-        + (own_index * owner_cols) % HEAD_WIDTH
-    )
-    values_own = lax.dynamic_slice_in_dim(
-        key_value_rows.reshape(request_count, NEW_TOKENS, -1), value_col, head_repeat, axis=2
-    )
-    fresh_num_own = jnp.einsum(
-        "rihj,rjd->rihd",
-        weights_own.astype(jnp.bfloat16),
-        values_own,
-        preferred_element_type=jnp.float32,
-    ).reshape(request_count * NEW_TOKENS, owner_cols)
-    fresh_den_own = jnp.sum(weights_own, axis=-1).reshape(request_count * NEW_TOKENS, owner_heads)
-    num_own = summed[:, :, :owner_cols].reshape(request_count * NEW_TOKENS, owner_cols)
-    den_own = summed[:, :, owner_cols:].reshape(request_count * NEW_TOKENS, owner_heads)
-    totals = den_own + fresh_den_own
-    attended_own = ((num_own + fresh_num_own) / jnp.repeat(totals, head_repeat, axis=1)).astype(
-        jnp.bfloat16
-    )
+        "rp,px->rx", owner_of_page.astype(jnp.float32), rescaled, precision=lax.Precision.HIGHEST
+    )
+    num_own = summed[:, :num_width].reshape(request_count * NEW_TOKENS, owner_cols)
+    den_own = summed[:, num_width:].reshape(request_count * NEW_TOKENS, owner_heads)
+    attended_own = (num_own / jnp.repeat(den_own, head_repeat, axis=1)).astype(jnp.bfloat16)
     attended = lax.all_gather(attended_own, "blk", axis=1, tiled=True)
     return jnp.dot(attended, output_weight, preferred_element_type=jnp.float32).astype(jnp.bfloat16)
 

time: 333 us -> 254 us (0.76)
  waiting for transfers between devices: 202 us -> 141 us
  local copies, waits for them, and re-layouts: 50.8 us -> 39.4 us
  other arithmetic: 20.4 us -> 13.2 us
    all_gather x1 -> x0, waiting for transfers between devices: 35.8 us -> none  [local(): joined = lax.all_gather(rotated_parts, 'blk', axis=1, tiled=False)]
    ppermute x12 -> x6, waiting for transfers between devices: 35.6 us -> 2.17 us  [butterfly(): lax.ppermute(value, 'blk', [(i, i ^ m) for i in range(size)])]
    all_to_all x1 -> x2, waiting for transfers between devices: 29.6 us -> 41.3 us  [the longest x1 32.5 us: local(): lax.all_to_all(packed, 'blk', 0, 0, tiled=True).reshape(group_pages, -1)]
    another operation x10 -> x5, local copies, waits for them, and re-layouts: 10.6 us -> 0.62 us  [the longest x1 0.47 us: local(): slot_queries.reshape(request_page_count, NEW_TOKENS, KEY_VALUE_HEADS, que...]
    all_to_all x1 -> x2, starting transfers between devices: 3.72 us -> 11 us  [the longest x1 6.53 us: local(): lax.all_to_all(packed, 'blk', 0, 0, tiled=True).reshape(group_pages, -1)]
    reduce_sum x3 -> x2, other arithmetic: 7.73 us -> 1.18 us  [local(): page_den = jnp.sum(weights, axis=-1) + jnp.sum(fresh_weights, axis=-1)]
    ppermute x12 -> x6, starting transfers between devices: 12.8 us -> 6.38 us  [butterfly(): lax.ppermute(value, 'blk', [(i, i ^ m) for i in range(size)])]
    reshape x2 -> x11, local copies, waits for them, and re-layouts: 3.32 us -> 8.91 us  [the longest x1 3.02 us: local(): jnp.repeat(rescale, head_repeat, axis=1)]
  transfers between devices with their start and end apart: 16 -> 10, of which waited for: 10 -> 5; matrix products, arithmetic and copies ran while one was open for 10% -> 11% of each run, Pallas kernels for 0% -> 0%
where the time goes in v6:
time: 254 us; the launch traced here: 253 us
  waiting for transfers between devices  141 us (56%)
  local copies, waits for them, and re-layouts  39.4 us (16%)
  matrix products  25.6 us (10%)
  starting transfers between devices  17.4 us (7%)
  between operations  14 us (6%)
  other arithmetic  13.2 us (5%)
    all_gather x1, waiting for transfers between devices, local(): attended = lax.all_gather(attended_own, 'blk', axis=1, tiled=True)  52.3 us
    all_gather x1, waiting for transfers between devices, local(): gathered = lax.all_gather(layer_input_tokens, 'blk', axis=1, tiled=True)  44.3 us
    all_to_all x1, waiting for transfers between devices, local(): lax.all_to_all(packed, 'blk', 0, 0, tiled=True).reshape(group_pages, -1)  32.5 us
    unnamed x18, local copies, waits for them, and re-layouts  13.6 us
    all_to_all x1, waiting for transfers between devices, local(): lax.all_to_all(outgoing, 'blk', 0, 0, tiled=True)  8.83 us
    dot_general x1, matrix products, local(): jnp.dot(attended, output_weight, preferred_element_type=jnp.float32)  6.94 us
    all_to_all x1, starting transfers between devices, local(): lax.all_to_all(packed, 'blk', 0, 0, tiled=True).reshape(group_pages, -1)  6.53 us
    ppermute x6, starting transfers between devices, butterfly(): lax.ppermute(value, 'blk', [(i, i ^ m) for i in range(size)])  6.38 us
  transfers between devices with their start and end apart: 10, of which 5 were waited for; matrix products, arithmetic and copies ran while one was open for 11% of the time, Pallas kernels for 0%

profile of v6, /device:TPU:0, one launch (start us, length us, event | category | flops | bytes accessed | tf_op | source)
XLA Modules:
  0.0 252.9 jit_solution(10308774158104880869)
XLA Ops:
  6.5 0.7 all-gather.3.cloned.1.call-update
  7.3 0.8 select_reduce_fusion.1
  8.2 0.7 add_convert_fusion
  9.1 0.8 copy.70
  10.1 1.4 scatter_custom_fusion
  11.6 0.7 fusion.45
  12.3 2.8 %fusion.26 = (f32[192,640]{1,0:T(8,128)}, f32[192,640]{1,0:T(8,128)}) fusion(f32[640]{0:T(1024)S(1)} %fusion.44, f32[192]{0:T(256)S(1)} %convert_element_type.43, pred[640]{0:T(1024)(128)(4,1)S(1)} %fusion.45), kind=kLoop, calls=%fused_computation.47 | loop fusion | flops 368640 | bytes 987008 | tf_op jit(solution)/shard_map/jit(_where)/select_n | solution.py:57
  15.1 44.3 %all-gather.3.cloned.1.call-done = bf16[192,8192]{1,0:T(8,128)(2,1)} async-done(((bf16[192,512]{1,0:T(8,128)(2,1)}), bf16[192,8192]{1,0:T(8,128)(2,1)}) %all-gather.3.cloned.1.call-update) | async-done | bytes 3145744 | tf_op jit(solution)/shard_map/all_gather | solution.py:119
  59.5 2.8 %fusion = f32[192]{0:T(256)S(1)} fusion(bf16[192,8192]{1,0:T(8,128)(2,1)} %all-gather.3.cloned.1.call-done), kind=kLoop, calls=%fused_computation.8 | loop fusion | flops 4718400 | bytes 3146496 | tf_op jit(solution)/shard_map/reduce_sum | solution.py:70
  62.3 2.4 fusion.13
  64.7 0.3 collective-permute-start
  65.0 1.3 collective-permute-start.1
  66.3 0.3 collective-permute-start.2
  66.6 5.2 %fusion.59 = f32[192,512]{1,0:T(8,128)S(1)} fusion(bf16[8192,512]{1,0:T(8,128)(2,1)} %param.15, bf16[192,8192]{1,0:T(8,128)(2,1)S(1)} %copy-done.3, f32[8192]{0:T(1024)S(1)} %copy-done.7, f32[192]{0:T(256)S(1)} %add_rsqrt_fusion), kind=kOutput, calls=%fused_computation.126 | convolution fusion | flops 1616904192 | bytes 11961088 | tf_op jit(solution)/shard_map/dot_general | solution.py:151
  71.9 0.2 collective-permute-start.3
  72.1 1.9 collective-permute-start.4
  74.0 2.4 collective-permute-start.5
  76.4 1.1 fusion.56
  77.6 2.2 collective-permute-done.5
  79.7 0.4 fusion.11
  80.1 0.8 pad_maximum_fusion.values_ref
  80.9 2.4 shard_map.127
  83.4 1.1 reshape.388
  84.4 1.9 gather_fusion
  86.3 1.7 reshape.389
  88.0 4.5 %all-to-all-start = ((bf16[16,16,1920]{2,1,0:T(8,128)(2,1)}), bf16[16,16,1920]{2,1,0:T(8,128)(2,1)S(1)}, u32[]{:S(2)}, u32[]{:S(2)}) async-start(bf16[16,16,1920]{2,1,0:T(8,128)(2,1)} %reshape.389), calls=%async_computation | async-start | bytes 1966080 | tf_op jit(solution)/shard_map/all_to_all | solution.py:191
  92.6 12.3 %copy.73 = bf16[16,128,2048]{1,2,0:T(8,128)(2,1)} copy(bf16[16,128,2048]{2,1,0:T(8,128)(2,1)} %param.20) | data formatting | bytes 16777216 | tf_op args[7]
  104.9 0.2 compare_reduce_fusion
  105.2 0.2 fusion.38
  105.6 8.8 %all-to-all-done = bf16[16,16,1920]{2,1,0:T(8,128)(2,1)S(1)} async-done(((bf16[16,16,1920]{2,1,0:T(8,128)(2,1)}), bf16[16,16,1920]{2,1,0:T(8,128)(2,1)S(1)}, u32[]{:S(2)}, u32[]{:S(2)}) %all-to-all-start) | async-done | bytes 983072 | tf_op jit(solution)/shard_map/all_to_all | solution.py:191
  114.4 0.3 reshape.390
  114.7 0.4 slice.52
  115.2 0.6 copy.71
  115.8 0.5 reshape_reshape.12
  116.3 0.2 copy.126
  116.5 3.5 %fusion.62 = (f32[16,8,24]{2,1,0:T(8,128)S(1)}, f32[16,8,24,128]{3,2,1,0:T(8,128)S(1)}) fusion(bf16[16,128,2,8,128]{1,4,3,2,0:T(8,128)(2,1)} %bitcast.97, pred[16,128]{1,0:T(8,128)(4,1)S(1)} %fusion.39, bf16[16,3,8,8,128]{4,3,2,1,0:T(8,128)(2,1)S(1)} %reshape_reshape.12), kind=kOutput, calls=%fused_computation.128 | convolution fusion | flops 101839872 | bytes 6567936 | tf_op jit(solution)/shard_map/skqd,spkd->skqp/dot_general | solution.py:229
  120.0 0.5 fusion.63
  120.7 0.3 fusion.30
  120.9 0.9 fusion.9
  122.1 0.7 gather_fusion.1
  122.8 0.2 copy.91
  122.9 0.6 fusion.32
  123.6 4.1 %add_bitcast_fusion = f32[16,8,3,8,128]{4,3,2,1,0:T(8,128)S(1)} fusion(f32[16,8,24,128]{3,2,1,0:T(8,128)S(1)} %fusion.32, bf16[16,128,2,8,128]{1,4,3,2,0:T(8,128)(2,1)} %bitcast.98, f32[16,8,24,128]{3,2,1,0:T(8,128)S(1)} %get-tuple-element.14, f32[16,8,24]{2,1,0:T(8,128)S(1)} %max.17, pred[16,128]{1,0:T(8,128)(4,1)S(1)} %fusion.39), kind=kOutput, calls=%fused_computation.21 | convolution fusion | flops 102236160 | bytes 8927232 | tf_op jit(solution)/shard_map/skqp,spkd->skqd/dot_general | solution.py:245
  127.7 0.2 copy.125
  127.9 1.4 reshape_reshape.13
  129.3 2.5 copy.80
  131.8 2.1 reshape.395
  134.0 0.7 gather_fusion.2
  134.6 0.2 copy.92
  134.8 0.5 copy-done.2
  135.3 1.4 concatenate.28
  136.7 6.5 %all-to-all-start.1 = ((f32[16,16,1560]{2,1,0:T(8,128)}), f32[16,16,1560]{2,1,0:T(8,128)S(1)}, u32[]{:S(2)}, u32[]{:S(2)}) async-start(f32[16,16,1560]{2,1,0:T(8,128)} %concatenate.28), calls=%async_computation.1 | async-start | bytes 3407872 | tf_op jit(solution)/shard_map/all_to_all | solution.py:275
  143.3 1.7 scatter_custom_fusion.1
  145.0 32.5 %all-to-all-done.1 = f32[16,16,1560]{2,1,0:T(8,128)S(1)} async-done(((f32[16,16,1560]{2,1,0:T(8,128)}), f32[16,16,1560]{2,1,0:T(8,128)S(1)}, u32[]{:S(2)}, u32[]{:S(2)}) %all-to-all-start.1) | async-done | bytes 1597472 | tf_op jit(solution)/shard_map/all_to_all | solution.py:275
  177.7 0.2 select_reduce_fusion
  177.9 0.7 gather_fusion.3
  178.9 1.3 broadcast_in_dim.239
  180.2 3.0 %copy.96 = f32[256,1536]{1,0:T(8,128)} copy(f32[256,1536]{0,1:T(8,128)} %bitcast.104) | data formatting | bytes 3145728 | tf_op jit(solution)/shard_map/reshape | solution.py:286
  183.2 1.6 slice_multiply_fusion
  184.8 0.7 fusion.5
  185.7 0.3 broadcast_in_dim.240
  186.0 0.7 fusion.27
  186.8 52.3 %all-gather.5.cloned.1.call-done = bf16[192,8192]{1,0:T(8,128)(2,1)} async-done(((bf16[192,512]{1,0:T(8,128)(2,1)}), bf16[192,8192]{1,0:T(8,128)(2,1)}) %all-gather.5.cloned.1.call-update) | async-done | bytes 3145744 | tf_op jit(solution)/shard_map/all_gather | solution.py:294
  239.1 6.9 %convolution_convert_fusion = bf16[192,512]{1,0:T(8,128)(2,1)} fusion(bf16[192,8192]{1,0:T(8,128)(2,1)} %all-gather.5.cloned.1.call-done, bf16[8192,512]{1,0:T(8,128)(2,1)} %param.17), kind=kOutput, calls=%fused_computation.28 | convolution fusion | flops 1610711040 | bytes 11730944 | tf_op jit(solution)/shard_map/dot_general | solution.py:295
  (75 shorter events, 2.4 us)
Async XLA Ops:
  6.5 69.9 %copy-start = (bf16[8192,128]{1,0:T(8,128)(2,1)S(1)}, bf16[8192,128]{1,0:T(8,128)(2,1)}, u32[]{:S(2)}) copy-start(bf16[8192,128]{1,0:T(8,128)(2,1)} %param.16) | copy-start | bytes 6291460
  6.5 52.9 %all-gather.3.cloned.1.call-start = ((), (), s32[]{:S(2)}) async-start(), calls=%async_computation.2 | async-start | bytes 3342336 | tf_op jit(solution)/shard_map/all_gather | solution.py:119
  10.0 52.2 %copy-start.7 = (f32[8192]{0:T(1024)S(1)}, f32[8192]{0:T(1024)}, u32[]{:S(2)}) copy-start(f32[8192]{0:T(1024)} %param.14) | copy-start | bytes 98308
  59.5 2.8 %copy-start.3 = (bf16[192,8192]{1,0:T(8,128)(2,1)S(1)}, bf16[192,8192]{1,0:T(8,128)(2,1)}, u32[]{:S(2)}) copy-start(bf16[192,8192]{1,0:T(8,128)(2,1)} %all-gather.3.cloned.1.call-done) | copy-start | bytes 9437188
  64.7 7.2 %collective-permute-start = (bf16[192,64]{0,1:T(8,128)(2,1)S(1)}, bf16[192,64]{0,1:T(8,128)(2,1)S(1)}, u32[]{:S(2)}, u32[]{:S(2)}) collective-permute-start(bf16[192,64]{0,1:T(8,128)(2,1)S(1)} %fusion.13), channel_id=1, source_target_pairs={{0,1},{1,0},{2,3},{3,2},{4,5},{5,4},{6,7},{7,6},{8,9},{9,8},{10,11... | collective-permute-start | bytes 73736 | tf_op jit(solution)/shard_map/ppermute | solution.py:97
  65.0 6.8 %collective-permute-start.1 = (bf16[192,64]{0,1:T(8,128)(2,1)S(1)}, bf16[192,64]{0,1:T(8,128)(2,1)S(1)}, u32[]{:S(2)}, u32[]{:S(2)}) collective-permute-start(bf16[192,64]{0,1:T(8,128)(2,1)S(1)} %fusion.13), channel_id=1, source_target_pairs={{0,2},{1,3},{2,0},{3,1},{4,6},{5,7},{6,4},{7,5},{8,10},{9,11},{10,... | collective-permute-start | bytes 73736 | tf_op jit(solution)/shard_map/ppermute | solution.py:97
  66.3 5.6 %collective-permute-start.2 = (bf16[192,64]{0,1:T(8,128)(2,1)S(1)}, bf16[192,64]{0,1:T(8,128)(2,1)S(1)}, u32[]{:S(2)}, u32[]{:S(2)}) collective-permute-start(bf16[192,64]{0,1:T(8,128)(2,1)S(1)} %fusion.13), channel_id=1, source_target_pairs={{0,3},{1,2},{2,1},{3,0},{4,7},{5,6},{6,5},{7,4},{8,11},{9,10},{10,... | collective-permute-start | bytes 73736 | tf_op jit(solution)/shard_map/ppermute | solution.py:97
  71.9 7.8 %copy-start.6 = (bf16[16,64,512]{2,1,0:T(8,128)(2,1)S(1)}, bf16[16,64,512]{2,1,0:T(8,128)(2,1)}, u32[]{:S(2)}) copy-start(bf16[16,64,512]{2,1,0:T(8,128)(2,1)} %param.19) | copy-start | bytes 3145732
  71.9 5.6 %collective-permute-start.3 = (bf16[192,64]{0,1:T(8,128)(2,1)S(1)}, bf16[192,64]{0,1:T(8,128)(2,1)S(1)}, u32[]{:S(2)}, u32[]{:S(2)}) collective-permute-start(bf16[192,64]{0,1:T(8,128)(2,1)S(1)} %add_add_fusion.1), channel_id=1, source_target_pairs={{0,4},{1,5},{2,6},{3,7},{4,0},{5,1},{6,2},{7,3},{8,12},{9,13},{10,... | collective-permute-start | bytes 73736 | tf_op jit(solution)/shard_map/ppermute | solution.py:97
  72.1 5.4 %collective-permute-start.4 = (bf16[192,64]{0,1:T(8,128)(2,1)S(1)}, bf16[192,64]{0,1:T(8,128)(2,1)S(1)}, u32[]{:S(2)}, u32[]{:S(2)}) collective-permute-start(bf16[192,64]{0,1:T(8,128)(2,1)S(1)} %add_add_fusion.1), channel_id=1, source_target_pairs={{0,8},{1,9},{2,10},{3,11},{4,12},{5,13},{6,14},{7,15},{8,0},{9,1},... | collective-permute-start | bytes 73736 | tf_op jit(solution)/shard_map/ppermute | solution.py:97
  74.0 5.7 %collective-permute-start.5 = (bf16[192,64]{0,1:T(8,128)(2,1)S(1)}, bf16[192,64]{0,1:T(8,128)(2,1)S(1)}, u32[]{:S(2)}, u32[]{:S(2)}) collective-permute-start(bf16[192,64]{0,1:T(8,128)(2,1)S(1)} %add_add_fusion.1), channel_id=1, source_target_pairs={{0,12},{1,13},{2,14},{3,15},{4,8},{5,9},{6,10},{7,11},{8,4},{9,5},... | collective-permute-start | bytes 73736 | tf_op jit(solution)/shard_map/ppermute | solution.py:97
  88.0 26.4 %all-to-all-start = ((bf16[16,16,1920]{2,1,0:T(8,128)(2,1)}), bf16[16,16,1920]{2,1,0:T(8,128)(2,1)S(1)}, u32[]{:S(2)}, u32[]{:S(2)}) async-start(bf16[16,16,1920]{2,1,0:T(8,128)(2,1)} %reshape.389), calls=%async_computation | async-start | bytes 1966080 | tf_op jit(solution)/shard_map/all_to_all | solution.py:191
  92.6 12.3 %copy-start.4 = (s32[64,4]{0,1:T(4,128)S(1)}, s32[64,4]{0,1:T(4,128)}, u32[]{:S(2)}) copy-start(s32[64,4]{0,1:T(4,128)} %param.24) | copy-start | bytes 3076
  92.6 12.5 %copy-start.5 = (s32[64]{0:T(128)S(1)}, s32[64]{0:T(128)}, u32[]{:S(2)}) copy-start(s32[64]{0:T(128)} %param.23) | copy-start | bytes 772
  133.9 1.4 copy-start.2
  136.7 40.8 %all-to-all-start.1 = ((f32[16,16,1560]{2,1,0:T(8,128)}), f32[16,16,1560]{2,1,0:T(8,128)S(1)}, u32[]{:S(2)}, u32[]{:S(2)}) async-start(f32[16,16,1560]{2,1,0:T(8,128)} %concatenate.28), calls=%async_computation.1 | async-start | bytes 3407872 | tf_op jit(solution)/shard_map/all_to_all | solution.py:275
  143.2 95.8 %all-gather.5.cloned.1.call-start = ((), (), s32[]{:S(2)}) async-start(), calls=%async_computation.3 | async-start | bytes 3342336 | tf_op jit(solution)/shard_map/all_gather | solution.py:294
  239.1 6.9 %copy-start.1 = (bf16[8192,128]{1,0:T(8,128)(2,1)S(1)}, bf16[8192,128]{1,0:T(8,128)(2,1)}, u32[]{:S(2)}) copy-start(bf16[8192,128]{1,0:T(8,128)(2,1)} %param.16) | copy-start | bytes 6291460
Sparse Core Ops, SparseCore 0:
  9.5 49.8 all-gather.2
  186.9 52.1 all-gather.4

commit v7 on v6

--- a/solution.py
+++ b/solution.py
@@ -265,19 +265,32 @@
     slot_num = to_tokens(page_num).reshape(request_page_count, NEW_TOKENS, device_count, owner_cols)
     slot_den = to_tokens(page_den[..., None]).reshape(request_page_count, NEW_TOKENS, head_count)
     slot_peak = to_tokens(page_peak[..., None]).reshape(request_page_count, NEW_TOKENS, head_count)
+    num_part, den_part, peak_part = [
+        part.transpose(2, 0, 1, 3).reshape(device_count, request_page_count, -1)
+        for part in (slot_num, slot_den[:, :, head_pick], slot_peak[:, :, head_pick])
+    ]
+    exact_part = jnp.concatenate([den_part, peak_part], axis=2)
+    high = lax.reduce_precision(exact_part, exponent_bits=8, mantissa_bits=7)
+    rest = exact_part - high
+    middle = lax.reduce_precision(rest, exponent_bits=8, mantissa_bits=7)
+    low = rest - middle
     packed = jnp.concatenate(
-        [
-            part.transpose(2, 0, 1, 3).reshape(device_count, request_page_count, -1)
-            for part in (slot_num, slot_den[:, :, head_pick], slot_peak[:, :, head_pick])
-        ],
+        [num_part.astype(jnp.bfloat16)] + [p.astype(jnp.bfloat16) for p in (high, middle, low)],
         axis=2,
     )
     arrived = lax.all_to_all(packed, "blk", 0, 0, tiled=True).reshape(group_pages, -1)
     num_width = NEW_TOKENS * owner_cols
     head_width = NEW_TOKENS * owner_heads
-    arrived_num = arrived[:, :num_width]
-    arrived_den = arrived[:, num_width : num_width + head_width]
-    arrived_peak = arrived[:, num_width + head_width :]
+    arrived_num = arrived[:, :num_width].astype(jnp.float32)
+    pieces = [
+        arrived[:, num_width + k * 2 * head_width : num_width + (k + 1) * 2 * head_width].astype(
+            jnp.float32
+        )
+        for k in range(3)
+    ]
+    arrived_exact = (pieces[0] + pieces[1]) + pieces[2]
+    arrived_den = arrived_exact[:, :head_width]
+    arrived_peak = arrived_exact[:, head_width:]
     top_flat = jnp.max(
         jnp.where(owner_of_page[:, None, :], arrived_peak.T[None], neg_large), axis=2
     )

time: 254 us -> 229 us (0.902)
  waiting for transfers between devices: 141 us -> 123 us
  local copies, waits for them, and re-layouts: 39.4 us -> 32.4 us
    all_to_all x1, waiting for transfers between devices: 32.5 us -> 18 us  [local(): lax.all_to_all(packed, 'blk', 0, 0, tiled=True).reshape(group_pages, -1)]
    all_gather x1, waiting for transfers between devices: 52.3 us -> 48.5 us  [local(): attended = lax.all_gather(attended_own, 'blk', axis=1, tiled=True)]
    unnamed x18 -> x16, local copies, waits for them, and re-layouts: 13.6 us -> 13.1 us
  transfers between devices with their start and end apart: 10 -> 10, of which waited for: 5 -> 5; matrix products, arithmetic and copies ran while one was open for 11% -> 13% of each run, Pallas kernels for 0% -> 0%
where the time goes in v7:
time: 229 us; the launch traced here: 228 us
  waiting for transfers between devices  123 us (54%)
  local copies, waits for them, and re-layouts  32.4 us (14%)
  matrix products  26.1 us (11%)
  starting transfers between devices  17.4 us (8%)
  between operations  14 us (6%)
  other arithmetic  13.4 us (6%)
  Pallas kernels  2.42 us (1%)
    all_gather x1, waiting for transfers between devices, local(): attended = lax.all_gather(attended_own, 'blk', axis=1, tiled=True)  48.5 us
    all_gather x1, waiting for transfers between devices, local(): gathered = lax.all_gather(layer_input_tokens, 'blk', axis=1, tiled=True)  44.3 us
    all_to_all x1, waiting for transfers between devices, local(): lax.all_to_all(packed, 'blk', 0, 0, tiled=True).reshape(group_pages, -1)  18 us
    unnamed x16, local copies, waits for them, and re-layouts  13.1 us
    all_to_all x1, waiting for transfers between devices, local(): lax.all_to_all(outgoing, 'blk', 0, 0, tiled=True)  8.83 us
    dot_general x1, matrix products, local(): jnp.dot(attended, output_weight, preferred_element_type=jnp.float32)  6.94 us
    all_to_all x1, starting transfers between devices, local(): lax.all_to_all(packed, 'blk', 0, 0, tiled=True).reshape(group_pages, -1)  6.52 us
    ppermute x6, starting transfers between devices, butterfly(): lax.ppermute(value, 'blk', [(i, i ^ m) for i in range(size)])  6.38 us
  transfers between devices with their start and end apart: 10, of which 5 were waited for; matrix products, arithmetic and copies ran while one was open for 13% of the time, Pallas kernels for 0%

profile of v7, /device:TPU:0, one launch (start us, length us, event | category | flops | bytes accessed | tf_op | source)
XLA Modules:
  0.0 228.2 jit_solution(17106982494823823072)
XLA Ops:
  6.5 0.7 all-gather.3.cloned.1.call-update
  7.3 0.8 select_reduce_fusion.1
  8.1 0.1 eq.92
  8.2 0.7 add_convert_fusion.1
  9.0 0.1 convert_element_type.77
  9.1 0.8 copy.70
  10.1 1.4 scatter_custom_fusion
  11.6 0.7 fusion.47
  12.3 2.8 %fusion.27 = (f32[192,640]{1,0:T(8,128)}, f32[192,640]{1,0:T(8,128)}) fusion(f32[640]{0:T(1024)S(1)} %fusion.46, f32[192]{0:T(256)S(1)} %convert_element_type.77, pred[640]{0:T(1024)(128)(4,1)S(1)} %fusion.47), kind=kLoop, calls=%fused_computation.48 | loop fusion | flops 368640 | bytes 987008 | tf_op jit(solution)/shard_map/jit(_where)/select_n | solution.py:57
  15.1 44.3 %all-gather.3.cloned.1.call-done = bf16[192,8192]{1,0:T(8,128)(2,1)} async-done(((bf16[192,512]{1,0:T(8,128)(2,1)}), bf16[192,8192]{1,0:T(8,128)(2,1)}) %all-gather.3.cloned.1.call-update) | async-done | bytes 3145744 | tf_op jit(solution)/shard_map/all_gather | solution.py:119
  59.5 2.8 %fusion = f32[192]{0:T(256)S(1)} fusion(bf16[192,8192]{1,0:T(8,128)(2,1)} %all-gather.3.cloned.1.call-done), kind=kLoop, calls=%fused_computation.8 | loop fusion | flops 4718400 | bytes 3146496 | tf_op jit(solution)/shard_map/reduce_sum | solution.py:70
  62.3 2.4 %fusion.14 = bf16[192,64]{0,1:T(8,128)(2,1)S(1)} fusion(bf16[1,64,8192]{2,1,0:T(8,128)(2,1)} %param.18, pred[192]{0:T(512)(128)(4,1)S(1)} %subtract_compare_fusion, bf16[192,8192]{1,0:T(8,128)(2,1)S(1)} %copy-done.2, f32[8192]{0:T(1024)S(1)} %copy-done.6, f32[192]{0:T(256)S(1)} %add_rsqrt_fusion), kind=kOutput, calls=%fused_computation.32 | convolution fusion | flops 207642624 | bytes 4252608 | tf_op jit(solution)/shard_map/ly,mxy->lmx/dot_general | solution.py:131
  64.7 0.3 collective-permute-start
  65.0 1.3 collective-permute-start.1
  66.3 0.3 collective-permute-start.2
  66.6 5.2 %fusion.61 = f32[192,512]{1,0:T(8,128)S(1)} fusion(bf16[8192,512]{1,0:T(8,128)(2,1)} %param.15, bf16[192,8192]{1,0:T(8,128)(2,1)S(1)} %copy-done.2, f32[8192]{0:T(1024)S(1)} %copy-done.6, f32[192]{0:T(256)S(1)} %add_rsqrt_fusion), kind=kOutput, calls=%fused_computation.134 | convolution fusion | flops 1616904192 | bytes 11961088 | tf_op jit(solution)/shard_map/dot_general | solution.py:151
  71.9 0.2 collective-permute-start.3
  72.1 1.9 collective-permute-start.4
  74.0 2.4 %collective-permute-start.5 = (bf16[192,64]{0,1:T(8,128)(2,1)S(1)}, bf16[192,64]{0,1:T(8,128)(2,1)S(1)}, u32[]{:S(2)}, u32[]{:S(2)}) collective-permute-start(bf16[192,64]{0,1:T(8,128)(2,1)S(1)} %add_add_fusion.1), channel_id=1, source_target_pairs={{0,12},{1,13},{2,14},{3,15},{4,8},{5,9},{6,10},{7,11},{8,4},{9,5},... | collective-permute-start | bytes 73736 | tf_op jit(solution)/shard_map/ppermute | solution.py:97
  76.4 1.1 fusion.58
  77.6 2.2 collective-permute-done.5
  79.7 0.4 fusion.12
  80.1 0.8 pad_maximum_fusion.values_ref
  81.0 2.4 %shard_map.127 = bf16[192,640]{1,0:T(8,128)(2,1)} custom-call(f32[192,640]{1,0:T(8,128)} %pad_maximum_fusion.values_ref, f32[192,640]{1,0:T(8,128)} %get-tuple-element.15.cos_ref, f32[192,640]{1,0:T(8,128)} %get-tuple-element.14.sine_ref), custom_call_target="tpu_custom_call" | custom-call | tf_op jit(solution)/shard_map/pallas_call | solution.py:61
  83.4 1.1 reshape.389
  84.4 1.9 gather_fusion
  86.3 1.7 reshape.390
  88.1 4.5 %all-to-all-start = ((bf16[16,16,1920]{2,1,0:T(8,128)(2,1)}), bf16[16,16,1920]{2,1,0:T(8,128)(2,1)S(1)}, u32[]{:S(2)}, u32[]{:S(2)}) async-start(bf16[16,16,1920]{2,1,0:T(8,128)(2,1)} %reshape.390), calls=%async_computation | async-start | bytes 1966080 | tf_op jit(solution)/shard_map/all_to_all | solution.py:191
  92.6 12.3 %copy.73 = bf16[16,128,2048]{1,2,0:T(8,128)(2,1)} copy(bf16[16,128,2048]{2,1,0:T(8,128)(2,1)} %param.20) | data formatting | bytes 16777216 | tf_op args[7]
  104.9 0.2 compare_reduce_fusion
  105.2 0.2 fusion.40
  105.6 8.8 %all-to-all-done = bf16[16,16,1920]{2,1,0:T(8,128)(2,1)S(1)} async-done(((bf16[16,16,1920]{2,1,0:T(8,128)(2,1)}), bf16[16,16,1920]{2,1,0:T(8,128)(2,1)S(1)}, u32[]{:S(2)}, u32[]{:S(2)}) %all-to-all-start) | async-done | bytes 983072 | tf_op jit(solution)/shard_map/all_to_all | solution.py:191
  114.4 0.3 reshape.391
  114.7 0.4 slice.64
  115.2 0.6 copy.71
  115.8 0.5 reshape_reshape.10
  116.3 0.2 copy.126
  116.5 3.5 %fusion.64 = (f32[16,8,24]{2,1,0:T(8,128)S(1)}, f32[16,8,24,128]{3,2,1,0:T(8,128)S(1)}) fusion(bf16[16,128,2,8,128]{1,4,3,2,0:T(8,128)(2,1)} %bitcast.99, pred[16,128]{1,0:T(8,128)(4,1)S(1)} %fusion.41, bf16[16,3,8,8,128]{4,3,2,1,0:T(8,128)(2,1)S(1)} %reshape_reshape.10), kind=kOutput, calls=%fused_computation.136 | convolution fusion | flops 101839872 | bytes 6567936 | tf_op jit(solution)/shard_map/skqd,spkd->skqp/dot_general | solution.py:229
  120.0 0.5 fusion.65
  120.7 0.3 fusion.31
  120.9 0.9 fusion.10
  122.1 0.7 gather_fusion.1
  122.8 0.2 copy.91
  123.0 0.7 gather_fusion.2
  123.7 0.2 copy.92
  123.9 0.6 fusion.33
  124.5 4.5 %fusion.9 = bf16[16,8,3,8,128]{4,3,2,1,0:T(8,128)(2,1)S(1)} fusion(f32[16,8,24,128]{3,2,1,0:T(8,128)S(1)} %fusion.33, bf16[16,128,2,8,128]{1,4,3,2,0:T(8,128)(2,1)} %bitcast.100, f32[16,8,24,128]{3,2,1,0:T(8,128)S(1)} %get-tuple-element.17, f32[16,8,24]{2,1,0:T(8,128)S(1)} %max.17, pred[16,128]{1,0:T(8,128)(4,1)S(1)} %fusion.41), kind=kOutput, calls=%fused_computation.23 | convolution fusion | flops 102629376 | bytes 8140800 | tf_op jit(solution)/shard_map/skqp,spkd->skqd/dot_general | solution.py:245
  129.0 0.2 copy.125
  129.3 0.5 convert_element_type.82
  129.7 0.7 copy.80
  130.4 1.1 convert_element_type.84
  131.7 1.1 concatenate.32
  132.7 6.5 %all-to-all-start.1 = ((bf16[16,16,1608]{2,1,0:T(8,128)(2,1)}), bf16[16,16,1608]{2,1,0:T(8,128)(2,1)S(1)}, u32[]{:S(2)}, u32[]{:S(2)}) async-start(bf16[16,16,1608]{2,1,0:T(8,128)(2,1)} %concatenate.32), calls=%async_computation.1 | async-start | bytes 1703936 | tf_op jit(solution)/shard_map/all_to_all | solution.py:281
  139.3 1.7 scatter_custom_fusion.1
  141.1 18.0 %all-to-all-done.1 = bf16[16,16,1608]{2,1,0:T(8,128)(2,1)S(1)} async-done(((bf16[16,16,1608]{2,1,0:T(8,128)(2,1)}), bf16[16,16,1608]{2,1,0:T(8,128)(2,1)S(1)}, u32[]{:S(2)}, u32[]{:S(2)}) %all-to-all-start.1) | async-done | bytes 823328 | tf_op jit(solution)/shard_map/all_to_all | solution.py:281
  159.3 0.2 select_reduce_fusion
  159.6 0.7 gather_fusion.3
  160.7 1.6 copy.96
  162.3 1.6 convert_multiply_fusion.2
  163.9 0.7 fusion.5
  164.9 0.3 broadcast_in_dim.240
  165.1 0.7 fusion.28
  165.9 48.5 %all-gather.5.cloned.1.call-done = bf16[192,8192]{1,0:T(8,128)(2,1)} async-done(((bf16[192,512]{1,0:T(8,128)(2,1)}), bf16[192,8192]{1,0:T(8,128)(2,1)}) %all-gather.5.cloned.1.call-update) | async-done | bytes 3145744 | tf_op jit(solution)/shard_map/all_gather | solution.py:307
  214.4 6.9 %convolution_convert_fusion = bf16[192,512]{1,0:T(8,128)(2,1)} fusion(bf16[192,8192]{1,0:T(8,128)(2,1)} %all-gather.5.cloned.1.call-done, bf16[8192,512]{1,0:T(8,128)(2,1)} %param.17), kind=kOutput, calls=%fused_computation.28 | convolution fusion | flops 1610711040 | bytes 11730944 | tf_op jit(solution)/shard_map/dot_general | solution.py:308
  (75 shorter events, 2.4 us)
Async XLA Ops:
  6.5 69.9 %copy-start = (bf16[8192,128]{1,0:T(8,128)(2,1)S(1)}, bf16[8192,128]{1,0:T(8,128)(2,1)}, u32[]{:S(2)}) copy-start(bf16[8192,128]{1,0:T(8,128)(2,1)} %param.16) | copy-start | bytes 6291460
  6.5 55.7 %copy-start.6 = (f32[8192]{0:T(1024)S(1)}, f32[8192]{0:T(1024)}, u32[]{:S(2)}) copy-start(f32[8192]{0:T(1024)} %param.14) | copy-start | bytes 98308
  6.5 52.9 %all-gather.3.cloned.1.call-start = ((), (), s32[]{:S(2)}) async-start(), calls=%async_computation.2 | async-start | bytes 3342336 | tf_op jit(solution)/shard_map/all_gather | solution.py:119
  59.5 2.8 %copy-start.2 = (bf16[192,8192]{1,0:T(8,128)(2,1)S(1)}, bf16[192,8192]{1,0:T(8,128)(2,1)}, u32[]{:S(2)}) copy-start(bf16[192,8192]{1,0:T(8,128)(2,1)} %all-gather.3.cloned.1.call-done) | copy-start | bytes 9437188
  64.7 7.2 %collective-permute-start = (bf16[192,64]{0,1:T(8,128)(2,1)S(1)}, bf16[192,64]{0,1:T(8,128)(2,1)S(1)}, u32[]{:S(2)}, u32[]{:S(2)}) collective-permute-start(bf16[192,64]{0,1:T(8,128)(2,1)S(1)} %fusion.14), channel_id=1, source_target_pairs={{0,1},{1,0},{2,3},{3,2},{4,5},{5,4},{6,7},{7,6},{8,9},{9,8},{10,11... | collective-permute-start | bytes 73736 | tf_op jit(solution)/shard_map/ppermute | solution.py:97
  65.0 6.8 %collective-permute-start.1 = (bf16[192,64]{0,1:T(8,128)(2,1)S(1)}, bf16[192,64]{0,1:T(8,128)(2,1)S(1)}, u32[]{:S(2)}, u32[]{:S(2)}) collective-permute-start(bf16[192,64]{0,1:T(8,128)(2,1)S(1)} %fusion.14), channel_id=1, source_target_pairs={{0,2},{1,3},{2,0},{3,1},{4,6},{5,7},{6,4},{7,5},{8,10},{9,11},{10,... | collective-permute-start | bytes 73736 | tf_op jit(solution)/shard_map/ppermute | solution.py:97
  66.3 5.6 %collective-permute-start.2 = (bf16[192,64]{0,1:T(8,128)(2,1)S(1)}, bf16[192,64]{0,1:T(8,128)(2,1)S(1)}, u32[]{:S(2)}, u32[]{:S(2)}) collective-permute-start(bf16[192,64]{0,1:T(8,128)(2,1)S(1)} %fusion.14), channel_id=1, source_target_pairs={{0,3},{1,2},{2,1},{3,0},{4,7},{5,6},{6,5},{7,4},{8,11},{9,10},{10,... | collective-permute-start | bytes 73736 | tf_op jit(solution)/shard_map/ppermute | solution.py:97
  71.9 7.8 %copy-start.5 = (bf16[16,64,512]{2,1,0:T(8,128)(2,1)S(1)}, bf16[16,64,512]{2,1,0:T(8,128)(2,1)}, u32[]{:S(2)}) copy-start(bf16[16,64,512]{2,1,0:T(8,128)(2,1)} %param.19) | copy-start | bytes 3145732
  71.9 5.6 %collective-permute-start.3 = (bf16[192,64]{0,1:T(8,128)(2,1)S(1)}, bf16[192,64]{0,1:T(8,128)(2,1)S(1)}, u32[]{:S(2)}, u32[]{:S(2)}) collective-permute-start(bf16[192,64]{0,1:T(8,128)(2,1)S(1)} %add_add_fusion.1), channel_id=1, source_target_pairs={{0,4},{1,5},{2,6},{3,7},{4,0},{5,1},{6,2},{7,3},{8,12},{9,13},{10,... | collective-permute-start | bytes 73736 | tf_op jit(solution)/shard_map/ppermute | solution.py:97
  72.1 5.4 %collective-permute-start.4 = (bf16[192,64]{0,1:T(8,128)(2,1)S(1)}, bf16[192,64]{0,1:T(8,128)(2,1)S(1)}, u32[]{:S(2)}, u32[]{:S(2)}) collective-permute-start(bf16[192,64]{0,1:T(8,128)(2,1)S(1)} %add_add_fusion.1), channel_id=1, source_target_pairs={{0,8},{1,9},{2,10},{3,11},{4,12},{5,13},{6,14},{7,15},{8,0},{9,1},... | collective-permute-start | bytes 73736 | tf_op jit(solution)/shard_map/ppermute | solution.py:97
  74.0 5.7 %collective-permute-start.5 = (bf16[192,64]{0,1:T(8,128)(2,1)S(1)}, bf16[192,64]{0,1:T(8,128)(2,1)S(1)}, u32[]{:S(2)}, u32[]{:S(2)}) collective-permute-start(bf16[192,64]{0,1:T(8,128)(2,1)S(1)} %add_add_fusion.1), channel_id=1, source_target_pairs={{0,12},{1,13},{2,14},{3,15},{4,8},{5,9},{6,10},{7,11},{8,4},{9,5},... | collective-permute-start | bytes 73736 | tf_op jit(solution)/shard_map/ppermute | solution.py:97
  88.1 26.4 %all-to-all-start = ((bf16[16,16,1920]{2,1,0:T(8,128)(2,1)}), bf16[16,16,1920]{2,1,0:T(8,128)(2,1)S(1)}, u32[]{:S(2)}, u32[]{:S(2)}) async-start(bf16[16,16,1920]{2,1,0:T(8,128)(2,1)} %reshape.390), calls=%async_computation | async-start | bytes 1966080 | tf_op jit(solution)/shard_map/all_to_all | solution.py:191
  92.6 12.3 %copy-start.3 = (s32[64,4]{0,1:T(4,128)S(1)}, s32[64,4]{0,1:T(4,128)}, u32[]{:S(2)}) copy-start(s32[64,4]{0,1:T(4,128)} %param.24) | copy-start | bytes 3076
  92.6 12.5 %copy-start.4 = (s32[64]{0:T(128)S(1)}, s32[64]{0:T(128)}, u32[]{:S(2)}) copy-start(s32[64]{0:T(128)} %param.23) | copy-start | bytes 772
  132.7 26.3 %all-to-all-start.1 = ((bf16[16,16,1608]{2,1,0:T(8,128)(2,1)}), bf16[16,16,1608]{2,1,0:T(8,128)(2,1)S(1)}, u32[]{:S(2)}, u32[]{:S(2)}) async-start(bf16[16,16,1608]{2,1,0:T(8,128)(2,1)} %concatenate.32), calls=%async_computation.1 | async-start | bytes 1703936 | tf_op jit(solution)/shard_map/all_to_all | solution.py:281
  139.3 75.1 %all-gather.5.cloned.1.call-start = ((), (), s32[]{:S(2)}) async-start(), calls=%async_computation.3 | async-start | bytes 3342336 | tf_op jit(solution)/shard_map/all_gather | solution.py:307
  214.4 6.9 %copy-start.1 = (bf16[8192,128]{1,0:T(8,128)(2,1)S(1)}, bf16[8192,128]{1,0:T(8,128)(2,1)}, u32[]{:S(2)}) copy-start(bf16[8192,128]{1,0:T(8,128)(2,1)} %param.16) | copy-start | bytes 6291460
Sparse Core Ops, SparseCore 0:
  9.5 49.8 all-gather.2
  166.0 48.3 all-gather.4

commit v8 on v6

--- a/solution.py
+++ b/solution.py
@@ -35,8 +35,8 @@
     return jnp.where((columns < rot_limit)[None, :], turned, values)
 
 
-def rotation_kernel(values_ref, cos_ref, sine_ref, out_ref):
-    values = values_ref[...]
+def rotation_kernel(base_ref, addend_ref, cos_ref, sine_ref, out_ref):
+    values = base_ref[...] + addend_ref[...]
     width = values.shape[1]
     following = pltpu.roll(values, width - 1, 1)
     preceding = pltpu.roll(values, 1, 1)
@@ -48,7 +48,7 @@
     ).astype(out_ref.dtype)
 
 
-def rotate_columns(values, token_positions, global_cols, rot_limit):
+def rotate_columns(values, addend, token_positions, global_cols, rot_limit):
     pair_index = (global_cols % HEAD_WIDTH // 2).astype(jnp.float32)
     inverse = jnp.exp(pair_index * (-2.0 * math.log(theta_base) / HEAD_WIDTH))
     angles = token_positions[:, None] * inverse[None, :]
@@ -57,7 +57,7 @@
     sine_val = jnp.where(rotated, jnp.sin(angles), 0.0)
     width = values.shape[1]
     pad = -(-width // 128) * 128 - width
-    operands = [jnp.pad(a, ((0, 0), (0, pad))) for a in (values, cos_val, sine_val)]
+    operands = [jnp.pad(a, ((0, 0), (0, pad))) for a in (values, addend, cos_val, sine_val)]
     out = pl.pallas_call(
         rotation_kernel,
         out_shape=jax.ShapeDtypeStruct(operands[0].shape, jnp.bfloat16),
@@ -148,12 +148,18 @@
     keyval_cols = key_value_weight.shape[1]
     both_parts = jnp.concatenate(
         [
-            jnp.dot(normalized_input, query_weight, preferred_element_type=jnp.float32)
-            + adapter_query_update,
+            jnp.dot(normalized_input, query_weight, preferred_element_type=jnp.float32),
             jnp.dot(normalized_input, key_value_weight, preferred_element_type=jnp.float32),
         ],
         axis=1,
     )
+    both_addends = jnp.concatenate(
+        [
+            adapter_query_update,
+            jnp.zeros((adapter_query_update.shape[0], keyval_cols), jnp.float32),
+        ],
+        axis=1,
+    )
     global_cols = jnp.concatenate(
         [
             own_index * query_cols + jnp.arange(query_cols, dtype=jnp.int32),
@@ -166,7 +172,7 @@
             jnp.full((keyval_cols,), KEY_VALUE_HEADS * HEAD_WIDTH, jnp.int32),
         ]
     )
-    rotated_parts = rotate_columns(both_parts, token_positions, global_cols, limits)
+    rotated_parts = rotate_columns(both_parts, both_addends, token_positions, global_cols, limits)
     device_count = lax.axis_size("blk")
     request_page_count = key_value_page_pool.shape[0]
     table_width = request_page_tables.shape[1]

time: 254 us -> 255 us (level)
  transfers between devices with their start and end apart: 10 -> 10, of which waited for: 5 -> 5; matrix products, arithmetic and copies ran while one was open for 11% -> 12% of each run, Pallas kernels for 0% -> 0%
where the time goes in v8:
time: 255 us; the launch traced here: 254 us
  waiting for transfers between devices  141 us (55%)
  local copies, waits for them, and re-layouts  40.3 us (16%)
  matrix products  25.6 us (10%)
  starting transfers between devices  17.4 us (7%)
  between operations  13.9 us (5%)
  other arithmetic  13.2 us (5%)
  Pallas kernels  2.56 us (1%)
    all_gather x1, waiting for transfers between devices, local(): attended = lax.all_gather(attended_own, 'blk', axis=1, tiled=True)  52.3 us
    all_gather x1, waiting for transfers between devices, local(): gathered = lax.all_gather(layer_input_tokens, 'blk', axis=1, tiled=True)  44.3 us
    all_to_all x1, waiting for transfers between devices, local(): lax.all_to_all(packed, 'blk', 0, 0, tiled=True).reshape(group_pages, -1)  32.5 us
    unnamed x18, local copies, waits for them, and re-layouts  13.6 us
    all_to_all x1, waiting for transfers between devices, local(): lax.all_to_all(outgoing, 'blk', 0, 0, tiled=True)  8.83 us
    dot_general x1, matrix products, local(): jnp.dot(attended, output_weight, preferred_element_type=jnp.float32)  6.94 us
    all_to_all x1, starting transfers between devices, local(): lax.all_to_all(packed, 'blk', 0, 0, tiled=True).reshape(group_pages, -1)  6.53 us
    ppermute x6, starting transfers between devices, butterfly(): lax.ppermute(value, 'blk', [(i, i ^ m) for i in range(size)])  6.38 us
  transfers between devices with their start and end apart: 10, of which 5 were waited for; matrix products, arithmetic and copies ran while one was open for 12% of the time, Pallas kernels for 0%

profile of v8, /device:TPU:0, one launch (start us, length us, event | category | flops | bytes accessed | tf_op | source)
XLA Modules:
  0.0 254.2 jit_solution(3489233863698121969)
XLA Ops:
  6.5 0.7 all-gather.3.cloned.1.call-update
  7.3 0.8 select_reduce_fusion.1
  8.2 0.7 add_convert_fusion
  9.1 0.8 copy.70
  10.1 1.4 scatter_custom_fusion
  11.6 0.7 fusion.44
  12.3 2.8 %fusion.25 = (f32[192,640]{1,0:T(8,128)}, f32[192,640]{1,0:T(8,128)}) fusion(f32[640]{0:T(1024)S(1)} %fusion.43, f32[192]{0:T(256)S(1)} %convert_element_type.43, pred[640]{0:T(1024)(128)(4,1)S(1)} %fusion.44), kind=kLoop, calls=%fused_computation.46 | loop fusion | flops 368640 | bytes 987008 | tf_op jit(solution)/shard_map/jit(_where)/select_n | solution.py:57
  15.1 44.3 %all-gather.3.cloned.1.call-done = bf16[192,8192]{1,0:T(8,128)(2,1)} async-done(((bf16[192,512]{1,0:T(8,128)(2,1)}), bf16[192,8192]{1,0:T(8,128)(2,1)}) %all-gather.3.cloned.1.call-update) | async-done | bytes 3145744 | tf_op jit(solution)/shard_map/all_gather | solution.py:119
  59.5 2.8 %fusion = f32[192]{0:T(256)S(1)} fusion(bf16[192,8192]{1,0:T(8,128)(2,1)} %all-gather.3.cloned.1.call-done), kind=kLoop, calls=%fused_computation.8 | loop fusion | flops 4718400 | bytes 3146496 | tf_op jit(solution)/shard_map/reduce_sum | solution.py:70
  62.3 2.4 fusion.12
  64.7 0.3 collective-permute-start
  65.0 1.3 collective-permute-start.1
  66.3 0.3 collective-permute-start.2
  66.6 5.2 %fusion.58 = f32[192,512]{1,0:T(8,128)S(1)} fusion(bf16[8192,512]{1,0:T(8,128)(2,1)} %param.15, bf16[192,8192]{1,0:T(8,128)(2,1)S(1)} %copy-done.3, f32[8192]{0:T(1024)S(1)} %copy-done.7, f32[192]{0:T(256)S(1)} %add_rsqrt_fusion), kind=kOutput, calls=%fused_computation.125 | convolution fusion | flops 1616904192 | bytes 11961088 | tf_op jit(solution)/shard_map/dot_general | solution.py:151
  71.9 1.1 fusion.56
  73.1 0.2 collective-permute-start.3
  73.3 1.9 collective-permute-start.4
  75.1 2.4 collective-permute-start.5
  77.5 0.8 pad_maximum_fusion.base_ref
  78.4 2.5 collective-permute-done.5
  80.9 0.4 convolution_bitcast_fusion
  81.3 0.8 concatenate.30.addend_ref
  82.1 2.6 %shard_map.127 = bf16[192,640]{1,0:T(8,128)(2,1)} custom-call(f32[192,640]{1,0:T(8,128)} %pad_maximum_fusion.base_ref, f32[192,640]{1,0:T(8,128)} %concatenate.30.addend_ref, f32[192,640]{1,0:T(8,128)} %get-tuple-element.12.cos_ref, f32[192,640]{1,0:T(8,128)} %get-tuple-element.11.sine_ref), custom_call_target="tpu_custom_call" | custom-call | tf_op jit(solution)/shard_map/pallas_call | solution.py:61
  84.7 1.1 reshape.388
  85.7 1.9 gather_fusion
  87.7 1.7 reshape.389
  89.4 4.5 %all-to-all-start = ((bf16[16,16,1920]{2,1,0:T(8,128)(2,1)}), bf16[16,16,1920]{2,1,0:T(8,128)(2,1)S(1)}, u32[]{:S(2)}, u32[]{:S(2)}) async-start(bf16[16,16,1920]{2,1,0:T(8,128)(2,1)} %reshape.389), calls=%async_computation | async-start | bytes 1966080 | tf_op jit(solution)/shard_map/all_to_all | solution.py:197
  93.9 12.3 %copy.73 = bf16[16,128,2048]{1,2,0:T(8,128)(2,1)} copy(bf16[16,128,2048]{2,1,0:T(8,128)(2,1)} %param.20) | data formatting | bytes 16777216 | tf_op args[7]
  106.2 0.2 compare_reduce_fusion
  106.5 0.2 fusion.37
  106.9 8.8 %all-to-all-done = bf16[16,16,1920]{2,1,0:T(8,128)(2,1)S(1)} async-done(((bf16[16,16,1920]{2,1,0:T(8,128)(2,1)}), bf16[16,16,1920]{2,1,0:T(8,128)(2,1)S(1)}, u32[]{:S(2)}, u32[]{:S(2)}) %all-to-all-start) | async-done | bytes 983072 | tf_op jit(solution)/shard_map/all_to_all | solution.py:197
  115.7 0.3 reshape.390
  116.0 0.4 slice.52
  116.5 0.6 copy.71
  117.1 0.5 reshape_reshape.12
  117.8 3.5 %fusion.61 = (f32[16,8,24]{2,1,0:T(8,128)S(1)}, f32[16,8,24,128]{3,2,1,0:T(8,128)S(1)}) fusion(bf16[16,128,2,8,128]{1,4,3,2,0:T(8,128)(2,1)} %bitcast.95, pred[16,128]{1,0:T(8,128)(4,1)S(1)} %fusion.38, bf16[16,3,8,8,128]{4,3,2,1,0:T(8,128)(2,1)S(1)} %reshape_reshape.12), kind=kOutput, calls=%fused_computation.127 | convolution fusion | flops 101839872 | bytes 6567936 | tf_op jit(solution)/shard_map/skqd,spkd->skqp/dot_general | solution.py:235
  121.3 0.5 fusion.62
  122.0 0.3 fusion.29
  122.2 0.9 fusion.9
  123.4 0.7 gather_fusion.1
  124.1 0.2 copy.91
  124.2 0.6 fusion.31
  124.9 4.1 %add_bitcast_fusion = f32[16,8,3,8,128]{4,3,2,1,0:T(8,128)S(1)} fusion(f32[16,8,24,128]{3,2,1,0:T(8,128)S(1)} %fusion.31, bf16[16,128,2,8,128]{1,4,3,2,0:T(8,128)(2,1)} %bitcast.96, f32[16,8,24,128]{3,2,1,0:T(8,128)S(1)} %get-tuple-element.14, f32[16,8,24]{2,1,0:T(8,128)S(1)} %max.17, pred[16,128]{1,0:T(8,128)(4,1)S(1)} %fusion.38), kind=kOutput, calls=%fused_computation.21 | convolution fusion | flops 102236160 | bytes 8927232 | tf_op jit(solution)/shard_map/skqp,spkd->skqd/dot_general | solution.py:251
  129.0 0.2 copy.125
  129.2 1.4 reshape_reshape.13
  130.6 2.5 copy.80
  133.1 2.1 reshape.395
  135.3 0.7 gather_fusion.2
  135.9 0.2 copy.92
  136.1 0.5 copy-done.2
  136.6 1.4 concatenate.32
  138.0 6.5 %all-to-all-start.1 = ((f32[16,16,1560]{2,1,0:T(8,128)}), f32[16,16,1560]{2,1,0:T(8,128)S(1)}, u32[]{:S(2)}, u32[]{:S(2)}) async-start(f32[16,16,1560]{2,1,0:T(8,128)} %concatenate.32), calls=%async_computation.1 | async-start | bytes 3407872 | tf_op jit(solution)/shard_map/all_to_all | solution.py:281
  144.6 1.7 scatter_custom_fusion.1
  146.3 32.5 %all-to-all-done.1 = f32[16,16,1560]{2,1,0:T(8,128)S(1)} async-done(((f32[16,16,1560]{2,1,0:T(8,128)}), f32[16,16,1560]{2,1,0:T(8,128)S(1)}, u32[]{:S(2)}, u32[]{:S(2)}) %all-to-all-start.1) | async-done | bytes 1597472 | tf_op jit(solution)/shard_map/all_to_all | solution.py:281
  179.0 0.2 select_reduce_fusion
  179.2 0.7 gather_fusion.3
  180.2 1.3 broadcast_in_dim.240
  181.5 3.0 %copy.96 = f32[256,1536]{1,0:T(8,128)} copy(f32[256,1536]{0,1:T(8,128)} %bitcast.102) | data formatting | bytes 3145728 | tf_op jit(solution)/shard_map/reshape | solution.py:292
  184.5 1.6 slice_multiply_fusion
  186.1 0.7 fusion.5
  187.0 0.3 broadcast_in_dim.241
  187.3 0.7 fusion.26
  188.1 52.3 %all-gather.5.cloned.1.call-done = bf16[192,8192]{1,0:T(8,128)(2,1)} async-done(((bf16[192,512]{1,0:T(8,128)(2,1)}), bf16[192,8192]{1,0:T(8,128)(2,1)}) %all-gather.5.cloned.1.call-update) | async-done | bytes 3145744 | tf_op jit(solution)/shard_map/all_gather | solution.py:300
  240.4 6.9 %convolution_convert_fusion = bf16[192,512]{1,0:T(8,128)(2,1)} fusion(bf16[192,8192]{1,0:T(8,128)(2,1)} %all-gather.5.cloned.1.call-done, bf16[8192,512]{1,0:T(8,128)(2,1)} %param.17), kind=kOutput, calls=%fused_computation.27 | convolution fusion | flops 1610711040 | bytes 11730944 | tf_op jit(solution)/shard_map/dot_general | solution.py:301
  (76 shorter events, 2.5 us)
Async XLA Ops:
  6.5 65.3 %copy-start = (bf16[8192,128]{1,0:T(8,128)(2,1)S(1)}, bf16[8192,128]{1,0:T(8,128)(2,1)}, u32[]{:S(2)}) copy-start(bf16[8192,128]{1,0:T(8,128)(2,1)} %param.16) | copy-start | bytes 6291460
  6.5 52.9 %all-gather.3.cloned.1.call-start = ((), (), s32[]{:S(2)}) async-start(), calls=%async_computation.2 | async-start | bytes 3342336 | tf_op jit(solution)/shard_map/all_gather | solution.py:119
  10.0 52.2 %copy-start.7 = (f32[8192]{0:T(1024)S(1)}, f32[8192]{0:T(1024)}, u32[]{:S(2)}) copy-start(f32[8192]{0:T(1024)} %param.14) | copy-start | bytes 98308
  59.5 2.8 %copy-start.3 = (bf16[192,8192]{1,0:T(8,128)(2,1)S(1)}, bf16[192,8192]{1,0:T(8,128)(2,1)}, u32[]{:S(2)}) copy-start(bf16[192,8192]{1,0:T(8,128)(2,1)} %all-gather.3.cloned.1.call-done) | copy-start | bytes 9437188
  64.7 8.3 %collective-permute-start = (bf16[192,64]{0,1:T(8,128)(2,1)S(1)}, bf16[192,64]{0,1:T(8,128)(2,1)S(1)}, u32[]{:S(2)}, u32[]{:S(2)}) collective-permute-start(bf16[192,64]{0,1:T(8,128)(2,1)S(1)} %fusion.12), channel_id=1, source_target_pairs={{0,1},{1,0},{2,3},{3,2},{4,5},{5,4},{6,7},{7,6},{8,9},{9,8},{10,11... | collective-permute-start | bytes 73736 | tf_op jit(solution)/shard_map/ppermute | solution.py:97
  65.0 8.0 %collective-permute-start.1 = (bf16[192,64]{0,1:T(8,128)(2,1)S(1)}, bf16[192,64]{0,1:T(8,128)(2,1)S(1)}, u32[]{:S(2)}, u32[]{:S(2)}) collective-permute-start(bf16[192,64]{0,1:T(8,128)(2,1)S(1)} %fusion.12), channel_id=1, source_target_pairs={{0,2},{1,3},{2,0},{3,1},{4,6},{5,7},{6,4},{7,5},{8,10},{9,11},{10,... | collective-permute-start | bytes 73736 | tf_op jit(solution)/shard_map/ppermute | solution.py:97
  66.3 6.7 %collective-permute-start.2 = (bf16[192,64]{0,1:T(8,128)(2,1)S(1)}, bf16[192,64]{0,1:T(8,128)(2,1)S(1)}, u32[]{:S(2)}, u32[]{:S(2)}) collective-permute-start(bf16[192,64]{0,1:T(8,128)(2,1)S(1)} %fusion.12), channel_id=1, source_target_pairs={{0,3},{1,2},{2,1},{3,0},{4,7},{5,6},{6,5},{7,4},{8,11},{9,10},{10,... | collective-permute-start | bytes 73736 | tf_op jit(solution)/shard_map/ppermute | solution.py:97
  71.9 9.0 %copy-start.6 = (bf16[16,64,512]{2,1,0:T(8,128)(2,1)S(1)}, bf16[16,64,512]{2,1,0:T(8,128)(2,1)}, u32[]{:S(2)}) copy-start(bf16[16,64,512]{2,1,0:T(8,128)(2,1)} %param.19) | copy-start | bytes 3145732
  73.1 5.3 %collective-permute-start.3 = (bf16[192,64]{0,1:T(8,128)(2,1)S(1)}, bf16[192,64]{0,1:T(8,128)(2,1)S(1)}, u32[]{:S(2)}, u32[]{:S(2)}) collective-permute-start(bf16[192,64]{0,1:T(8,128)(2,1)S(1)} %add_add_fusion.1), channel_id=1, source_target_pairs={{0,4},{1,5},{2,6},{3,7},{4,0},{5,1},{6,2},{7,3},{8,12},{9,13},{10,... | collective-permute-start | bytes 73736 | tf_op jit(solution)/shard_map/ppermute | solution.py:97
  73.3 5.1 %collective-permute-start.4 = (bf16[192,64]{0,1:T(8,128)(2,1)S(1)}, bf16[192,64]{0,1:T(8,128)(2,1)S(1)}, u32[]{:S(2)}, u32[]{:S(2)}) collective-permute-start(bf16[192,64]{0,1:T(8,128)(2,1)S(1)} %add_add_fusion.1), channel_id=1, source_target_pairs={{0,8},{1,9},{2,10},{3,11},{4,12},{5,13},{6,14},{7,15},{8,0},{9,1},... | collective-permute-start | bytes 73736 | tf_op jit(solution)/shard_map/ppermute | solution.py:97
  75.1 5.7 %collective-permute-start.5 = (bf16[192,64]{0,1:T(8,128)(2,1)S(1)}, bf16[192,64]{0,1:T(8,128)(2,1)S(1)}, u32[]{:S(2)}, u32[]{:S(2)}) collective-permute-start(bf16[192,64]{0,1:T(8,128)(2,1)S(1)} %add_add_fusion.1), channel_id=1, source_target_pairs={{0,12},{1,13},{2,14},{3,15},{4,8},{5,9},{6,10},{7,11},{8,4},{9,5},... | collective-permute-start | bytes 73736 | tf_op jit(solution)/shard_map/ppermute | solution.py:97
  89.4 26.4 %all-to-all-start = ((bf16[16,16,1920]{2,1,0:T(8,128)(2,1)}), bf16[16,16,1920]{2,1,0:T(8,128)(2,1)S(1)}, u32[]{:S(2)}, u32[]{:S(2)}) async-start(bf16[16,16,1920]{2,1,0:T(8,128)(2,1)} %reshape.389), calls=%async_computation | async-start | bytes 1966080 | tf_op jit(solution)/shard_map/all_to_all | solution.py:197
  93.9 12.3 %copy-start.4 = (s32[64,4]{0,1:T(4,128)S(1)}, s32[64,4]{0,1:T(4,128)}, u32[]{:S(2)}) copy-start(s32[64,4]{0,1:T(4,128)} %param.24) | copy-start | bytes 3076
  93.9 12.5 %copy-start.5 = (s32[64]{0:T(128)S(1)}, s32[64]{0:T(128)}, u32[]{:S(2)}) copy-start(s32[64]{0:T(128)} %param.23) | copy-start | bytes 772
  135.2 1.4 copy-start.2
  138.0 40.8 %all-to-all-start.1 = ((f32[16,16,1560]{2,1,0:T(8,128)}), f32[16,16,1560]{2,1,0:T(8,128)S(1)}, u32[]{:S(2)}, u32[]{:S(2)}) async-start(f32[16,16,1560]{2,1,0:T(8,128)} %concatenate.32), calls=%async_computation.1 | async-start | bytes 3407872 | tf_op jit(solution)/shard_map/all_to_all | solution.py:281
  144.5 95.8 %all-gather.5.cloned.1.call-start = ((), (), s32[]{:S(2)}) async-start(), calls=%async_computation.3 | async-start | bytes 3342336 | tf_op jit(solution)/shard_map/all_gather | solution.py:300
  240.4 6.9 %copy-start.1 = (bf16[8192,128]{1,0:T(8,128)(2,1)S(1)}, bf16[8192,128]{1,0:T(8,128)(2,1)}, u32[]{:S(2)}) copy-start(bf16[8192,128]{1,0:T(8,128)(2,1)} %param.16) | copy-start | bytes 6291460
Sparse Core Ops, SparseCore 0:
  9.5 49.8 all-gather.2
  188.2 52.1 all-gather.4

commit v9 on v8

--- a/solution.py
+++ b/solution.py
@@ -249,12 +249,12 @@
     weights = jnp.where(valid_full, jnp.exp(masked - page_peak[..., None]), 0.0)
     fresh_weights = jnp.where(fresh_valid, jnp.exp(fresh_masked - page_peak[..., None]), 0.0)
     page_num = jnp.einsum(
-        "skqp,spkd->skqd",
+        "skqp,spkd->ksqd",
         weights.astype(jnp.bfloat16),
         cache_pages[:, :, 1],
         preferred_element_type=jnp.float32,
     ) + jnp.einsum(
-        "skqj,sjkd->skqd",
+        "skqj,sjkd->ksqd",
         fresh_weights.astype(jnp.bfloat16),
         slot_fresh[:, :, 1],
         preferred_element_type=jnp.float32,
@@ -268,13 +268,21 @@
     head_pick = jnp.asarray(
         [[first + j for j in range(owner_heads)] for first in owner_first_head], jnp.int32
     )
-    slot_num = to_tokens(page_num).reshape(request_page_count, NEW_TOKENS, device_count, owner_cols)
+    owners_per_group = (query_group_width * HEAD_WIDTH) // owner_cols
+    num_part = (
+        page_num.reshape(
+            KEY_VALUE_HEADS, request_page_count, NEW_TOKENS, owners_per_group, owner_cols
+        )
+        .transpose(0, 3, 1, 2, 4)
+        .reshape(device_count, request_page_count, NEW_TOKENS * owner_cols)
+    )
     slot_den = to_tokens(page_den[..., None]).reshape(request_page_count, NEW_TOKENS, head_count)
     slot_peak = to_tokens(page_peak[..., None]).reshape(request_page_count, NEW_TOKENS, head_count)
     packed = jnp.concatenate(
-        [
+        [num_part]
+        + [
             part.transpose(2, 0, 1, 3).reshape(device_count, request_page_count, -1)
-            for part in (slot_num, slot_den[:, :, head_pick], slot_peak[:, :, head_pick])
+            for part in (slot_den[:, :, head_pick], slot_peak[:, :, head_pick])
         ],
         axis=2,
     )

time: 255 us -> 257 us (level)
  local copies, waits for them, and re-layouts: 40.3 us -> 52.8 us
  waiting for transfers between devices: 141 us -> 132 us
    all_to_all x1, waiting for transfers between devices: 8.83 us -> 0.01 us  [local(): lax.all_to_all(outgoing, 'blk', 0, 0, tiled=True)]
    reshape x1 -> x3, local copies, waits for them, and re-layouts: 0.19 us -> 6.97 us  [the longest x2 4.88 us: local(): page_num.reshape(KEY_VALUE_HEADS, request_page_count, NEW_TOKENS, owners_...]
    unnamed x18 -> x17, local copies, waits for them, and re-layouts: 13.6 us -> 19.6 us
    slice x1 -> x2, local copies, waits for them, and re-layouts: 0.04 us -> 4.77 us  [the longest x1 4.73 us: local(): cache_pages[:, :, 1]]
  transfers between devices with their start and end apart: 10 -> 10, of which waited for: 5 -> 5; matrix products, arithmetic and copies ran while one was open for 12% -> 16% of each run, Pallas kernels for 0% -> 0%
where the time goes in v9:
time: 257 us; the launch traced here: 256 us
  waiting for transfers between devices  132 us (51%)
  local copies, waits for them, and re-layouts  52.8 us (21%)
  matrix products  26 us (10%)
  starting transfers between devices  16.2 us (6%)
  between operations  13.9 us (5%)
  other arithmetic  13 us (5%)
    all_gather x1, waiting for transfers between devices, local(): attended = lax.all_gather(attended_own, 'blk', axis=1, tiled=True)  52.3 us
    all_gather x1, waiting for transfers between devices, local(): gathered = lax.all_gather(layer_input_tokens, 'blk', axis=1, tiled=True)  44.3 us
    all_to_all x1, waiting for transfers between devices, local(): lax.all_to_all(packed, 'blk', 0, 0, tiled=True).reshape(group_pages, -1)  32.5 us
    unnamed x17, local copies, waits for them, and re-layouts  19.6 us
    dot_general x1, matrix products, local(): jnp.dot(attended, output_weight, preferred_element_type=jnp.float32)  6.94 us
    ppermute x6, starting transfers between devices, butterfly(): lax.ppermute(value, 'blk', [(i, i ^ m) for i in range(size)])  6.41 us
    all_to_all x1, starting transfers between devices, local(): lax.all_to_all(packed, 'blk', 0, 0, tiled=True).reshape(group_pages, -1)  5.88 us
    dot_general x1, matrix products, local(): jnp.dot(normalized_input, query_weight, preferred_element_type=jnp.float32)  5.21 us
  transfers between devices with their start and end apart: 10, of which 5 were waited for; matrix products, arithmetic and copies ran while one was open for 16% of the time, Pallas kernels for 0%

profile of v9, /device:TPU:0, one launch (start us, length us, event | category | flops | bytes accessed | tf_op | source)
XLA Modules:
  0.0 256.2 jit_solution(4162871109729241181)
XLA Ops:
  6.5 0.7 all-gather.3.cloned.1.call-update
  7.3 0.8 select_reduce_fusion.1
  8.1 0.1 eq.92
  8.2 0.7 add_convert_fusion
  9.1 0.8 copy.104
  10.1 1.4 scatter_custom_fusion
  11.6 0.7 fusion.44
  12.3 2.8 %fusion.26 = (f32[192,640]{1,0:T(8,128)}, f32[192,640]{1,0:T(8,128)}) fusion(f32[640]{0:T(1024)S(1)} %fusion.43, f32[192]{0:T(256)S(1)} %convert_element_type.43, pred[640]{0:T(1024)(128)(4,1)S(1)} %fusion.44), kind=kLoop, calls=%fused_computation.43 | loop fusion | flops 368640 | bytes 987008 | tf_op jit(solution)/shard_map/jit(_where)/select_n | solution.py:57
  15.1 44.3 %all-gather.3.cloned.1.call-done = bf16[192,8192]{1,0:T(8,128)(2,1)} async-done(((bf16[192,512]{1,0:T(8,128)(2,1)}), bf16[192,8192]{1,0:T(8,128)(2,1)}) %all-gather.3.cloned.1.call-update) | async-done | bytes 3145744 | tf_op jit(solution)/shard_map/all_gather | solution.py:119
  59.5 2.8 %fusion = f32[192]{0:T(256)S(1)} fusion(bf16[192,8192]{1,0:T(8,128)(2,1)} %all-gather.3.cloned.1.call-done), kind=kLoop, calls=%fused_computation.8 | loop fusion | flops 4718400 | bytes 3146496 | tf_op jit(solution)/shard_map/reduce_sum | solution.py:70
  62.3 2.4 fusion.15
  64.7 1.2 collective-permute-start.2
  65.9 0.7 collective-permute-start.1
  66.7 5.2 %fusion.56 = f32[192,512]{1,0:T(8,128)S(1)} fusion(bf16[8192,512]{1,0:T(8,128)(2,1)} %param.15, bf16[192,8192]{1,0:T(8,128)(2,1)S(1)} %copy-done.2, f32[8192]{0:T(1024)S(1)} %copy-done.6, f32[192]{0:T(256)S(1)} %add_rsqrt_fusion), kind=kOutput, calls=%fused_computation.121 | convolution fusion | flops 1616904192 | bytes 11961088 | tf_op jit(solution)/shard_map/dot_general | solution.py:151
  71.9 1.1 fusion.54
  73.1 1.5 collective-permute-start.5
  74.6 0.1 collective-permute-start.4
  74.7 2.8 %collective-permute-start.3 = (bf16[192,64]{0,1:T(8,128)(2,1)S(1)}, bf16[192,64]{0,1:T(8,128)(2,1)S(1)}, u32[]{:S(2)}, u32[]{:S(2)}) collective-permute-start(bf16[192,64]{0,1:T(8,128)(2,1)S(1)} %add_add_fusion.1), channel_id=1, source_target_pairs={{0,4},{1,5},{2,6},{3,7},{4,0},{5,1},{6,2},{7,3},{8,12},{9,13},{10,... | collective-permute-start | bytes 73736 | tf_op jit(solution)/shard_map/ppermute | solution.py:97
  77.5 0.8 pad_maximum_fusion.base_ref
  78.4 0.9 collective-permute-done.5
  79.2 1.0 collective-permute-done.4
  80.2 0.4 convolution_bitcast_fusion
  80.6 0.8 concatenate.30.addend_ref
  81.4 2.6 shard_map.127
  84.0 1.1 reshape.388
  85.1 1.9 gather_fusion
  87.0 1.6 reshape.389
  88.6 3.8 %all-to-all-start = ((bf16[16,16,1920]{2,1,0:T(8,128)(2,1)}), bf16[16,16,1920]{2,1,0:T(8,128)(2,1)S(1)}, u32[]{:S(2)}, u32[]{:S(2)}) async-start(bf16[16,16,1920]{2,1,0:T(8,128)(2,1)} %reshape.389), calls=%async_computation | async-start | bytes 1966080 | tf_op jit(solution)/shard_map/all_to_all | solution.py:197
  92.5 12.3 %copy.107 = bf16[16,128,2048]{1,2,0:T(8,128)(2,1)} copy(bf16[16,128,2048]{2,1,0:T(8,128)(2,1)} %param.20) | data formatting | bytes 16777216 | tf_op args[7]
  104.8 4.7 %slice.56 = bf16[16,128,1,8,128]{1,4,3,2,0:T(8,128)(2,1)} slice(bf16[16,128,2,8,128]{1,4,3,2,0:T(8,128)(2,1)} %bitcast.89), slice={[0:16], [0:128], [1:2], [0:8], [0:128]} | slice | bytes 8388608 | tf_op jit(solution)/shard_map/slice | solution.py:254
  109.5 6.5 %copy.139 = bf16[16,128,1,8,128]{4,1,0,3,2:T(8,128)(2,1)} copy(bf16[16,128,1,8,128]{1,4,3,2,0:T(8,128)(2,1)} %slice.56) | data formatting | bytes 8388608
  116.0 0.2 compare_reduce_fusion.1
  116.3 0.2 fusion.37
  116.7 0.3 reshape.390
  117.2 0.4 slice.52
  117.6 0.6 copy.105
  118.1 0.2 copy.175
  118.3 0.5 reshape_reshape.9
  118.8 0.5 fusion.17
  119.3 3.5 %fusion.59 = (f32[16,8,24]{2,1,0:T(8,128)S(1)}, f32[16,8,24,128]{3,2,1,0:T(8,128)S(1)}) fusion(bf16[16,128,2,8,128]{1,4,3,2,0:T(8,128)(2,1)} %bitcast.90, pred[16,128]{1,0:T(8,128)(4,1)S(1)} %fusion.38, bf16[16,3,8,8,128]{4,3,2,1,0:T(8,128)(2,1)S(1)} %reshape_reshape.9), kind=kOutput, calls=%fused_computation.123 | convolution fusion | flops 101839872 | bytes 6567936 | tf_op jit(solution)/shard_map/skqd,spkd->skqp/dot_general | solution.py:235
  123.1 0.9 fusion.13
  124.3 0.7 gather_fusion.1
  125.0 0.2 copy.129
  125.2 0.7 gather_fusion.2
  125.9 0.2 copy.130
  126.1 0.6 fusion.33
  126.7 4.6 %fusion.10 = f32[8,16,24,128]{3,2,1,0:T(8,128)} fusion(f32[8,16,24,128]{3,2,1,0:T(8,128)S(1)} %fusion.33, bf16[16,128,1,8,128]{4,1,0,3,2:T(8,128)(2,1)} %copy.139, bf16[16,8,24,128]{3,2,1,0:T(8,128)(2,1)S(1)} %get-tuple-element.10), kind=kOutput, calls=%fused_computation.23 | convolution fusion | flops 101056512 | bytes 8126464 | tf_op jit(solution)/shard_map/skqp,spkd->ksqd/dot_general | solution.py:251
  131.3 2.9 %reshape.394 = f32[8,16,3,2,512]{4,3,2,1,0:T(2,128)} reshape(f32[8,16,24,128]{3,2,1,0:T(8,128)} %fusion.10) | data formatting | bytes 3145728 | tf_op jit(solution)/shard_map/reshape | solution.py:273
  134.2 2.0 copy.174
  136.1 2.1 reshape.395
  138.2 2.4 concatenate.32
  140.6 5.9 %all-to-all-start.1 = ((f32[16,16,1560]{2,1,0:T(8,128)}), f32[16,16,1560]{2,1,0:T(8,128)S(1)}, u32[]{:S(2)}, u32[]{:S(2)}) async-start(f32[16,16,1560]{2,1,0:T(8,128)} %concatenate.32), calls=%async_computation.1 | async-start | bytes 3407872 | tf_op jit(solution)/shard_map/all_to_all | solution.py:289
  146.6 1.7 scatter_custom_fusion.1
  148.3 32.5 %all-to-all-done.1 = f32[16,16,1560]{2,1,0:T(8,128)S(1)} async-done(((f32[16,16,1560]{2,1,0:T(8,128)}), f32[16,16,1560]{2,1,0:T(8,128)S(1)}, u32[]{:S(2)}, u32[]{:S(2)}) %all-to-all-start.1) | async-done | bytes 1597472 | tf_op jit(solution)/shard_map/all_to_all | solution.py:289
  181.0 0.2 select_reduce_fusion
  181.3 0.7 gather_fusion.3
  182.2 1.3 broadcast_in_dim.240
  183.5 3.0 %copy.134 = f32[256,1536]{1,0:T(8,128)} copy(f32[256,1536]{0,1:T(8,128)} %bitcast.95) | data formatting | bytes 3145728 | tf_op jit(solution)/shard_map/reshape | solution.py:300
  186.5 1.6 slice_multiply_fusion
  188.1 0.7 fusion.6
  189.1 0.3 broadcast_in_dim.241
  189.3 0.7 fusion.27
  190.1 52.3 %all-gather.5.cloned.1.call-done = bf16[192,8192]{1,0:T(8,128)(2,1)} async-done(((bf16[192,512]{1,0:T(8,128)(2,1)}), bf16[192,8192]{1,0:T(8,128)(2,1)}) %all-gather.5.cloned.1.call-update) | async-done | bytes 3145744 | tf_op jit(solution)/shard_map/all_gather | solution.py:308
  242.4 6.9 %convolution_convert_fusion = bf16[192,512]{1,0:T(8,128)(2,1)} fusion(bf16[192,8192]{1,0:T(8,128)(2,1)} %all-gather.5.cloned.1.call-done, bf16[8192,512]{1,0:T(8,128)(2,1)} %param.17), kind=kOutput, calls=%fused_computation.27 | convolution fusion | flops 1610711040 | bytes 11730944 | tf_op jit(solution)/shard_map/dot_general | solution.py:309
  (76 shorter events, 2.4 us)
Async XLA Ops:
  6.5 65.4 %copy-start = (bf16[8192,128]{1,0:T(8,128)(2,1)S(1)}, bf16[8192,128]{1,0:T(8,128)(2,1)}, u32[]{:S(2)}) copy-start(bf16[8192,128]{1,0:T(8,128)(2,1)} %param.16) | copy-start | bytes 6291460
  6.5 55.7 %copy-start.6 = (f32[8192]{0:T(1024)S(1)}, f32[8192]{0:T(1024)}, u32[]{:S(2)}) copy-start(f32[8192]{0:T(1024)} %param.14) | copy-start | bytes 98308
  6.5 52.9 %all-gather.3.cloned.1.call-start = ((), (), s32[]{:S(2)}) async-start(), calls=%async_computation.2 | async-start | bytes 3342336 | tf_op jit(solution)/shard_map/all_gather | solution.py:119
  59.5 2.8 %copy-start.2 = (bf16[192,8192]{1,0:T(8,128)(2,1)S(1)}, bf16[192,8192]{1,0:T(8,128)(2,1)}, u32[]{:S(2)}) copy-start(bf16[192,8192]{1,0:T(8,128)(2,1)} %all-gather.3.cloned.1.call-done) | copy-start | bytes 9437188
  64.7 8.3 %collective-permute-start.2 = (bf16[192,64]{0,1:T(8,128)(2,1)S(1)}, bf16[192,64]{0,1:T(8,128)(2,1)S(1)}, u32[]{:S(2)}, u32[]{:S(2)}) collective-permute-start(bf16[192,64]{0,1:T(8,128)(2,1)S(1)} %fusion.15), channel_id=1, source_target_pairs={{0,3},{1,2},{2,1},{3,0},{4,7},{5,6},{6,5},{7,4},{8,11},{9,10},{10,... | collective-permute-start | bytes 73736 | tf_op jit(solution)/shard_map/ppermute | solution.py:97
  65.9 7.1 %collective-permute-start.1 = (bf16[192,64]{0,1:T(8,128)(2,1)S(1)}, bf16[192,64]{0,1:T(8,128)(2,1)S(1)}, u32[]{:S(2)}, u32[]{:S(2)}) collective-permute-start(bf16[192,64]{0,1:T(8,128)(2,1)S(1)} %fusion.15), channel_id=1, source_target_pairs={{0,2},{1,3},{2,0},{3,1},{4,6},{5,7},{6,4},{7,5},{8,10},{9,11},{10,... | collective-permute-start | bytes 73736 | tf_op jit(solution)/shard_map/ppermute | solution.py:97
  66.7 6.4 %collective-permute-start = (bf16[192,64]{0,1:T(8,128)(2,1)S(1)}, bf16[192,64]{0,1:T(8,128)(2,1)S(1)}, u32[]{:S(2)}, u32[]{:S(2)}) collective-permute-start(bf16[192,64]{0,1:T(8,128)(2,1)S(1)} %fusion.15), channel_id=1, source_target_pairs={{0,1},{1,0},{2,3},{3,2},{4,5},{5,4},{6,7},{7,6},{8,9},{9,8},{10,11... | collective-permute-start | bytes 73736 | tf_op jit(solution)/shard_map/ppermute | solution.py:97
  71.9 8.3 %copy-start.5 = (bf16[16,64,512]{2,1,0:T(8,128)(2,1)S(1)}, bf16[16,64,512]{2,1,0:T(8,128)(2,1)}, u32[]{:S(2)}) copy-start(bf16[16,64,512]{2,1,0:T(8,128)(2,1)} %param.19) | copy-start | bytes 3145732
  73.1 6.1 %collective-permute-start.5 = (bf16[192,64]{0,1:T(8,128)(2,1)S(1)}, bf16[192,64]{0,1:T(8,128)(2,1)S(1)}, u32[]{:S(2)}, u32[]{:S(2)}) collective-permute-start(bf16[192,64]{0,1:T(8,128)(2,1)S(1)} %add_add_fusion.1), channel_id=1, source_target_pairs={{0,12},{1,13},{2,14},{3,15},{4,8},{5,9},{6,10},{7,11},{8,4},{9,5},... | collective-permute-start | bytes 73736 | tf_op jit(solution)/shard_map/ppermute | solution.py:97
  74.6 5.6 %collective-permute-start.4 = (bf16[192,64]{0,1:T(8,128)(2,1)S(1)}, bf16[192,64]{0,1:T(8,128)(2,1)S(1)}, u32[]{:S(2)}, u32[]{:S(2)}) collective-permute-start(bf16[192,64]{0,1:T(8,128)(2,1)S(1)} %add_add_fusion.1), channel_id=1, source_target_pairs={{0,8},{1,9},{2,10},{3,11},{4,12},{5,13},{6,14},{7,15},{8,0},{9,1},... | collective-permute-start | bytes 73736 | tf_op jit(solution)/shard_map/ppermute | solution.py:97
  74.7 5.4 %collective-permute-start.3 = (bf16[192,64]{0,1:T(8,128)(2,1)S(1)}, bf16[192,64]{0,1:T(8,128)(2,1)S(1)}, u32[]{:S(2)}, u32[]{:S(2)}) collective-permute-start(bf16[192,64]{0,1:T(8,128)(2,1)S(1)} %add_add_fusion.1), channel_id=1, source_target_pairs={{0,4},{1,5},{2,6},{3,7},{4,0},{5,1},{6,2},{7,3},{8,12},{9,13},{10,... | collective-permute-start | bytes 73736 | tf_op jit(solution)/shard_map/ppermute | solution.py:97
  88.6 28.1 %all-to-all-start = ((bf16[16,16,1920]{2,1,0:T(8,128)(2,1)}), bf16[16,16,1920]{2,1,0:T(8,128)(2,1)S(1)}, u32[]{:S(2)}, u32[]{:S(2)}) async-start(bf16[16,16,1920]{2,1,0:T(8,128)(2,1)} %reshape.389), calls=%async_computation | async-start | bytes 1966080 | tf_op jit(solution)/shard_map/all_to_all | solution.py:197
  109.5 6.5 %copy-start.3 = (s32[64,4]{0,1:T(4,128)S(1)}, s32[64,4]{0,1:T(4,128)}, u32[]{:S(2)}) copy-start(s32[64,4]{0,1:T(4,128)} %param.24) | copy-start | bytes 3076
  109.5 6.7 %copy-start.4 = (s32[64]{0:T(128)S(1)}, s32[64]{0:T(128)}, u32[]{:S(2)}) copy-start(s32[64]{0:T(128)} %param.23) | copy-start | bytes 772
  140.6 40.1 %all-to-all-start.1 = ((f32[16,16,1560]{2,1,0:T(8,128)}), f32[16,16,1560]{2,1,0:T(8,128)S(1)}, u32[]{:S(2)}, u32[]{:S(2)}) async-start(f32[16,16,1560]{2,1,0:T(8,128)} %concatenate.32), calls=%async_computation.1 | async-start | bytes 3407872 | tf_op jit(solution)/shard_map/all_to_all | solution.py:289
  146.5 95.8 %all-gather.5.cloned.1.call-start = ((), (), s32[]{:S(2)}) async-start(), calls=%async_computation.3 | async-start | bytes 3342336 | tf_op jit(solution)/shard_map/all_gather | solution.py:308
  242.4 6.9 %copy-start.1 = (bf16[8192,128]{1,0:T(8,128)(2,1)S(1)}, bf16[8192,128]{1,0:T(8,128)(2,1)}, u32[]{:S(2)}) copy-start(bf16[8192,128]{1,0:T(8,128)(2,1)} %param.16) | copy-start | bytes 6291460
Sparse Core Ops, SparseCore 0:
  9.5 49.8 all-gather.2
  190.2 52.1 all-gather.4

commit v10 on v6

--- a/solution.py
+++ b/solution.py
@@ -218,42 +218,6 @@
     cache_pages = key_value_page_pool.reshape(
         request_page_count, PAGE_LENGTH, 2, KEY_VALUE_HEADS, HEAD_WIDTH
     )
-    query_page = (
-        slot_queries.reshape(
-            request_page_count, NEW_TOKENS, KEY_VALUE_HEADS, query_group_width, HEAD_WIDTH
-        )
-        .transpose(0, 2, 1, 3, 4)
-        .reshape(request_page_count, KEY_VALUE_HEADS, query_feature_width, HEAD_WIDTH)
-    )
-    scores = (
-        jnp.einsum(
-            "skqd,spkd->skqp", query_page, cache_pages[:, :, 0], preferred_element_type=jnp.float32
-        )
-        * score_scale
-    )
-    fresh_scores = (
-        jnp.einsum(
-            "skqd,sjkd->skqj", query_page, slot_fresh[:, :, 0], preferred_element_type=jnp.float32
-        )
-        * score_scale
-    )
-    masked = jnp.where(valid_full, scores, neg_large)
-    fresh_masked = jnp.where(fresh_valid, fresh_scores, neg_large)
-    page_peak = jnp.maximum(jnp.max(masked, axis=-1), jnp.max(fresh_masked, axis=-1))
-    weights = jnp.where(valid_full, jnp.exp(masked - page_peak[..., None]), 0.0)
-    fresh_weights = jnp.where(fresh_valid, jnp.exp(fresh_masked - page_peak[..., None]), 0.0)
-    page_num = jnp.einsum(
-        "skqp,spkd->skqd",
-        weights.astype(jnp.bfloat16),
-        cache_pages[:, :, 1],
-        preferred_element_type=jnp.float32,
-    ) + jnp.einsum(
-        "skqj,sjkd->skqd",
-        fresh_weights.astype(jnp.bfloat16),
-        slot_fresh[:, :, 1],
-        preferred_element_type=jnp.float32,
-    )
-    page_den = jnp.sum(weights, axis=-1) + jnp.sum(fresh_weights, axis=-1)
     head_count = QUERY_HEADS
     owner_cols = query_cols
     owner_heads = max(1, owner_cols // HEAD_WIDTH)
@@ -262,17 +226,66 @@
     head_pick = jnp.asarray(
         [[first + j for j in range(owner_heads)] for first in owner_first_head], jnp.int32
     )
-    slot_num = to_tokens(page_num).reshape(request_page_count, NEW_TOKENS, device_count, owner_cols)
-    slot_den = to_tokens(page_den[..., None]).reshape(request_page_count, NEW_TOKENS, head_count)
-    slot_peak = to_tokens(page_peak[..., None]).reshape(request_page_count, NEW_TOKENS, head_count)
-    packed = jnp.concatenate(
-        [
-            part.transpose(2, 0, 1, 3).reshape(device_count, request_page_count, -1)
-            for part in (slot_num, slot_den[:, :, head_pick], slot_peak[:, :, head_pick])
-        ],
-        axis=2,
-    )
-    arrived = lax.all_to_all(packed, "blk", 0, 0, tiled=True).reshape(group_pages, -1)
+
+    def page_exchange(first, chunk_pages):
+        chunk_queries = slot_queries[first : first + chunk_pages]
+        chunk_cache = cache_pages[first : first + chunk_pages]
+        chunk_fresh = slot_fresh[first : first + chunk_pages]
+        chunk_valid = valid_full[first : first + chunk_pages]
+        chunk_fresh_valid = fresh_valid[first : first + chunk_pages]
+        query_page = (
+            chunk_queries.reshape(
+                chunk_pages, NEW_TOKENS, KEY_VALUE_HEADS, query_group_width, HEAD_WIDTH
+            )
+            .transpose(0, 2, 1, 3, 4)
+            .reshape(chunk_pages, KEY_VALUE_HEADS, query_feature_width, HEAD_WIDTH)
+        )
+        scores = (
+            jnp.einsum(
+                "skqd,spkd->skqp", query_page, chunk_cache[:, :, 0], preferred_element_type=jnp.float32
+            )
+            * score_scale
+        )
+        fresh_scores = (
+            jnp.einsum(
+                "skqd,sjkd->skqj", query_page, chunk_fresh[:, :, 0], preferred_element_type=jnp.float32
+            )
+            * score_scale
+        )
+        masked = jnp.where(chunk_valid, scores, neg_large)
+        fresh_masked = jnp.where(chunk_fresh_valid, fresh_scores, neg_large)
+        page_peak = jnp.maximum(jnp.max(masked, axis=-1), jnp.max(fresh_masked, axis=-1))
+        weights = jnp.where(chunk_valid, jnp.exp(masked - page_peak[..., None]), 0.0)
+        fresh_weights = jnp.where(chunk_fresh_valid, jnp.exp(fresh_masked - page_peak[..., None]), 0.0)
+        page_num = jnp.einsum(
+            "skqp,spkd->skqd",
+            weights.astype(jnp.bfloat16),
+            chunk_cache[:, :, 1],
+            preferred_element_type=jnp.float32,
+        ) + jnp.einsum(
+            "skqj,sjkd->skqd",
+            fresh_weights.astype(jnp.bfloat16),
+            chunk_fresh[:, :, 1],
+            preferred_element_type=jnp.float32,
+        )
+        page_den = jnp.sum(weights, axis=-1) + jnp.sum(fresh_weights, axis=-1)
+        slot_num = to_tokens(page_num).reshape(chunk_pages, NEW_TOKENS, device_count, owner_cols)
+        slot_den = to_tokens(page_den[..., None]).reshape(chunk_pages, NEW_TOKENS, head_count)
+        slot_peak = to_tokens(page_peak[..., None]).reshape(chunk_pages, NEW_TOKENS, head_count)
+        packed = jnp.concatenate(
+            [
+                part.transpose(2, 0, 1, 3).reshape(device_count, chunk_pages, -1)
+                for part in (slot_num, slot_den[:, :, head_pick], slot_peak[:, :, head_pick])
+            ],
+            axis=2,
+        )
+        return lax.all_to_all(packed, "blk", 0, 0, tiled=True)
+
+    half_pages = request_page_count // 2
+    arrived = jnp.concatenate(
+        [page_exchange(0, half_pages), page_exchange(half_pages, request_page_count - half_pages)],
+        axis=1,
+    ).reshape(group_pages, -1)
     num_width = NEW_TOKENS * owner_cols
     head_width = NEW_TOKENS * owner_heads
     arrived_num = arrived[:, :num_width]

time: 254 us -> 253 us (level)
  waiting for transfers between devices: 141 us -> 119 us
  local copies, waits for them, and re-layouts: 39.4 us -> 48.7 us
  starting transfers between devices: 17.4 us -> 22.7 us
  other arithmetic: 13.2 us -> 16.4 us
  matrix products: 25.6 us -> 28.7 us
    all_to_all x1 -> x2, waiting for transfers between devices: 32.5 us -> 22.9 us  [page_exchange(): return lax.all_to_all(packed, 'blk', 0, 0, tiled=True)]
    all_gather x1, waiting for transfers between devices: 44.3 us -> 37.3 us  [local(): gathered = lax.all_gather(layer_input_tokens, 'blk', axis=1, tiled=True)]
    slice x5 -> x9, local copies, waits for them, and re-layouts: 1.27 us -> 8.11 us  [the longest x1 6.13 us: page_exchange(): chunk_cache = cache_pages[first:first + chunk_pages]]
    all_to_all x1 -> x2, starting transfers between devices: 6.53 us -> 12.4 us  [page_exchange(): return lax.all_to_all(packed, 'blk', 0, 0, tiled=True)]
    all_gather x1, waiting for transfers between devices: 52.3 us -> 48.5 us  [local(): attended = lax.all_gather(attended_own, 'blk', axis=1, tiled=True)]
    dot_general x4 -> x8, matrix products: 8.78 us -> 11.9 us  [the longest x2 5.68 us: page_exchange(): jnp.einsum('skqp,spkd->skqd', weights.astype(jnp.bfloat16), chunk_cache[:...]
    unnamed x18 -> x23, local copies, waits for them, and re-layouts: 13.6 us -> 13.8 us
  transfers between devices with their start and end apart: 10 -> 11, of which waited for: 5 -> 7; matrix products, arithmetic and copies ran while one was open for 11% -> 20% of each run, Pallas kernels for 0% -> 0%
where the time goes in v10:
time: 253 us; the launch traced here: 252 us
  waiting for transfers between devices  119 us (47%)
  local copies, waits for them, and re-layouts  48.7 us (19%)
  matrix products  28.7 us (11%)
  starting transfers between devices  22.7 us (9%)
  other arithmetic  16.4 us (6%)
  between operations  14.1 us (6%)
    all_gather x1, waiting for transfers between devices, local(): attended = lax.all_gather(attended_own, 'blk', axis=1, tiled=True)  48.5 us
    all_gather x1, waiting for transfers between devices, local(): gathered = lax.all_gather(layer_input_tokens, 'blk', axis=1, tiled=True)  37.3 us
    all_to_all x2, waiting for transfers between devices, page_exchange(): return lax.all_to_all(packed, 'blk', 0, 0, tiled=True)  22.9 us
    unnamed x23, local copies, waits for them, and re-layouts  13.8 us
    all_to_all x2, starting transfers between devices, page_exchange(): return lax.all_to_all(packed, 'blk', 0, 0, tiled=True)  12.4 us
    all_to_all x1, waiting for transfers between devices, local(): lax.all_to_all(outgoing, 'blk', 0, 0, tiled=True)  8.26 us
    dot_general x1, matrix products, local(): jnp.dot(attended, output_weight, preferred_element_type=jnp.float32)  6.95 us
    ppermute x6, starting transfers between devices, butterfly(): lax.ppermute(value, 'blk', [(i, i ^ m) for i in range(size)])  6.41 us
  transfers between devices with their start and end apart: 11, of which 7 were waited for; matrix products, arithmetic and copies ran while one was open for 20% of the time, Pallas kernels for 0%

profile of v10, /device:TPU:0, one launch (start us, length us, event | category | flops | bytes accessed | tf_op | source)
XLA Modules:
  0.0 252.2 jit_solution(5994572856426024351)
XLA Ops:
  6.5 0.7 all-gather.3.cloned.1.call-update
  7.3 0.8 select_reduce_fusion.1
  8.2 0.7 add_convert_fusion
  9.1 0.8 copy.104
  10.1 1.4 scatter_custom_fusion
  11.6 0.9 compare_reduce_fusion
  12.5 0.7 fusion.73
  13.2 2.8 %fusion.31 = (f32[192,640]{1,0:T(8,128)}, f32[192,640]{1,0:T(8,128)}) fusion(f32[640]{0:T(1024)S(1)} %fusion.72, f32[192]{0:T(256)S(1)} %convert_element_type.49, pred[640]{0:T(1024)(128)(4,1)S(1)} %fusion.73), kind=kLoop, calls=%fused_computation.59 | loop fusion | flops 368640 | bytes 987008 | tf_op jit(solution)/shard_map/jit(_where)/select_n | solution.py:57
  16.0 6.1 %fusion.91 = (bf16[8,128,2048]{2,1,0:T(8,128)(2,1)}, bf16[8,128,2048]{2,1,0:T(8,128)(2,1)}) fusion(bf16[16,128,2048]{2,1,0:T(8,128)(2,1)} %param.20), kind=kLoop, calls=%fused_computation.165 | loop fusion | bytes 16777216 | tf_op jit(solution)/shard_map/slice | solution.py:232
  22.1 37.3 %all-gather.3.cloned.1.call-done = bf16[192,8192]{1,0:T(8,128)(2,1)} async-done(((bf16[192,512]{1,0:T(8,128)(2,1)}), bf16[192,8192]{1,0:T(8,128)(2,1)}) %all-gather.3.cloned.1.call-update) | async-done | bytes 3145744 | tf_op jit(solution)/shard_map/all_gather | solution.py:119
  59.5 2.8 %fusion = f32[192]{0:T(256)S(1)} fusion(bf16[192,8192]{1,0:T(8,128)(2,1)} %all-gather.3.cloned.1.call-done), kind=kLoop, calls=%fused_computation.10 | loop fusion | flops 4718400 | bytes 3146496 | tf_op jit(solution)/shard_map/reduce_sum | solution.py:70
  62.3 2.4 fusion.22
  64.7 1.2 collective-permute-start.2
  65.9 0.7 collective-permute-start.1
  66.7 5.2 %fusion.89 = f32[192,512]{1,0:T(8,128)S(1)} fusion(bf16[8192,512]{1,0:T(8,128)(2,1)} %param.15, bf16[192,8192]{1,0:T(8,128)(2,1)S(1)} %copy-done.2, f32[8192]{0:T(1024)S(1)} %copy-done.9, f32[192]{0:T(256)S(1)} %add_rsqrt_fusion), kind=kOutput, calls=%fused_computation.164 | convolution fusion | flops 1616904192 | bytes 11961088 | tf_op jit(solution)/shard_map/dot_general | solution.py:151
  72.0 1.5 collective-permute-start.5
  73.6 2.8 %collective-permute-start.3 = (bf16[192,64]{0,1:T(8,128)(2,1)S(1)}, bf16[192,64]{0,1:T(8,128)(2,1)S(1)}, u32[]{:S(2)}, u32[]{:S(2)}) collective-permute-start(bf16[192,64]{0,1:T(8,128)(2,1)S(1)} %add_add_fusion.1), channel_id=1, source_target_pairs={{0,4},{1,5},{2,6},{3,7},{4,0},{5,1},{6,2},{7,3},{8,12},{9,13},{10,... | collective-permute-start | bytes 73736 | tf_op jit(solution)/shard_map/ppermute | solution.py:97
  76.4 1.1 fusion.86
  77.6 0.5 collective-permute-done.5
  78.1 1.0 collective-permute-done.4
  79.5 0.9 pad_maximum_fusion.1.values_ref
  80.4 2.4 shard_map.127
  82.8 1.1 reshape.422
  83.9 1.9 gather_fusion
  85.8 1.7 reshape.423
  87.5 3.8 %all-to-all-start = ((bf16[16,16,1920]{2,1,0:T(8,128)(2,1)}), bf16[16,16,1920]{2,1,0:T(8,128)(2,1)S(1)}, u32[]{:S(2)}, u32[]{:S(2)}) async-start(bf16[16,16,1920]{2,1,0:T(8,128)(2,1)} %reshape.423), calls=%async_computation | async-start | bytes 1966080 | tf_op jit(solution)/shard_map/all_to_all | solution.py:191
  91.3 6.5 %copy.162 = bf16[8,128,2048]{1,2,0:T(8,128)(2,1)} copy(bf16[8,128,2048]{2,1,0:T(8,128)(2,1)} %get-tuple-element.10) | data formatting | bytes 8388608
  97.8 6.5 %copy.157 = bf16[8,128,2048]{1,2,0:T(8,128)(2,1)} copy(bf16[8,128,2048]{2,1,0:T(8,128)(2,1)} %get-tuple-element.9) | data formatting | bytes 8388608
  104.8 8.3 %all-to-all-done = bf16[16,16,1920]{2,1,0:T(8,128)(2,1)S(1)} async-done(((bf16[16,16,1920]{2,1,0:T(8,128)(2,1)}), bf16[16,16,1920]{2,1,0:T(8,128)(2,1)S(1)}, u32[]{:S(2)}, u32[]{:S(2)}) %all-to-all-start) | async-done | bytes 983072 | tf_op jit(solution)/shard_map/all_to_all | solution.py:191
  113.5 0.5 fusion.93
  114.0 0.7 copy_bitcast_fusion.2
  115.7 2.3 fusion.97
  118.0 0.8 max.37
  119.3 0.5 fusion.26
  119.9 2.8 %fusion.18 = f32[8,8,3,8,128]{4,3,2,1,0:T(8,128)S(1)} fusion(f32[8,8,24,128]{3,2,1,0:T(8,128)S(1)} %fusion.55, bf16[8,128,2,8,128]{1,4,3,2,0:T(8,128)(2,1)} %bitcast.164, f32[8,8,24,128]{3,2,1,0:T(8,128)S(1)} %get-tuple-element.26, f32[8,8,24]{2,1,0:T(8,128)S(1)} %max.36, pred[8,128]{1,0:T(8,128)(4,1)S(1)} %get-tuple-element.24), kind=kOutput, calls=%fused_computation.34 | convolution fusion | flops 51118080 | bytes 4463616 | tf_op jit(solution)/shard_map/skqp,spkd->skqd/dot_general | solution.py:260
  123.0 0.5 copy.134
  123.5 0.6 reshape.434
  124.4 0.7 gather_fusion.3
  125.5 0.7 gather_fusion.4
  126.3 1.0 concatenate.35
  127.3 6.5 %all-to-all-start.2 = ((f32[16,8,1560]{2,1,0:T(8,128)}), f32[16,8,1560]{2,1,0:T(8,128)S(1)}, u32[]{:S(2)}, u32[]{:S(2)}) async-start(f32[16,8,1560]{2,1,0:T(8,128)} %concatenate.35), calls=%async_computation.2 | async-start | bytes 1703936 | tf_op jit(solution)/shard_map/all_to_all | solution.py:282
  134.8 2.3 fusion.99
  137.7 2.8 %fusion.14 = f32[8,8,3,8,128]{4,3,2,1,0:T(8,128)S(1)} fusion(f32[8,8,24,128]{3,2,1,0:T(8,128)S(1)} %fusion.57, bf16[8,128,2,8,128]{1,4,3,2,0:T(8,128)(2,1)} %bitcast.162, f32[8,8,24,128]{3,2,1,0:T(8,128)S(1)} %get-tuple-element.30, f32[8,8,24]{2,1,0:T(8,128)S(1)} %max.34, pred[8,128]{1,0:T(8,128)(4,1)S(1)} %get-tuple-element.23), kind=kOutput, calls=%fused_computation.30 | convolution fusion | flops 51118080 | bytes 4463616 | tf_op jit(solution)/shard_map/skqp,spkd->skqd/dot_general | solution.py:260
  140.6 1.0 copy.210
  141.6 1.3 reshape_reshape.18
  142.8 0.5 copy.114
  143.4 0.6 reshape.428
  144.1 1.7 fusion.24
  146.1 0.7 gather_fusion.1
  147.1 0.7 gather_fusion.2
  148.0 1.0 concatenate.34
  149.0 4.6 %all-to-all-done.2 = f32[16,8,1560]{2,1,0:T(8,128)S(1)} async-done(((f32[16,8,1560]{2,1,0:T(8,128)}), f32[16,8,1560]{2,1,0:T(8,128)S(1)}, u32[]{:S(2)}, u32[]{:S(2)}) %all-to-all-start.2) | async-done | bytes 798752 | tf_op jit(solution)/shard_map/all_to_all | solution.py:282
  153.6 5.9 %all-to-all-start.1 = ((f32[16,8,1560]{2,1,0:T(8,128)}), f32[16,8,1560]{2,1,0:T(8,128)}, u32[]{:S(2)}, u32[]{:S(2)}) async-start(f32[16,8,1560]{2,1,0:T(8,128)} %concatenate.34), calls=%async_computation.1 | async-start | bytes 1703936 | tf_op jit(solution)/shard_map/all_to_all | solution.py:282
  159.6 1.5 scatter_custom_fusion.1
  161.1 18.2 %all-to-all-done.1 = f32[16,8,1560]{2,1,0:T(8,128)} async-done(((f32[16,8,1560]{2,1,0:T(8,128)}), f32[16,8,1560]{2,1,0:T(8,128)}, u32[]{:S(2)}, u32[]{:S(2)}) %all-to-all-start.1) | async-done | bytes 798752 | tf_op jit(solution)/shard_map/all_to_all | solution.py:282
  179.3 1.3 pad_maximum_fusion
  181.1 0.7 gather_fusion.5
  182.0 1.3 broadcast_in_dim.271
  183.3 3.0 %copy.148 = f32[256,1536]{1,0:T(8,128)} copy(f32[256,1536]{0,1:T(8,128)} %bitcast.168) | data formatting | bytes 3145728 | tf_op jit(solution)/shard_map/reshape | solution.py:299
  186.3 1.6 slice_multiply_fusion
  187.9 0.7 fusion.7
  189.1 0.7 fusion.34
  189.9 48.5 %all-gather.5.cloned.1.call-done = bf16[192,8192]{1,0:T(8,128)(2,1)} async-done(((bf16[192,512]{1,0:T(8,128)(2,1)}), bf16[192,8192]{1,0:T(8,128)(2,1)}) %all-gather.5.cloned.1.call-update) | async-done | bytes 3145744 | tf_op jit(solution)/shard_map/all_gather | solution.py:307
  238.4 6.9 %convolution_convert_fusion = bf16[192,512]{1,0:T(8,128)(2,1)} fusion(bf16[192,8192]{1,0:T(8,128)(2,1)} %all-gather.5.cloned.1.call-done, bf16[8192,512]{1,0:T(8,128)(2,1)} %param.17), kind=kOutput, calls=%fused_computation.37 | convolution fusion | flops 1610711040 | bytes 11730944 | tf_op jit(solution)/shard_map/dot_general | solution.py:308
  (112 shorter events, 8.3 us)
Async XLA Ops:
  6.5 69.9 %copy-start = (bf16[8192,128]{1,0:T(8,128)(2,1)S(1)}, bf16[8192,128]{1,0:T(8,128)(2,1)}, u32[]{:S(2)}) copy-start(bf16[8192,128]{1,0:T(8,128)(2,1)} %param.16) | copy-start | bytes 6291460
  6.5 52.9 %all-gather.3.cloned.1.call-start = ((), (), s32[]{:S(2)}) async-start(), calls=%async_computation.3 | async-start | bytes 3342336 | tf_op jit(solution)/shard_map/all_gather | solution.py:119
  16.0 46.2 %copy-start.9 = (f32[8192]{0:T(1024)S(1)}, f32[8192]{0:T(1024)}, u32[]{:S(2)}) copy-start(f32[8192]{0:T(1024)} %param.14) | copy-start | bytes 98308
  59.5 2.8 %copy-start.2 = (bf16[192,8192]{1,0:T(8,128)(2,1)S(1)}, bf16[192,8192]{1,0:T(8,128)(2,1)}, u32[]{:S(2)}) copy-start(bf16[192,8192]{1,0:T(8,128)(2,1)} %all-gather.3.cloned.1.call-done) | copy-start | bytes 9437188
  64.7 7.2 %collective-permute-start.2 = (bf16[192,64]{0,1:T(8,128)(2,1)S(1)}, bf16[192,64]{0,1:T(8,128)(2,1)S(1)}, u32[]{:S(2)}, u32[]{:S(2)}) collective-permute-start(bf16[192,64]{0,1:T(8,128)(2,1)S(1)} %fusion.22), channel_id=1, source_target_pairs={{0,3},{1,2},{2,1},{3,0},{4,7},{5,6},{6,5},{7,4},{8,11},{9,10},{10,... | collective-permute-start | bytes 73736 | tf_op jit(solution)/shard_map/ppermute | solution.py:97
  65.9 6.0 %collective-permute-start.1 = (bf16[192,64]{0,1:T(8,128)(2,1)S(1)}, bf16[192,64]{0,1:T(8,128)(2,1)S(1)}, u32[]{:S(2)}, u32[]{:S(2)}) collective-permute-start(bf16[192,64]{0,1:T(8,128)(2,1)S(1)} %fusion.22), channel_id=1, source_target_pairs={{0,2},{1,3},{2,0},{3,1},{4,6},{5,7},{6,4},{7,5},{8,10},{9,11},{10,... | collective-permute-start | bytes 73736 | tf_op jit(solution)/shard_map/ppermute | solution.py:97
  66.7 5.3 %collective-permute-start = (bf16[192,64]{0,1:T(8,128)(2,1)S(1)}, bf16[192,64]{0,1:T(8,128)(2,1)S(1)}, u32[]{:S(2)}, u32[]{:S(2)}) collective-permute-start(bf16[192,64]{0,1:T(8,128)(2,1)S(1)} %fusion.22), channel_id=1, source_target_pairs={{0,1},{1,0},{2,3},{3,2},{4,5},{5,4},{6,7},{7,6},{8,9},{9,8},{10,11... | collective-permute-start | bytes 73736 | tf_op jit(solution)/shard_map/ppermute | solution.py:97
  72.0 7.1 %copy-start.8 = (bf16[16,64,512]{2,1,0:T(8,128)(2,1)S(1)}, bf16[16,64,512]{2,1,0:T(8,128)(2,1)}, u32[]{:S(2)}) copy-start(bf16[16,64,512]{2,1,0:T(8,128)(2,1)} %param.19) | copy-start | bytes 3145732
  72.0 6.1 %collective-permute-start.5 = (bf16[192,64]{0,1:T(8,128)(2,1)S(1)}, bf16[192,64]{0,1:T(8,128)(2,1)S(1)}, u32[]{:S(2)}, u32[]{:S(2)}) collective-permute-start(bf16[192,64]{0,1:T(8,128)(2,1)S(1)} %add_add_fusion.1), channel_id=1, source_target_pairs={{0,12},{1,13},{2,14},{3,15},{4,8},{5,9},{6,10},{7,11},{8,4},{9,5},... | collective-permute-start | bytes 73736 | tf_op jit(solution)/shard_map/ppermute | solution.py:97
  73.5 5.6 %collective-permute-start.4 = (bf16[192,64]{0,1:T(8,128)(2,1)S(1)}, bf16[192,64]{0,1:T(8,128)(2,1)S(1)}, u32[]{:S(2)}, u32[]{:S(2)}) collective-permute-start(bf16[192,64]{0,1:T(8,128)(2,1)S(1)} %add_add_fusion.1), channel_id=1, source_target_pairs={{0,8},{1,9},{2,10},{3,11},{4,12},{5,13},{6,14},{7,15},{8,0},{9,1},... | collective-permute-start | bytes 73736 | tf_op jit(solution)/shard_map/ppermute | solution.py:97
  73.6 5.4 %collective-permute-start.3 = (bf16[192,64]{0,1:T(8,128)(2,1)S(1)}, bf16[192,64]{0,1:T(8,128)(2,1)S(1)}, u32[]{:S(2)}, u32[]{:S(2)}) collective-permute-start(bf16[192,64]{0,1:T(8,128)(2,1)S(1)} %add_add_fusion.1), channel_id=1, source_target_pairs={{0,4},{1,5},{2,6},{3,7},{4,0},{5,1},{6,2},{7,3},{8,12},{9,13},{10,... | collective-permute-start | bytes 73736 | tf_op jit(solution)/shard_map/ppermute | solution.py:97
  87.5 25.6 %all-to-all-start = ((bf16[16,16,1920]{2,1,0:T(8,128)(2,1)}), bf16[16,16,1920]{2,1,0:T(8,128)(2,1)S(1)}, u32[]{:S(2)}, u32[]{:S(2)}) async-start(bf16[16,16,1920]{2,1,0:T(8,128)(2,1)} %reshape.423), calls=%async_computation | async-start | bytes 1966080 | tf_op jit(solution)/shard_map/all_to_all | solution.py:191
  97.8 6.5 %copy-start.7 = (s32[64]{0:T(128)S(1)}, s32[64]{0:T(128)}, u32[]{:S(2)}) copy-start(s32[64]{0:T(128)} %param.23) | copy-start | bytes 772
  97.8 6.6 %copy-start.6 = (s32[64,4]{0,1:T(4,128)S(1)}, s32[64,4]{0,1:T(4,128)}, u32[]{:S(2)}) copy-start(s32[64,4]{0,1:T(4,128)} %param.24) | copy-start | bytes 3076
  123.0 2.3 copy-start.4
  125.3 9.1 %copy-start.5 = (bf16[8,3,2,8,128]{4,3,2,1,0:T(8,128)(2,1)S(1)}, bf16[8,3,2,8,128]{4,3,2,1,0:T(8,128)(2,1)}, u32[]{:S(2)}) copy-start(bf16[8,3,2,8,128]{4,3,2,1,0:T(8,128)(2,1)} %get-tuple-element.34) | copy-start | bytes 294916
  127.3 26.3 %all-to-all-start.2 = ((f32[16,8,1560]{2,1,0:T(8,128)}), f32[16,8,1560]{2,1,0:T(8,128)S(1)}, u32[]{:S(2)}, u32[]{:S(2)}) async-start(f32[16,8,1560]{2,1,0:T(8,128)} %concatenate.35), calls=%async_computation.2 | async-start | bytes 1703936 | tf_op jit(solution)/shard_map/all_to_all | solution.py:282
  137.2 4.4 %copy-start.3 = (f32[8,8,24,128]{3,2,1,0:T(8,128)}, f32[8,8,24,128]{3,2,1,0:T(8,128)S(1)}, u32[]{:S(2)}) copy-start(f32[8,8,24,128]{3,2,1,0:T(8,128)S(1)} %get-tuple-element.30) | copy-start | bytes 2359300
  153.6 25.7 %all-to-all-start.1 = ((f32[16,8,1560]{2,1,0:T(8,128)}), f32[16,8,1560]{2,1,0:T(8,128)}, u32[]{:S(2)}, u32[]{:S(2)}) async-start(f32[16,8,1560]{2,1,0:T(8,128)} %concatenate.34), calls=%async_computation.1 | async-start | bytes 1703936 | tf_op jit(solution)/shard_map/all_to_all | solution.py:282
  159.5 78.9 %all-gather.5.cloned.1.call-start = ((), (), s32[]{:S(2)}) async-start(), calls=%async_computation.4 | async-start | bytes 3342336 | tf_op jit(solution)/shard_map/all_gather | solution.py:307
  238.4 7.0 %copy-start.1 = (bf16[8192,128]{1,0:T(8,128)(2,1)S(1)}, bf16[8192,128]{1,0:T(8,128)(2,1)}, u32[]{:S(2)}) copy-start(bf16[8192,128]{1,0:T(8,128)(2,1)} %param.16) | copy-start | bytes 6291460
Sparse Core Ops, SparseCore 0:
  9.5 49.9 all-gather.2
  190.0 48.3 all-gather.4

commit v11 on v10

--- a/solution.py
+++ b/solution.py
@@ -281,7 +281,7 @@
         )
         return lax.all_to_all(packed, "blk", 0, 0, tiled=True)
 
-    half_pages = request_page_count // 2
+    half_pages = (3 * request_page_count) // 8
     arrived = jnp.concatenate(
         [page_exchange(0, half_pages), page_exchange(half_pages, request_page_count - half_pages)],
         axis=1,

time: 253 us -> 271 us (1.071)
  waiting for transfers between devices: 119 us -> 137 us
    all_to_all x2, waiting for transfers between devices: 22.9 us -> 40.2 us  [page_exchange(): return lax.all_to_all(packed, 'blk', 0, 0, tiled=True)]
    all_to_all x1, waiting for transfers between devices: 8.26 us -> 0.01 us  [local(): lax.all_to_all(outgoing, 'blk', 0, 0, tiled=True)]
    all_gather x1, waiting for transfers between devices: 37.3 us -> 42.6 us  [local(): gathered = lax.all_gather(layer_input_tokens, 'blk', axis=1, tiled=True)]
    all_gather x1, waiting for transfers between devices: 48.5 us -> 52.3 us  [local(): attended = lax.all_gather(attended_own, 'blk', axis=1, tiled=True)]
    slice x1 -> x2, local copies, waits for them, and re-layouts: 6.13 us -> 9.66 us  [page_exchange(): chunk_cache = cache_pages[first:first + chunk_pages]]
    unnamed x23 -> x15, local copies, waits for them, and re-layouts: 13.8 us -> 13.4 us
  transfers between devices with their start and end apart: 11 -> 11, of which waited for: 7 -> 6; matrix products, arithmetic and copies ran while one was open for 20% -> 19% of each run, Pallas kernels for 0% -> 0%
where the time goes in v11:
time: 271 us; the launch traced here: 269 us
  waiting for transfers between devices  137 us (51%)
  local copies, waits for them, and re-layouts  48.1 us (18%)
  matrix products  28.6 us (11%)
  starting transfers between devices  22.3 us (8%)
  other arithmetic  16.5 us (6%)
  between operations  14.1 us (5%)
    all_gather x1, waiting for transfers between devices, local(): attended = lax.all_gather(attended_own, 'blk', axis=1, tiled=True)  52.3 us
    all_gather x1, waiting for transfers between devices, local(): gathered = lax.all_gather(layer_input_tokens, 'blk', axis=1, tiled=True)  42.6 us
    all_to_all x2, waiting for transfers between devices, page_exchange(): return lax.all_to_all(packed, 'blk', 0, 0, tiled=True)  40.2 us
    unnamed x15, local copies, waits for them, and re-layouts  13.4 us
    all_to_all x2, starting transfers between devices, page_exchange(): return lax.all_to_all(packed, 'blk', 0, 0, tiled=True)  11.8 us
    slice x2, local copies, waits for them, and re-layouts, page_exchange(): chunk_cache = cache_pages[first:first + chunk_pages]  9.66 us
    dot_general x1, matrix products, local(): jnp.dot(attended, output_weight, preferred_element_type=jnp.float32)  6.95 us
    ppermute x6, starting transfers between devices, butterfly(): lax.ppermute(value, 'blk', [(i, i ^ m) for i in range(size)])  6.41 us
  transfers between devices with their start and end apart: 11, of which 6 were waited for; matrix products, arithmetic and copies ran while one was open for 19% of the time, Pallas kernels for 0%

profile of v11, /device:TPU:0, one launch (start us, length us, event | category | flops | bytes accessed | tf_op | source)
XLA Modules:
  0.0 269.4 jit_solution(12218511533347161970)
XLA Ops:
  6.5 0.7 all-gather.3.cloned.1.call-update
  7.3 0.8 select_reduce_fusion.1
  8.2 0.7 add_convert_fusion
  9.1 0.8 copy.113
  10.1 1.4 scatter_custom_fusion
  11.6 0.9 fusion.66
  12.5 0.9 compare_reduce_fusion
  13.4 0.7 fusion.73
  14.1 2.8 %fusion.29 = (f32[192,640]{1,0:T(8,128)}, f32[192,640]{1,0:T(8,128)}) fusion(f32[640]{0:T(1024)S(1)} %fusion.72, f32[192]{0:T(256)S(1)} %convert_element_type.49, pred[640]{0:T(1024)(128)(4,1)S(1)} %fusion.73), kind=kLoop, calls=%fused_computation.57 | loop fusion | flops 368640 | bytes 987008 | tf_op jit(solution)/shard_map/jit(_where)/select_n | solution.py:57
  16.9 42.6 %all-gather.3.cloned.1.call-done = bf16[192,8192]{1,0:T(8,128)(2,1)} async-done(((bf16[192,512]{1,0:T(8,128)(2,1)}), bf16[192,8192]{1,0:T(8,128)(2,1)}) %all-gather.3.cloned.1.call-update) | async-done | bytes 3145744 | tf_op jit(solution)/shard_map/all_gather | solution.py:119
  59.5 2.8 %fusion = f32[192]{0:T(256)S(1)} fusion(bf16[192,8192]{1,0:T(8,128)(2,1)} %all-gather.3.cloned.1.call-done), kind=kLoop, calls=%fused_computation.10 | loop fusion | flops 4718400 | bytes 3146496 | tf_op jit(solution)/shard_map/reduce_sum | solution.py:70
  62.3 2.4 fusion.22
  64.7 1.2 collective-permute-start.2
  65.9 0.7 collective-permute-start.1
  66.7 5.2 %fusion.89 = f32[192,512]{1,0:T(8,128)S(1)} fusion(bf16[8192,512]{1,0:T(8,128)(2,1)} %param.15, bf16[192,8192]{1,0:T(8,128)(2,1)S(1)} %copy-done.2, f32[8192]{0:T(1024)S(1)} %copy-done.5, f32[192]{0:T(256)S(1)} %add_rsqrt_fusion), kind=kOutput, calls=%fused_computation.164 | convolution fusion | flops 1616904192 | bytes 11961088 | tf_op jit(solution)/shard_map/dot_general | solution.py:151
  72.0 1.5 collective-permute-start.5
  73.6 2.8 %collective-permute-start.3 = (bf16[192,64]{0,1:T(8,128)(2,1)S(1)}, bf16[192,64]{0,1:T(8,128)(2,1)S(1)}, u32[]{:S(2)}, u32[]{:S(2)}) collective-permute-start(bf16[192,64]{0,1:T(8,128)(2,1)S(1)} %add_add_fusion.1), channel_id=1, source_target_pairs={{0,4},{1,5},{2,6},{3,7},{4,0},{5,1},{6,2},{7,3},{8,12},{9,13},{10,... | collective-permute-start | bytes 73736 | tf_op jit(solution)/shard_map/ppermute | solution.py:97
  76.4 1.1 fusion.86
  77.6 0.5 collective-permute-done.5
  78.1 1.0 collective-permute-done.4
  79.1 0.4 fusion.19
  79.5 0.8 pad_maximum_fusion.1.values_ref
  80.3 2.4 shard_map.127
  82.7 1.1 reshape.422
  83.8 1.9 gather_fusion
  85.7 1.6 reshape.423
  87.3 3.8 %all-to-all-start = ((bf16[16,16,1920]{2,1,0:T(8,128)(2,1)}), bf16[16,16,1920]{2,1,0:T(8,128)(2,1)S(1)}, u32[]{:S(2)}, u32[]{:S(2)}) async-start(bf16[16,16,1920]{2,1,0:T(8,128)(2,1)} %reshape.423), calls=%async_computation | async-start | bytes 1966080 | tf_op jit(solution)/shard_map/all_to_all | solution.py:191
  91.4 4.0 %slice.93 = bf16[6,128,2048]{2,1,0:T(8,128)(2,1)} slice(bf16[16,128,2048]{2,1,0:T(8,128)(2,1)} %param.20), slice={[0:6], [0:128], [0:2048]} | slice | bytes 6291456 | tf_op jit(solution)/shard_map/slice | solution.py:232
  95.4 5.7 %slice.104 = bf16[10,128,2048]{2,1,0:T(8,128)(2,1)} slice(bf16[16,128,2048]{2,1,0:T(8,128)(2,1)} %param.20), slice={[6:16], [0:128], [0:2048]} | slice | bytes 10485760 | tf_op jit(solution)/shard_map/slice | solution.py:232
  101.1 4.7 %copy.172 = bf16[6,128,2048]{1,2,0:T(8,128)(2,1)} copy(bf16[6,128,2048]{2,1,0:T(8,128)(2,1)} %slice.93) | data formatting | bytes 6291456
  105.7 7.9 %copy.177 = bf16[10,128,2048]{1,2,0:T(8,128)(2,1)} copy(bf16[10,128,2048]{2,1,0:T(8,128)(2,1)} %slice.104) | data formatting | bytes 10485760
  113.8 0.3 reshape.424
  115.2 0.3 reshape.431
  115.8 2.0 fusion.95
  118.0 0.4 fusion.36
  118.9 0.7 gather_fusion.1
  119.5 0.4 copy.163
  120.6 0.7 gather_fusion.2
  121.2 0.4 copy.165
  122.0 0.4 fusion.61
  122.4 2.4 fusion.18
  125.1 1.1 copy.134
  126.2 5.9 %all-to-all-start.1 = ((f32[16,6,1560]{2,1,0:T(8,128)}), f32[16,6,1560]{2,1,0:T(8,128)}, u32[]{:S(2)}, u32[]{:S(2)}) async-start(f32[16,6,1560]{2,1,0:T(8,128)} %copy.134), calls=%async_computation.1 | async-start | bytes 1703936 | tf_op jit(solution)/shard_map/all_to_all | solution.py:282
  132.1 2.6 fusion.93
  134.8 0.4 fusion.94
  135.5 0.6 fusion.24
  136.3 0.7 gather_fusion.3
  137.3 0.7 gather_fusion.4
  138.3 0.5 fusion.53
  138.8 3.3 %fusion.13 = f32[10,8,3,8,128]{4,3,2,1,0:T(8,128)S(1)} fusion(f32[10,8,24,128]{3,2,1,0:T(8,128)S(1)} %fusion.53, bf16[10,128,2,8,128]{1,4,3,2,0:T(8,128)(2,1)} %bitcast.176, f32[10,8,24,128]{3,2,1,0:T(8,128)S(1)} %get-tuple-element.16, f32[10,8,24]{2,1,0:T(8,128)S(1)} %max.36, pred[10,128]{1,0:T(8,128)(4,1)S(1)} %slice.138), kind=kOutput, calls=%fused_computation.29 | convolution fusion | flops 63897600 | bytes 5579520 | tf_op jit(solution)/shard_map/skqp,spkd->skqd/dot_general | solution.py:260
  142.7 1.5 copy.157
  144.2 7.7 %all-to-all-done.1 = f32[16,6,1560]{2,1,0:T(8,128)} async-done(((f32[16,6,1560]{2,1,0:T(8,128)}), f32[16,6,1560]{2,1,0:T(8,128)}, u32[]{:S(2)}, u32[]{:S(2)}) %all-to-all-start.1) | async-done | bytes 599072 | tf_op jit(solution)/shard_map/all_to_all | solution.py:282
  152.0 5.9 %all-to-all-start.2 = ((f32[16,10,1560]{2,1,0:T(8,128)}), f32[16,10,1560]{2,1,0:T(8,128)}, u32[]{:S(2)}, u32[]{:S(2)}) async-start(f32[16,10,1560]{2,1,0:T(8,128)} %copy.157), calls=%async_computation.2 | async-start | bytes 3407872 | tf_op jit(solution)/shard_map/all_to_all | solution.py:282
  158.1 1.5 scatter_custom_fusion.1
  159.6 32.5 %all-to-all-done.2 = f32[16,10,1560]{2,1,0:T(8,128)} async-done(((f32[16,10,1560]{2,1,0:T(8,128)}), f32[16,10,1560]{2,1,0:T(8,128)}, u32[]{:S(2)}, u32[]{:S(2)}) %all-to-all-start.2) | async-done | bytes 998432 | tf_op jit(solution)/shard_map/all_to_all | solution.py:282
  192.2 1.9 pad_maximum_fusion
  194.5 0.7 gather_fusion.5
  195.4 1.3 broadcast_in_dim.291
  196.7 3.0 %copy.161 = f32[256,1536]{1,0:T(8,128)} copy(f32[256,1536]{0,1:T(8,128)} %bitcast.182) | data formatting | bytes 3145728 | tf_op jit(solution)/shard_map/reshape | solution.py:299
  199.8 1.6 slice_multiply_fusion
  201.3 0.7 fusion.5
  202.6 0.7 fusion.40
  203.3 52.3 %all-gather.5.cloned.1.call-done = bf16[192,8192]{1,0:T(8,128)(2,1)} async-done(((bf16[192,512]{1,0:T(8,128)(2,1)}), bf16[192,8192]{1,0:T(8,128)(2,1)}) %all-gather.5.cloned.1.call-update) | async-done | bytes 3145744 | tf_op jit(solution)/shard_map/all_gather | solution.py:307
  255.6 6.9 %convolution_convert_fusion = bf16[192,512]{1,0:T(8,128)(2,1)} fusion(bf16[192,8192]{1,0:T(8,128)(2,1)} %all-gather.5.cloned.1.call-done, bf16[8192,512]{1,0:T(8,128)(2,1)} %param.17), kind=kOutput, calls=%fused_computation.37 | convolution fusion | flops 1610711040 | bytes 11730944 | tf_op jit(solution)/shard_map/dot_general | solution.py:308
  (114 shorter events, 7.5 us)
Async XLA Ops:
  6.5 69.9 %copy-start = (bf16[8192,128]{1,0:T(8,128)(2,1)S(1)}, bf16[8192,128]{1,0:T(8,128)(2,1)}, u32[]{:S(2)}) copy-start(bf16[8192,128]{1,0:T(8,128)(2,1)} %param.16) | copy-start | bytes 6291460
  6.5 55.7 %copy-start.5 = (f32[8192]{0:T(1024)S(1)}, f32[8192]{0:T(1024)}, u32[]{:S(2)}) copy-start(f32[8192]{0:T(1024)} %param.14) | copy-start | bytes 98308
  6.5 52.9 %all-gather.3.cloned.1.call-start = ((), (), s32[]{:S(2)}) async-start(), calls=%async_computation.3 | async-start | bytes 3342336 | tf_op jit(solution)/shard_map/all_gather | solution.py:119
  59.5 2.8 %copy-start.2 = (bf16[192,8192]{1,0:T(8,128)(2,1)S(1)}, bf16[192,8192]{1,0:T(8,128)(2,1)}, u32[]{:S(2)}) copy-start(bf16[192,8192]{1,0:T(8,128)(2,1)} %all-gather.3.cloned.1.call-done) | copy-start | bytes 9437188
  64.7 7.2 %collective-permute-start.2 = (bf16[192,64]{0,1:T(8,128)(2,1)S(1)}, bf16[192,64]{0,1:T(8,128)(2,1)S(1)}, u32[]{:S(2)}, u32[]{:S(2)}) collective-permute-start(bf16[192,64]{0,1:T(8,128)(2,1)S(1)} %fusion.22), channel_id=1, source_target_pairs={{0,3},{1,2},{2,1},{3,0},{4,7},{5,6},{6,5},{7,4},{8,11},{9,10},{10,... | collective-permute-start | bytes 73736 | tf_op jit(solution)/shard_map/ppermute | solution.py:97
  65.9 6.0 %collective-permute-start.1 = (bf16[192,64]{0,1:T(8,128)(2,1)S(1)}, bf16[192,64]{0,1:T(8,128)(2,1)S(1)}, u32[]{:S(2)}, u32[]{:S(2)}) collective-permute-start(bf16[192,64]{0,1:T(8,128)(2,1)S(1)} %fusion.22), channel_id=1, source_target_pairs={{0,2},{1,3},{2,0},{3,1},{4,6},{5,7},{6,4},{7,5},{8,10},{9,11},{10,... | collective-permute-start | bytes 73736 | tf_op jit(solution)/shard_map/ppermute | solution.py:97
  66.7 5.3 %collective-permute-start = (bf16[192,64]{0,1:T(8,128)(2,1)S(1)}, bf16[192,64]{0,1:T(8,128)(2,1)S(1)}, u32[]{:S(2)}, u32[]{:S(2)}) collective-permute-start(bf16[192,64]{0,1:T(8,128)(2,1)S(1)} %fusion.22), channel_id=1, source_target_pairs={{0,1},{1,0},{2,3},{3,2},{4,5},{5,4},{6,7},{7,6},{8,9},{9,8},{10,11... | collective-permute-start | bytes 73736 | tf_op jit(solution)/shard_map/ppermute | solution.py:97
  71.9 7.1 %copy-start.4 = (bf16[16,64,512]{2,1,0:T(8,128)(2,1)S(1)}, bf16[16,64,512]{2,1,0:T(8,128)(2,1)}, u32[]{:S(2)}) copy-start(bf16[16,64,512]{2,1,0:T(8,128)(2,1)} %param.19) | copy-start | bytes 3145732
  72.0 6.1 %collective-permute-start.5 = (bf16[192,64]{0,1:T(8,128)(2,1)S(1)}, bf16[192,64]{0,1:T(8,128)(2,1)S(1)}, u32[]{:S(2)}, u32[]{:S(2)}) collective-permute-start(bf16[192,64]{0,1:T(8,128)(2,1)S(1)} %add_add_fusion.1), channel_id=1, source_target_pairs={{0,12},{1,13},{2,14},{3,15},{4,8},{5,9},{6,10},{7,11},{8,4},{9,5},... | collective-permute-start | bytes 73736 | tf_op jit(solution)/shard_map/ppermute | solution.py:97
  73.5 5.6 %collective-permute-start.4 = (bf16[192,64]{0,1:T(8,128)(2,1)S(1)}, bf16[192,64]{0,1:T(8,128)(2,1)S(1)}, u32[]{:S(2)}, u32[]{:S(2)}) collective-permute-start(bf16[192,64]{0,1:T(8,128)(2,1)S(1)} %add_add_fusion.1), channel_id=1, source_target_pairs={{0,8},{1,9},{2,10},{3,11},{4,12},{5,13},{6,14},{7,15},{8,0},{9,1},... | collective-permute-start | bytes 73736 | tf_op jit(solution)/shard_map/ppermute | solution.py:97
  73.6 5.4 %collective-permute-start.3 = (bf16[192,64]{0,1:T(8,128)(2,1)S(1)}, bf16[192,64]{0,1:T(8,128)(2,1)S(1)}, u32[]{:S(2)}, u32[]{:S(2)}) collective-permute-start(bf16[192,64]{0,1:T(8,128)(2,1)S(1)} %add_add_fusion.1), channel_id=1, source_target_pairs={{0,4},{1,5},{2,6},{3,7},{4,0},{5,1},{6,2},{7,3},{8,12},{9,13},{10,... | collective-permute-start | bytes 73736 | tf_op jit(solution)/shard_map/ppermute | solution.py:97
  83.8 7.4 %copy-start.3 = (s32[64]{0:T(128)S(1)}, s32[64]{0:T(128)}, u32[]{:S(2)}) copy-start(s32[64]{0:T(128)} %param.23) | copy-start | bytes 772
  87.3 26.5 %all-to-all-start = ((bf16[16,16,1920]{2,1,0:T(8,128)(2,1)}), bf16[16,16,1920]{2,1,0:T(8,128)(2,1)S(1)}, u32[]{:S(2)}, u32[]{:S(2)}) async-start(bf16[16,16,1920]{2,1,0:T(8,128)(2,1)} %reshape.423), calls=%async_computation | async-start | bytes 1966080 | tf_op jit(solution)/shard_map/all_to_all | solution.py:191
  126.2 25.8 %all-to-all-start.1 = ((f32[16,6,1560]{2,1,0:T(8,128)}), f32[16,6,1560]{2,1,0:T(8,128)}, u32[]{:S(2)}, u32[]{:S(2)}) async-start(f32[16,6,1560]{2,1,0:T(8,128)} %copy.134), calls=%async_computation.1 | async-start | bytes 1703936 | tf_op jit(solution)/shard_map/all_to_all | solution.py:282
  152.0 40.2 %all-to-all-start.2 = ((f32[16,10,1560]{2,1,0:T(8,128)}), f32[16,10,1560]{2,1,0:T(8,128)}, u32[]{:S(2)}, u32[]{:S(2)}) async-start(f32[16,10,1560]{2,1,0:T(8,128)} %copy.157), calls=%async_computation.2 | async-start | bytes 3407872 | tf_op jit(solution)/shard_map/all_to_all | solution.py:282
  157.8 97.8 %all-gather.5.cloned.1.call-start = ((), (), s32[]{:S(2)}) async-start(), calls=%async_computation.4 | async-start | bytes 3342336 | tf_op jit(solution)/shard_map/all_gather | solution.py:307
  255.6 7.0 %copy-start.1 = (bf16[8192,128]{1,0:T(8,128)(2,1)S(1)}, bf16[8192,128]{1,0:T(8,128)(2,1)}, u32[]{:S(2)}) copy-start(bf16[8192,128]{1,0:T(8,128)(2,1)} %param.16) | copy-start | bytes 6291460
Sparse Core Ops, SparseCore 0:
  9.5 49.8 all-gather.2
  203.5 52.1 all-gather.4
